TPU v7x, 512 devices: a whole 4x8x8 slice. The times are simulated.
512 devices in a mesh: rep: 16 (over y_lo, x, core), space: 32 (over y_hi, z).
Axes of the slice: x: 4, y: 8 (y_hi: 4, y_lo: 2; y = y_hi * 2 + y_lo), z: 8, core: 2. Of those that a mesh axis runs over, the one named last changes fastest.
Arguments:
- positions: float32 [16, 2048, 3, 128], P('rep', 'space'), may hold values from 0 to 0.6
- velocities: float32 [16, 2048, 3, 128], P('rep', 'space')
- strength: float32 [16, 2048, 128], P('rep', 'space'), may hold values from 0.5 to 1.5
- noise: float32 [4, 16, 2048, 128], P(None, 'rep', 'space'), may hold values from -4 to 4
- neighbours: int32 [16, 2048, 3], P('rep', 'space'), may hold values from 0 to 95, as said below
- bins: int32 [16, 2048, 128], P('rep', 'space'), may hold values from 0 to 1023, as said below
- thermal: float32 [16, 3, 128], P('rep'), may hold values from -3 to 3
- slot_counts: int32 [16], P('rep'), may hold values from 32 to 128, as said below
Outputs:
- new_positions: float32 [16, 2048, 3, 128], P('rep', 'space')
- new_velocities: float32 [16, 2048, 3, 128], P('rep', 'space')
- bin_velocity: float32 [3, 32768], P(None, 'space')
- inserted: float32 [16, 3, 128], P('rep')
Inputs may be any that keep to these rules, and one draw needn't show every extreme that they name: `neighbours`: entry e names tile e - 16 counted from the first tile of the same slab. The first entry of every list is the tile itself, the second lies exactly 16 tiles away, the others are distinct, nonzero and at most 16 tiles away, and differ from the second. The beads of each replica in each slab name every one of the slab's 1024 bins at least once. `slot_counts`: some replica fills all 128 slots.
All inputs are finite; a program needn't handle non-finite values.
Results may differ from a plain program's by a relative error of at most 0.00014.
Values sent between devices are 32-bit elements; how exact they have to be, the bound alone decides.
No kernel may reach another device: no remote copies, remote signals or barrier semaphores. Data moves between devices by JAX's collectives and lax.ppermute only.
A program may use at most 64 MiB of HBM per device.

v0:
```python
import jax
import jax.numpy as jnp
from jax import lax
from jax.sharding import PartitionSpec as P

HALO = 16
BINS_DEV = 1024


TIME_STEP = 0.02
REPULSION = 0.25
FRICTION = 1.0
NOISE_AMP = 0.25
SPACING = 0.02
TARGET_FLOW = 1.0


def padded(value, sides, width):
    for axis, dim in sides:
        count, length = (lax.axis_size(axis), value.shape[dim])
        up = [(i, (i + 1) % count) for i in range(count - 1)]
        down = [(j, i) for i, j in up]
        last = lax.slice_in_dim(value, length - width, length, axis=dim)
        initial = lax.slice_in_dim(value, 0, width, axis=dim)
        before = lax.ppermute(last, axis, up)
        after = lax.ppermute(initial, axis, down)
        value = jnp.concatenate([before, value, after], axis=dim)
    return value


def bead_forces(own_tile, partners, shift_x):
    offset_x = own_tile[0][None, :, None] - partners[:, 0][:, None, :] + shift_x[:, None, None]
    offset_y = own_tile[1][None, :, None] - partners[:, 1][:, None, :]
    offset_z = own_tile[2][None, :, None] - partners[:, 2][:, None, :]
    closing = offset_x * (own_tile[3][None, :, None] - partners[:, 3][:, None, :])
    closing = closing + offset_y * (own_tile[4][None, :, None] - partners[:, 4][:, None, :])
    closing = closing + offset_z * (own_tile[5][None, :, None] - partners[:, 5][:, None, :])
    weight = jnp.maximum(
        1.0 - (offset_x * offset_x + offset_y * offset_y + offset_z * offset_z), 0.0
    )
    kicks = own_tile[7][None, :, None] + partners[:, 7][:, None, :]
    factor = own_tile[6][None, :, None] * partners[:, 6][:, None, :] * weight
    factor = factor * (REPULSION - FRICTION * weight * closing + NOISE_AMP * kicks)
    return jnp.stack(
        [
            jnp.sum(factor * offset_x, axis=(0, 2)),
            jnp.sum(factor * offset_y, axis=(0, 2)),
            jnp.sum(factor * offset_z, axis=(0, 2)),
        ]
    )


def slab_forces(extended, links):
    tiles = links.shape[0]
    margin = (extended.shape[0] - tiles) // 2
    group = 8
    width = extended.shape[-1]
    own_index = jnp.arange(tiles, dtype=jnp.int32) + margin
    own_tiles = extended[margin : margin + tiles]

    def per_group(item):
        own_group, link_group, index_group = item
        partners = extended[link_group]
        shifts = SPACING * (index_group[:, None] - link_group).astype(jnp.float32)
        return jax.vmap(bead_forces)(own_group, partners, shifts)

    result = lax.map(
        per_group,
        (
            own_tiles.reshape(tiles // group, group, 8, width),
            links.reshape(tiles // group, group, links.shape[1]),
            own_index.reshape(tiles // group, group),
        ),
    )
    return result.reshape(tiles, 3, width)


def shards(positions, velocities, strength, noise, neighbours, bins, thermal, slot_counts):
    place = positions[0]
    speed = velocities[0]
    weights = strength[0]
    links = neighbours[0]
    substeps = noise.shape[0]
    for substep in range(substeps):
        packed = jnp.concatenate(
            [place, speed, weights[:, None, :], noise[substep, 0][:, None, :]], axis=1
        )
        extended = padded(packed, (("space", 0),), HALO)
        speed = speed + TIME_STEP * slab_forces(extended, links)
        place = place + TIME_STEP * speed
    tiles = speed.shape[0]
    width = speed.shape[-1]
    group = 8
    labels = jnp.arange(BINS_DEV, dtype=jnp.int32)
    grouped_speed = speed.reshape(tiles // group, group, 3, width)
    grouped_bins = bins[0].reshape(tiles // group, group * width)

    def accumulate(carry, item):
        momentum, counts = carry
        block_speed, block_bins = item
        table = (block_bins[:, None] == labels[None, :]).astype(jnp.float32)
        rows_now = jnp.transpose(block_speed, (1, 0, 2)).reshape(3, group * width)
        momentum = momentum + jnp.dot(
            rows_now, table, precision=lax.Precision.HIGHEST, preferred_element_type=jnp.float32
        )
        counts = counts + jnp.sum(table, axis=0)
        return ((momentum, counts), None)

    start = (jnp.zeros((3, BINS_DEV), jnp.float32), jnp.zeros((BINS_DEV,), jnp.float32))
    (momentum, counts), unused = lax.scan(accumulate, start, (grouped_speed, grouped_bins))
    momentum, counts = lax.psum((momentum, counts), "rep")
    bin_velocity = momentum / counts[None, :]
    flux_sum = lax.psum(jnp.sum(speed[:, 0, :]), ("rep", "space"))
    total_beads = lax.axis_size("rep") * lax.axis_size("space") * tiles * width
    inflow = 2.0 * TARGET_FLOW - flux_sum / total_beads
    slots = jnp.arange(thermal.shape[-1], dtype=jnp.int32)
    live = slots[None, :] < slot_counts[:, None]
    lift = jnp.where(jnp.arange(3)[:, None] == 0, inflow, jnp.float32(0.0))
    inserted = jnp.where(live[:, None, :], thermal + lift[None], jnp.float32(0.0))
    return (place[None], speed[None], bin_velocity, inserted)


def solution(mesh):
    return jax.shard_map(
        shards,
        mesh=mesh,
        in_specs=(
            P("rep", "space", None, None),
            P("rep", "space", None, None),
            P("rep", "space", None),
            P(None, "rep", "space", None),
            P("rep", "space", None),
            P("rep", "space", None),
            P("rep", None, None),
            P("rep"),
        ),
        out_specs=(
            P("rep", "space", None, None),
            P("rep", "space", None, None),
            P(None, "space"),
            P("rep", None, None),
        ),
        check_vma=False,
    )
```

profile of v0, /device:TPU:16, one launch (start us, length us, event | category | flops | bytes accessed | tf_op | source)
XLA Modules:
  0.0 355.1 jit_solution(9035465614638465549)
XLA Ops:
  0.6 0.8 fusion.110
  1.5 1.1 copy_bitcast_fusion.36
  2.8 4.3 %collective-permute-start = (f32[16,8,128]{2,1,0:T(8,128)S(1)}, f32[16,8,128]{2,1,0:T(8,128)S(1)}, u32[]{:S(2)}, u32[]{:S(2)}) collective-permute-start(f32[16,8,128]{2,1,0:T(8,128)S(1)} %get-tuple-element.459), channel_id=1, source_target_pairs={{0,1},{1,2},{2,3},{3,4},{4,5},{5,6},{6,7},{7,8},{8,9},{9,10},{10,1... | collective-permute-start | bytes 196616 | tf_op jit(solution)/shard_map/ppermute | solution.py:25
  7.1 8.4 %collective-permute-start.1 = (f32[16,8,128]{2,1,0:T(8,128)S(1)}, f32[16,8,128]{2,1,0:T(8,128)S(1)}, u32[]{:S(2)}, u32[]{:S(2)}) collective-permute-start(f32[16,8,128]{2,1,0:T(8,128)S(1)} %get-tuple-element.460), channel_id=1, source_target_pairs={{1,0},{2,1},{3,2},{4,3},{5,4},{6,5},{7,6},{8,7},{9,8},{10,9},{11,1... | collective-permute-start | bytes 196616 | tf_op jit(solution)/shard_map/ppermute | solution.py:26
  16.4 2.1 collective-permute-done.1
  18.6 30.8 %while.53 = (s32[]{:T(128)}, f32[8,8,3,128]{3,1,2,0:T(8,128)S(1)}, f32[8,8,8,128]{3,2,1,0:T(8,128)S(1)}, s32[8,8,3]{1,2,0:T(4,128)S(1)}, f32[96,8,128]{2,1,0:T(8,128)S(1)}, /*index=5*/s32[8,8]{1,0:T(8,128)S(1)}, s32[]{:T(128)}) while((s32[]{:T(128)}, f32[8,8,3,128]{3,1,2,0:T(8,128)S(1)}, f32[8,8,8,128]{3,2,1,0:T(8,128)S(1)}, ...), condition=%wide.region_4.5_spmd, body=%wide.region_0.4_spmd.sunk | while | flops 12980370 | bytes 1156605 | solution.py:67
  19.8 2.6 multiply_reduce_fusion.8
  23.7 2.6 multiply_reduce_fusion.8
  27.5 2.6 multiply_reduce_fusion.8
  31.4 2.6 multiply_reduce_fusion.8
  35.2 2.6 multiply_reduce_fusion.8
  39.1 2.6 multiply_reduce_fusion.8
  42.9 2.6 multiply_reduce_fusion.8
  46.8 2.6 multiply_reduce_fusion.8
  49.6 0.8 copy-done.1
  50.7 1.9 collective-permute-start.2
  52.7 7.4 %collective-permute-start.3 = (f32[16,8,128]{2,1,0:T(8,128)S(1)}, f32[16,8,128]{2,1,0:T(8,128)S(1)}, u32[]{:S(2)}, u32[]{:S(2)}) collective-permute-start(f32[16,8,128]{2,1,0:T(8,128)S(1)} %get-tuple-element.458), channel_id=1, source_target_pairs={{1,0},{2,1},{3,2},{4,3},{5,4},{6,5},{7,6},{8,7},{9,8},{10,9},{11,1... | collective-permute-start | bytes 196616 | tf_op jit(solution)/shard_map/ppermute | solution.py:26
  60.3 1.9 collective-permute-done.3
  62.4 30.8 %while.54 = (s32[]{:T(128)}, f32[8,8,3,128]{3,1,2,0:T(8,128)S(1)}, f32[8,8,8,128]{3,2,1,0:T(8,128)S(1)}, s32[8,8,3]{1,2,0:T(4,128)S(1)}, f32[96,8,128]{2,1,0:T(8,128)S(1)}, /*index=5*/s32[8,8]{1,0:T(8,128)S(1)}, s32[]{:T(128)}) while((s32[]{:T(128)}, f32[8,8,3,128]{3,1,2,0:T(8,128)S(1)}, f32[8,8,8,128]{3,2,1,0:T(8,128)S(1)}, ...), condition=%wide.region_9.10_spmd, body=%wide.region_5.9_spmd.sunk | while | flops 12980370 | bytes 1156605 | solution.py:67
  63.6 2.6 multiply_reduce_fusion.9
  67.4 2.6 multiply_reduce_fusion.9
  71.3 2.6 multiply_reduce_fusion.9
  75.1 2.6 multiply_reduce_fusion.9
  79.0 2.6 multiply_reduce_fusion.9
  82.8 2.6 multiply_reduce_fusion.9
  86.7 2.6 multiply_reduce_fusion.9
  90.5 2.6 multiply_reduce_fusion.9
  93.6 1.9 collective-permute-start.4
  95.5 7.4 %collective-permute-start.5 = (f32[16,8,128]{2,1,0:T(8,128)S(1)}, f32[16,8,128]{2,1,0:T(8,128)S(1)}, u32[]{:S(2)}, u32[]{:S(2)}) collective-permute-start(f32[16,8,128]{2,1,0:T(8,128)S(1)} %get-tuple-element.456), channel_id=1, source_target_pairs={{1,0},{2,1},{3,2},{4,3},{5,4},{6,5},{7,6},{8,7},{9,8},{10,9},{11,1... | collective-permute-start | bytes 196616 | tf_op jit(solution)/shard_map/ppermute | solution.py:26
  103.2 1.6 collective-permute-done.5
  104.9 30.8 %while.55 = (s32[]{:T(128)}, f32[8,8,3,128]{3,1,2,0:T(8,128)S(1)}, f32[8,8,8,128]{3,2,1,0:T(8,128)S(1)}, s32[8,8,3]{1,2,0:T(4,128)S(1)}, f32[96,8,128]{2,1,0:T(8,128)S(1)}, /*index=5*/s32[8,8]{1,0:T(8,128)S(1)}, s32[]{:T(128)}) while((s32[]{:T(128)}, f32[8,8,3,128]{3,1,2,0:T(8,128)S(1)}, f32[8,8,8,128]{3,2,1,0:T(8,128)S(1)}, ...), condition=%wide.region_14.15_spmd, body=%wide.region_10.14_spmd.sunk | while | flops 12980370 | bytes 1156605 | solution.py:67
  106.1 2.6 multiply_reduce_fusion.10
  110.0 2.6 multiply_reduce_fusion.10
  113.8 2.6 multiply_reduce_fusion.10
  117.7 2.6 multiply_reduce_fusion.10
  121.5 2.6 multiply_reduce_fusion.10
  125.4 2.6 multiply_reduce_fusion.10
  129.2 2.6 multiply_reduce_fusion.10
  133.1 2.6 multiply_reduce_fusion.10
  136.1 1.9 collective-permute-start.6
  138.0 7.3 %collective-permute-start.7 = (f32[16,8,128]{2,1,0:T(8,128)S(1)}, f32[16,8,128]{2,1,0:T(8,128)S(1)}, u32[]{:S(2)}, u32[]{:S(2)}) collective-permute-start(f32[16,8,128]{2,1,0:T(8,128)S(1)} %get-tuple-element.454), channel_id=1, source_target_pairs={{1,0},{2,1},{3,2},{4,3},{5,4},{6,5},{7,6},{8,7},{9,8},{10,9},{11,1... | collective-permute-start | bytes 196616 | tf_op jit(solution)/shard_map/ppermute | solution.py:26
  145.7 1.6 collective-permute-done.7
  147.4 30.8 %while.56 = (s32[]{:T(128)}, f32[8,8,3,128]{3,1,2,0:T(8,128)S(1)}, f32[8,8,8,128]{3,2,1,0:T(8,128)S(1)}, s32[8,8,3]{1,2,0:T(4,128)S(1)}, f32[96,8,128]{2,1,0:T(8,128)S(1)}, /*index=5*/s32[8,8]{1,0:T(8,128)S(1)}, s32[]{:T(128)}) while((s32[]{:T(128)}, f32[8,8,3,128]{3,1,2,0:T(8,128)S(1)}, f32[8,8,8,128]{3,2,1,0:T(8,128)S(1)}, ...), condition=%wide.region_19.20_spmd, body=%wide.region_15.19_spmd.sunk | while | flops 12980370 | bytes 1156605 | solution.py:67
  148.6 2.6 multiply_reduce_fusion.11
  152.4 2.6 multiply_reduce_fusion.11
  156.3 2.6 multiply_reduce_fusion.11
  160.1 2.6 multiply_reduce_fusion.11
  164.0 2.6 multiply_reduce_fusion.11
  167.8 2.6 multiply_reduce_fusion.11
  171.7 2.6 multiply_reduce_fusion.11
  175.5 2.6 multiply_reduce_fusion.11
  178.3 0.7 fusion.94
  179.0 0.7 multiply_add_fusion.6
  179.7 102.9 %psum.23 = f32[]{:T(128)} all-reduce(f32[]{:T(128)} %fusion.94), channel_id=1, replica_groups=mesh['rep'=16,'space'=32] {'rep','space'}, use_global_device_ids=true, to_apply=%region_26.27 | all-reduce | flops 1 | bytes 8 | tf_op jit(solution)/shard_map/psum | solution.py:113
  283.3 16.1 %while.57 = (s32[]{:T(128)}, f32[3,1024]{1,0:T(4,128)S(1)}, f32[1024]{0:T(1024)S(1)}, f32[8,8,3,128]{3,2,1,0:T(4,128)S(1)}, s32[8,1024]{1,0:T(8,128)S(1)}, /*index=5*/s32[]{:T(128)}, s32[]{:T(128)}) while((s32[]{:T(128)}, f32[3,1024]{1,0:T(4,128)S(1)}, f32[1024]{0:T(1024)S(1)}, f32[8,8,3,128]{3,2,1,0:T(4,128)S(1)}, ...), condition=%wide.region_22.23_spmd.clone, body=%wide.region_20.22_spmd.clone.sunk | while | flops 41950208 | bytes 77920 | solution.py:110
  283.3 1.5 fusion.147
  285.3 1.5 fusion.147
  287.3 1.5 fusion.147
  289.4 1.5 fusion.147
  291.4 1.5 fusion.147
  293.4 1.5 fusion.147
  295.4 1.5 fusion.147
  297.4 1.5 fusion.147
  299.4 54.4 %all-reduce = (f32[3,1024]{1,0:T(4,128)S(1)}, f32[1024]{0:T(1024)S(1)}) all-reduce(f32[3,1024]{1,0:T(4,128)S(1)} %get-tuple-element.169, f32[1024]{0:T(1024)S(1)} %get-tuple-element.170), channel_id=1, replica_groups=mesh['rep'=16,'space'=32] {'rep'}, use_global_device_ids=true, to_apply=%region_23.24 | all-reduce | flops 4096 | bytes 32768 | tf_op jit(solution)/shard_map/psum | solution.py:111
  (877 shorter events, 41.2 us)
Async XLA Ops:
  1.5 1.1 copy-start
  2.6 12.9 %copy-start.4 = (s32[1,64,3]{1,0,2:T(1,128)S(1)}, s32[1,64,3]{1,0,2:T(1,128)}, u32[]{:S(2)}) copy-start(s32[1,64,3]{1,0,2:T(1,128)} %param.22) | copy-start | bytes 2308
  2.6 13.6 %copy-start.3 = (s32[1,64,128]{2,1,0:T(8,128)S(1)}, s32[1,64,128]{2,1,0:T(8,128)}, u32[]{:S(2)}) copy-start(s32[1,64,128]{2,1,0:T(8,128)} %param.23) | copy-start | bytes 98308
  2.8 13.6 %collective-permute-start = (f32[16,8,128]{2,1,0:T(8,128)S(1)}, f32[16,8,128]{2,1,0:T(8,128)S(1)}, u32[]{:S(2)}, u32[]{:S(2)}) collective-permute-start(f32[16,8,128]{2,1,0:T(8,128)S(1)} %get-tuple-element.459), channel_id=1, source_target_pairs={{0,1},{1,2},{2,3},{3,4},{4,5},{5,6},{6,7},{7,8},{8,9},{9,10},{10,1... | collective-permute-start | bytes 196616 | tf_op jit(solution)/shard_map/ppermute | solution.py:25
  7.1 11.4 %collective-permute-start.1 = (f32[16,8,128]{2,1,0:T(8,128)S(1)}, f32[16,8,128]{2,1,0:T(8,128)S(1)}, u32[]{:S(2)}, u32[]{:S(2)}) collective-permute-start(f32[16,8,128]{2,1,0:T(8,128)S(1)} %get-tuple-element.460), channel_id=1, source_target_pairs={{1,0},{2,1},{3,2},{4,3},{5,4},{6,5},{7,6},{8,7},{9,8},{10,9},{11,1... | collective-permute-start | bytes 196616 | tf_op jit(solution)/shard_map/ppermute | solution.py:26
  49.5 0.9 copy-start.1
  49.5 0.9 copy-start.2
  50.7 9.6 %collective-permute-start.2 = (f32[16,8,128]{2,1,0:T(8,128)S(1)}, f32[16,8,128]{2,1,0:T(8,128)S(1)}, u32[]{:S(2)}, u32[]{:S(2)}) collective-permute-start(f32[16,8,128]{2,1,0:T(8,128)S(1)} %get-tuple-element.457), channel_id=1, source_target_pairs={{0,1},{1,2},{2,3},{3,4},{4,5},{5,6},{6,7},{7,8},{8,9},{9,10},{10,1... | collective-permute-start | bytes 196616 | tf_op jit(solution)/shard_map/ppermute | solution.py:25
  52.7 9.6 %collective-permute-start.3 = (f32[16,8,128]{2,1,0:T(8,128)S(1)}, f32[16,8,128]{2,1,0:T(8,128)S(1)}, u32[]{:S(2)}, u32[]{:S(2)}) collective-permute-start(f32[16,8,128]{2,1,0:T(8,128)S(1)} %get-tuple-element.458), channel_id=1, source_target_pairs={{1,0},{2,1},{3,2},{4,3},{5,4},{6,5},{7,6},{8,7},{9,8},{10,9},{11,1... | collective-permute-start | bytes 196616 | tf_op jit(solution)/shard_map/ppermute | solution.py:26
  93.6 9.6 %collective-permute-start.4 = (f32[16,8,128]{2,1,0:T(8,128)S(1)}, f32[16,8,128]{2,1,0:T(8,128)S(1)}, u32[]{:S(2)}, u32[]{:S(2)}) collective-permute-start(f32[16,8,128]{2,1,0:T(8,128)S(1)} %get-tuple-element.455), channel_id=1, source_target_pairs={{0,1},{1,2},{2,3},{3,4},{4,5},{5,6},{6,7},{7,8},{8,9},{9,10},{10,1... | collective-permute-start | bytes 196616 | tf_op jit(solution)/shard_map/ppermute | solution.py:25
  95.5 9.3 %collective-permute-start.5 = (f32[16,8,128]{2,1,0:T(8,128)S(1)}, f32[16,8,128]{2,1,0:T(8,128)S(1)}, u32[]{:S(2)}, u32[]{:S(2)}) collective-permute-start(f32[16,8,128]{2,1,0:T(8,128)S(1)} %get-tuple-element.456), channel_id=1, source_target_pairs={{1,0},{2,1},{3,2},{4,3},{5,4},{6,5},{7,6},{8,7},{9,8},{10,9},{11,1... | collective-permute-start | bytes 196616 | tf_op jit(solution)/shard_map/ppermute | solution.py:26
  136.1 9.6 %collective-permute-start.6 = (f32[16,8,128]{2,1,0:T(8,128)S(1)}, f32[16,8,128]{2,1,0:T(8,128)S(1)}, u32[]{:S(2)}, u32[]{:S(2)}) collective-permute-start(f32[16,8,128]{2,1,0:T(8,128)S(1)} %get-tuple-element.453), channel_id=1, source_target_pairs={{0,1},{1,2},{2,3},{3,4},{4,5},{5,6},{6,7},{7,8},{8,9},{9,10},{10,1... | collective-permute-start | bytes 196616 | tf_op jit(solution)/shard_map/ppermute | solution.py:25
  138.0 9.2 %collective-permute-start.7 = (f32[16,8,128]{2,1,0:T(8,128)S(1)}, f32[16,8,128]{2,1,0:T(8,128)S(1)}, u32[]{:S(2)}, u32[]{:S(2)}) collective-permute-start(f32[16,8,128]{2,1,0:T(8,128)S(1)} %get-tuple-element.454), channel_id=1, source_target_pairs={{1,0},{2,1},{3,2},{4,3},{5,4},{6,5},{7,6},{8,7},{9,8},{10,9},{11,1... | collective-permute-start | bytes 196616 | tf_op jit(solution)/shard_map/ppermute | solution.py:26
  283.3 71.2 %copy-start.5 = (f32[1,3,128]{2,0,1:T(1,128)S(1)}, f32[1,3,128]{2,0,1:T(1,128)}, u32[]{:S(2)}) copy-start(f32[1,3,128]{2,0,1:T(1,128)} %param.24) | copy-start | bytes 4612
where the time goes:
time: 356 us; the launch traced here: 355 us
  blocking collectives  157 us (44%)
  other arithmetic  94.4 us (27%)
  starting transfers between devices  40.5 us (11%)
  local copies, waits for them, and re-layouts  34.7 us (10%)
  matrix products  11.7 us (3%)
  waiting for transfers between devices  7.66 us (2%)
  loops' own time  6.37 us (2%)
    psum x1, blocking collectives, shards(): flux_sum = lax.psum(jnp.sum(speed[:, 0, :]), ('rep', 'space'))  103 us
    reduce_sum x32, other arithmetic, bead_forces(): jnp.sum(factor * offset_x, axis=(0, 2))  84.4 us
    psum x1, blocking collectives, shards(): momentum, counts = lax.psum((momentum, counts), 'rep')  54.4 us
    ppermute x4, starting transfers between devices, padded(): after = lax.ppermute(initial, axis, down)  30.4 us
    gather x32, local copies, waits for them, and re-layouts, per_group(): partners = extended[link_group]  18.5 us
    dot_general x8, matrix products, accumulate(): jnp.dot(rows_now, table, precision=lax.Precision.HIGHEST, preferred_eleme...  11.7 us
    ppermute x4, starting transfers between devices, padded(): before = lax.ppermute(last, axis, up)  10 us
    ppermute x4, waiting for transfers between devices, padded(): after = lax.ppermute(initial, axis, down)  7.15 us
  transfers between devices with their start and end apart: 8, of which 7 were waited for; matrix products, arithmetic and copies ran while one was open for 0% of the time, Pallas kernels for 0%

commit v1 on v0

--- a/solution.py
+++ b/solution.py
@@ -25,6 +25,22 @@
         before = lax.ppermute(last, axis, up)
         after = lax.ppermute(initial, axis, down)
         value = jnp.concatenate([before, value, after], axis=dim)
+    return value
+
+
+def butterfly_sum(value, axis, radix=4):
+    count = lax.axis_size(axis)
+    stride = 1
+    while stride < count:
+        group = min(radix, count // stride)
+        leaves = [value]
+        for j in range(1, group):
+            pairs = [(i, i ^ (j * stride)) for i in range(count)]
+            leaves.append(lax.ppermute(value, axis, pairs))
+        while len(leaves) > 1:
+            leaves = [leaves[k] + leaves[k + 1] for k in range(0, len(leaves), 2)]
+        value = leaves[0]
+        stride *= group
     return value
 
 
@@ -108,9 +124,15 @@
 
     start = (jnp.zeros((3, BINS_DEV), jnp.float32), jnp.zeros((BINS_DEV,), jnp.float32))
     (momentum, counts), unused = lax.scan(accumulate, start, (grouped_speed, grouped_bins))
-    momentum, counts = lax.psum((momentum, counts), "rep")
+    local_flux = jnp.sum(speed[:, 0, :])
+    packed = jnp.concatenate(
+        [momentum, counts[None, :], jnp.full((4, BINS_DEV), local_flux, jnp.float32)], axis=0
+    )
+    packed = butterfly_sum(packed, "rep")
+    momentum, counts = packed[0:3], packed[3]
+    slab_flux = jnp.full((8, 128), packed[4, 0], jnp.float32)
+    flux_sum = butterfly_sum(slab_flux, "space")[0, 0]
     bin_velocity = momentum / counts[None, :]
-    flux_sum = lax.psum(jnp.sum(speed[:, 0, :]), ("rep", "space"))
     total_beads = lax.axis_size("rep") * lax.axis_size("space") * tiles * width
     inflow = 2.0 * TARGET_FLOW - flux_sum / total_beads
     slots = jnp.arange(thermal.shape[-1], dtype=jnp.int32)

time: 356 us -> 280 us (0.79)
  the two profiles are of different devices: /device:TPU:16 before, /device:TPU:8 now
where the time goes in v1:
time: 280 us; the launch traced here: 279 us
  other arithmetic  95.2 us (34%)
  starting transfers between devices  77.4 us (28%)
  waiting for transfers between devices  48.6 us (17%)
  local copies, waits for them, and re-layouts  37.1 us (13%)
  matrix products  11.7 us (4%)
  loops' own time  6.34 us (2%)
    reduce_sum x32, other arithmetic, bead_forces(): jnp.sum(factor * offset_x, axis=(0, 2))  84.4 us
    ppermute x13, starting transfers between devices, butterfly_sum(): leaves.append(lax.ppermute(value, axis, pairs))  54.6 us
    ppermute x13, waiting for transfers between devices, butterfly_sum(): leaves.append(lax.ppermute(value, axis, pairs))  27.9 us
    ppermute x4, waiting for transfers between devices, padded(): after = lax.ppermute(initial, axis, down)  19 us
    gather x32, local copies, waits for them, and re-layouts, per_group(): partners = extended[link_group]  18.5 us
    ppermute x4, starting transfers between devices, padded(): before = lax.ppermute(last, axis, up)  17.6 us
    dot_general x8, matrix products, accumulate(): jnp.dot(rows_now, table, precision=lax.Precision.HIGHEST, preferred_eleme...  11.7 us
    another operation x4, loops' own time, slab_forces(): lax.map(per_group, (own_tiles.reshape(tiles // group, group, 8, width), l...  6.03 us
  transfers between devices with their start and end apart: 21, of which 13 were waited for; matrix products, arithmetic and copies ran while one was open for 1% of the time, Pallas kernels for 0%

profile of v1, /device:TPU:8, one launch (start us, length us, event | category | flops | bytes accessed | tf_op | source)
XLA Modules:
  0.0 278.9 jit_solution(11519129999141517834)
XLA Ops:
  2.8 4.3 %collective-permute-start = (f32[16,8,128]{2,1,0:T(8,128)S(1)}, f32[16,8,128]{2,1,0:T(8,128)S(1)}, u32[]{:S(2)}, u32[]{:S(2)}) collective-permute-start(f32[16,8,128]{2,1,0:T(8,128)S(1)} %get-tuple-element.457), channel_id=1, source_target_pairs={{0,1},{1,2},{2,3},{3,4},{4,5},{5,6},{6,7},{7,8},{8,9},{9,10},{10,1... | collective-permute-start | bytes 196616 | tf_op jit(solution)/shard_map/ppermute | solution.py:25
  8.9 4.6 %collective-permute-done.1 = f32[16,8,128]{2,1,0:T(8,128)S(1)} collective-permute-done((f32[16,8,128]{2,1,0:T(8,128)S(1)}, f32[16,8,128]{2,1,0:T(8,128)S(1)}, u32[]{:S(2)}, u32[]{:S(2)}) %collective-permute-start.1) | collective-permute-done | bytes 65568 | tf_op jit(solution)/shard_map/ppermute | solution.py:26
  13.7 30.8 %while.53 = (s32[]{:T(128)}, f32[8,8,3,128]{3,1,2,0:T(8,128)S(1)}, f32[8,8,8,128]{3,2,1,0:T(8,128)S(1)}, s32[8,8,3]{1,2,0:T(4,128)S(1)}, f32[96,8,128]{2,1,0:T(8,128)S(1)}, /*index=5*/s32[8,8]{1,0:T(8,128)S(1)}, s32[]{:T(128)}) while((s32[]{:T(128)}, f32[8,8,3,128]{3,1,2,0:T(8,128)S(1)}, f32[8,8,8,128]{3,2,1,0:T(8,128)S(1)}, ...), condition=%wide.region_4.5_spmd, body=%wide.region_0.4_spmd.sunk | while | flops 12980370 | bytes 1156605 | solution.py:83
  14.9 2.6 multiply_reduce_fusion.8
  18.8 2.6 multiply_reduce_fusion.8
  22.6 2.6 multiply_reduce_fusion.8
  26.5 2.6 multiply_reduce_fusion.8
  30.3 2.6 multiply_reduce_fusion.8
  34.2 2.6 multiply_reduce_fusion.8
  38.0 2.6 multiply_reduce_fusion.8
  41.9 2.6 multiply_reduce_fusion.8
  45.8 4.3 %collective-permute-start.2 = (f32[16,8,128]{2,1,0:T(8,128)S(1)}, f32[16,8,128]{2,1,0:T(8,128)S(1)}, u32[]{:S(2)}, u32[]{:S(2)}) collective-permute-start(f32[16,8,128]{2,1,0:T(8,128)S(1)} %get-tuple-element.455), channel_id=1, source_target_pairs={{0,1},{1,2},{2,3},{3,4},{4,5},{5,6},{6,7},{7,8},{8,9},{9,10},{10,1... | collective-permute-start | bytes 196616 | tf_op jit(solution)/shard_map/ppermute | solution.py:25
  52.0 5.8 %collective-permute-done.3 = f32[16,8,128]{2,1,0:T(8,128)S(1)} collective-permute-done((f32[16,8,128]{2,1,0:T(8,128)S(1)}, f32[16,8,128]{2,1,0:T(8,128)S(1)}, u32[]{:S(2)}, u32[]{:S(2)}) %collective-permute-start.3) | collective-permute-done | bytes 65568 | tf_op jit(solution)/shard_map/ppermute | solution.py:26
  58.0 30.8 %while.54 = (s32[]{:T(128)}, f32[8,8,3,128]{3,1,2,0:T(8,128)S(1)}, f32[8,8,8,128]{3,2,1,0:T(8,128)S(1)}, s32[8,8,3]{1,2,0:T(4,128)S(1)}, f32[96,8,128]{2,1,0:T(8,128)S(1)}, /*index=5*/s32[8,8]{1,0:T(8,128)S(1)}, s32[]{:T(128)}) while((s32[]{:T(128)}, f32[8,8,3,128]{3,1,2,0:T(8,128)S(1)}, f32[8,8,8,128]{3,2,1,0:T(8,128)S(1)}, ...), condition=%wide.region_9.10_spmd, body=%wide.region_5.9_spmd.sunk | while | flops 12980370 | bytes 1156605 | solution.py:83
  59.2 2.6 multiply_reduce_fusion.9
  63.0 2.6 multiply_reduce_fusion.9
  66.9 2.6 multiply_reduce_fusion.9
  70.7 2.6 multiply_reduce_fusion.9
  74.6 2.6 multiply_reduce_fusion.9
  78.4 2.6 multiply_reduce_fusion.9
  82.3 2.6 multiply_reduce_fusion.9
  86.1 2.6 multiply_reduce_fusion.9
  89.2 5.1 %collective-permute-start.4 = (f32[16,8,128]{2,1,0:T(8,128)S(1)}, f32[16,8,128]{2,1,0:T(8,128)S(1)}, u32[]{:S(2)}, u32[]{:S(2)}) collective-permute-start(f32[16,8,128]{2,1,0:T(8,128)S(1)} %get-tuple-element.453), channel_id=1, source_target_pairs={{0,1},{1,2},{2,3},{3,4},{4,5},{5,6},{6,7},{7,8},{8,9},{9,10},{10,1... | collective-permute-start | bytes 196616 | tf_op jit(solution)/shard_map/ppermute | solution.py:25
  96.2 4.3 %collective-permute-done.5 = f32[16,8,128]{2,1,0:T(8,128)S(1)} collective-permute-done((f32[16,8,128]{2,1,0:T(8,128)S(1)}, f32[16,8,128]{2,1,0:T(8,128)S(1)}, u32[]{:S(2)}, u32[]{:S(2)}) %collective-permute-start.5) | collective-permute-done | bytes 65568 | tf_op jit(solution)/shard_map/ppermute | solution.py:26
  100.6 30.8 %while.55 = (s32[]{:T(128)}, f32[8,8,3,128]{3,1,2,0:T(8,128)S(1)}, f32[8,8,8,128]{3,2,1,0:T(8,128)S(1)}, s32[8,8,3]{1,2,0:T(4,128)S(1)}, f32[96,8,128]{2,1,0:T(8,128)S(1)}, /*index=5*/s32[8,8]{1,0:T(8,128)S(1)}, s32[]{:T(128)}) while((s32[]{:T(128)}, f32[8,8,3,128]{3,1,2,0:T(8,128)S(1)}, f32[8,8,8,128]{3,2,1,0:T(8,128)S(1)}, ...), condition=%wide.region_14.15_spmd, body=%wide.region_10.14_spmd.sunk | while | flops 12980370 | bytes 1156605 | solution.py:83
  101.8 2.6 multiply_reduce_fusion.10
  105.6 2.6 multiply_reduce_fusion.10
  109.5 2.6 multiply_reduce_fusion.10
  113.3 2.6 multiply_reduce_fusion.10
  117.2 2.6 multiply_reduce_fusion.10
  121.0 2.6 multiply_reduce_fusion.10
  124.9 2.6 multiply_reduce_fusion.10
  128.8 2.6 multiply_reduce_fusion.10
  131.8 3.9 %collective-permute-start.6 = (f32[16,8,128]{2,1,0:T(8,128)S(1)}, f32[16,8,128]{2,1,0:T(8,128)S(1)}, u32[]{:S(2)}, u32[]{:S(2)}) collective-permute-start(f32[16,8,128]{2,1,0:T(8,128)S(1)} %get-tuple-element.451), channel_id=1, source_target_pairs={{0,1},{1,2},{2,3},{3,4},{4,5},{5,6},{6,7},{7,8},{8,9},{9,10},{10,1... | collective-permute-start | bytes 196616 | tf_op jit(solution)/shard_map/ppermute | solution.py:25
  137.6 4.3 %collective-permute-done.7 = f32[16,8,128]{2,1,0:T(8,128)S(1)} collective-permute-done((f32[16,8,128]{2,1,0:T(8,128)S(1)}, f32[16,8,128]{2,1,0:T(8,128)S(1)}, u32[]{:S(2)}, u32[]{:S(2)}) %collective-permute-start.7) | collective-permute-done | bytes 65568 | tf_op jit(solution)/shard_map/ppermute | solution.py:26
  142.0 30.8 %while.56 = (s32[]{:T(128)}, f32[8,8,3,128]{3,1,2,0:T(8,128)S(1)}, f32[8,8,8,128]{3,2,1,0:T(8,128)S(1)}, s32[8,8,3]{1,2,0:T(4,128)S(1)}, f32[96,8,128]{2,1,0:T(8,128)S(1)}, /*index=5*/s32[8,8]{1,0:T(8,128)S(1)}, s32[]{:T(128)}) while((s32[]{:T(128)}, f32[8,8,3,128]{3,1,2,0:T(8,128)S(1)}, f32[8,8,8,128]{3,2,1,0:T(8,128)S(1)}, ...), condition=%wide.region_19.20_spmd, body=%wide.region_15.19_spmd.sunk | while | flops 12980370 | bytes 1156605 | solution.py:83
  143.2 2.6 multiply_reduce_fusion.11
  147.1 2.6 multiply_reduce_fusion.11
  150.9 2.6 multiply_reduce_fusion.11
  154.8 2.6 multiply_reduce_fusion.11
  158.6 2.6 multiply_reduce_fusion.11
  162.5 2.6 multiply_reduce_fusion.11
  166.3 2.6 multiply_reduce_fusion.11
  170.2 2.6 multiply_reduce_fusion.11
  173.6 16.0 %while.57 = (s32[]{:T(128)}, f32[3,1024]{1,0:T(4,128)S(1)}, f32[1024]{0:T(1024)S(1)}, f32[8,8,3,128]{3,2,1,0:T(4,128)S(1)}, s32[8,1024]{1,0:T(8,128)S(1)}, /*index=5*/s32[]{:T(128)}, s32[]{:T(128)}) while((s32[]{:T(128)}, f32[3,1024]{1,0:T(4,128)S(1)}, f32[1024]{0:T(1024)S(1)}, f32[8,8,3,128]{3,2,1,0:T(4,128)S(1)}, ...), condition=%wide.region_22.23_spmd.clone, body=%wide.region_20.22_spmd.clone.sunk | while | flops 41950208 | bytes 77920 | solution.py:126
  175.6 1.5 fusion.147
  190.5 1.9 collective-permute-start.10
  192.4 3.5 %collective-permute-start.8 = (f32[8,1024]{1,0:T(8,128)S(1)}, f32[8,1024]{1,0:T(8,128)S(1)}, u32[]{:S(2)}, u32[]{:S(2)}) collective-permute-start(f32[8,1024]{1,0:T(8,128)S(1)} %maximum_maximum_fusion), channel_id=1, source_target_pairs={{0,32},{32,0},{64,96},{96,64},{128,160},{160,128},{192,224},{224,1... | collective-permute-start | bytes 98312 | tf_op jit(solution)/shard_map/ppermute | solution.py:39
  195.9 2.4 collective-permute-start.9
  198.4 3.3 %collective-permute-done.9 = f32[8,1024]{1,0:T(8,128)S(1)} collective-permute-done((f32[8,1024]{1,0:T(8,128)S(1)}, f32[8,1024]{1,0:T(8,128)S(1)}, u32[]{:S(2)}, u32[]{:S(2)}) %collective-permute-start.9) | collective-permute-done | bytes 32800 | tf_op jit(solution)/shard_map/ppermute | solution.py:39
  201.8 4.6 %collective-permute-start.11 = (f32[8,1024]{1,0:T(8,128)S(1)}, f32[8,1024]{1,0:T(8,128)S(1)}, u32[]{:S(2)}, u32[]{:S(2)}) collective-permute-start(f32[8,1024]{1,0:T(8,128)S(1)} %add_add_fusion.1), channel_id=1, source_target_pairs={{0,128},{32,160},{64,192},{96,224},{128,0},{160,32},{192,64},{224,... | collective-permute-start | bytes 98312 | tf_op jit(solution)/shard_map/ppermute | solution.py:39
  206.4 2.4 collective-permute-start.12
  208.8 3.7 %collective-permute-start.13 = (f32[8,1024]{1,0:T(8,128)S(1)}, f32[8,1024]{1,0:T(8,128)S(1)}, u32[]{:S(2)}, u32[]{:S(2)}) collective-permute-start(f32[8,1024]{1,0:T(8,128)S(1)} %add_add_fusion.1), channel_id=1, source_target_pairs={{0,384},{32,416},{64,448},{96,480},{128,256},{160,288},{192,320},{... | collective-permute-start | bytes 98312 | tf_op jit(solution)/shard_map/ppermute | solution.py:39
  213.2 3.8 %collective-permute-done.13 = f32[8,1024]{1,0:T(8,128)S(1)} collective-permute-done((f32[8,1024]{1,0:T(8,128)S(1)}, f32[8,1024]{1,0:T(8,128)S(1)}, u32[]{:S(2)}, u32[]{:S(2)}) %collective-permute-start.13) | collective-permute-done | bytes 32800 | tf_op jit(solution)/shard_map/ppermute | solution.py:39
  218.2 3.4 %collective-permute-start.14 = (f32[8,128]{1,0:T(8,128)S(1)}, f32[8,128]{1,0:T(8,128)S(1)}, u32[]{:S(2)}, u32[]{:S(2)}) collective-permute-start(f32[8,128]{1,0:T(8,128)S(1)} %broadcast_in_dim.74), channel_id=1, source_target_pairs={{0,1},{1,0},{2,3},{3,2},{4,5},{5,4},{6,7},{7,6},{8,9},{9,8},{10,11... | collective-permute-start | bytes 12296 | tf_op jit(solution)/shard_map/ppermute | solution.py:39
  221.6 6.8 %collective-permute-start.15 = (f32[8,128]{1,0:T(8,128)S(1)}, f32[8,128]{1,0:T(8,128)S(1)}, u32[]{:S(2)}, u32[]{:S(2)}) collective-permute-start(f32[8,128]{1,0:T(8,128)S(1)} %broadcast_in_dim.74), channel_id=1, source_target_pairs={{0,2},{1,3},{2,0},{3,1},{4,6},{5,7},{6,4},{7,5},{8,10},{9,11},{10,... | collective-permute-start | bytes 12296 | tf_op jit(solution)/shard_map/ppermute | solution.py:39
  228.4 1.9 collective-permute-start.16
  230.3 5.3 %collective-permute-done.16 = f32[8,128]{1,0:T(8,128)S(1)} collective-permute-done((f32[8,128]{1,0:T(8,128)S(1)}, f32[8,128]{1,0:T(8,128)S(1)}, u32[]{:S(2)}, u32[]{:S(2)}) %collective-permute-start.16) | collective-permute-done | bytes 4128 | tf_op jit(solution)/shard_map/ppermute | solution.py:39
  236.3 10.3 %collective-permute-start.17 = (f32[8,128]{1,0:T(8,128)S(1)}, f32[8,128]{1,0:T(8,128)S(1)}, u32[]{:S(2)}, u32[]{:S(2)}) collective-permute-start(f32[8,128]{1,0:T(8,128)S(1)} %add_add_fusion.3), channel_id=1, source_target_pairs={{0,4},{1,5},{2,6},{3,7},{4,0},{5,1},{6,2},{7,3},{8,12},{9,13},{10,... | collective-permute-start | bytes 12296 | tf_op jit(solution)/shard_map/ppermute | solution.py:39
  246.7 9.8 %collective-permute-start.18 = (f32[8,128]{1,0:T(8,128)S(1)}, f32[8,128]{1,0:T(8,128)S(1)}, u32[]{:S(2)}, u32[]{:S(2)}) collective-permute-start(f32[8,128]{1,0:T(8,128)S(1)} %add_add_fusion.3), channel_id=1, source_target_pairs={{0,8},{1,9},{2,10},{3,11},{4,12},{5,13},{6,14},{7,15},{8,0},{9,1},... | collective-permute-start | bytes 12296 | tf_op jit(solution)/shard_map/ppermute | solution.py:39
  256.5 1.9 collective-permute-start.19
  259.2 8.5 %collective-permute-done.19 = f32[8,128]{1,0:T(8,128)S(1)} collective-permute-done((f32[8,128]{1,0:T(8,128)S(1)}, f32[8,128]{1,0:T(8,128)S(1)}, u32[]{:S(2)}, u32[]{:S(2)}) %collective-permute-start.19) | collective-permute-done | bytes 4128 | tf_op jit(solution)/shard_map/ppermute | solution.py:39
  267.7 1.9 collective-permute-start.20
  270.2 6.9 %collective-permute-done.20 = f32[8,128]{1,0:T(8,128)S(1)} collective-permute-done((f32[8,128]{1,0:T(8,128)S(1)}, f32[8,128]{1,0:T(8,128)S(1)}, u32[]{:S(2)}, u32[]{:S(2)}) %collective-permute-start.20) | collective-permute-done | bytes 4128 | tf_op jit(solution)/shard_map/ppermute | solution.py:39
  (913 shorter events, 65.0 us)
Async XLA Ops:
  1.5 1.1 copy-start
  2.6 5.8 %copy-start.4 = (s32[1,64,3]{1,0,2:T(1,128)S(1)}, s32[1,64,3]{1,0,2:T(1,128)}, u32[]{:S(2)}) copy-start(s32[1,64,3]{1,0,2:T(1,128)} %param.22) | copy-start | bytes 2308
  2.6 5.9 %copy-start.3 = (s32[1,64,128]{2,1,0:T(8,128)S(1)}, s32[1,64,128]{2,1,0:T(8,128)}, u32[]{:S(2)}) copy-start(s32[1,64,128]{2,1,0:T(8,128)} %param.23) | copy-start | bytes 98308
  2.8 6.2 %collective-permute-start = (f32[16,8,128]{2,1,0:T(8,128)S(1)}, f32[16,8,128]{2,1,0:T(8,128)S(1)}, u32[]{:S(2)}, u32[]{:S(2)}) collective-permute-start(f32[16,8,128]{2,1,0:T(8,128)S(1)} %get-tuple-element.457), channel_id=1, source_target_pairs={{0,1},{1,2},{2,3},{3,4},{4,5},{5,6},{6,7},{7,8},{8,9},{9,10},{10,1... | collective-permute-start | bytes 196616 | tf_op jit(solution)/shard_map/ppermute | solution.py:25
  7.1 6.5 %collective-permute-start.1 = (f32[16,8,128]{2,1,0:T(8,128)S(1)}, f32[16,8,128]{2,1,0:T(8,128)S(1)}, u32[]{:S(2)}, u32[]{:S(2)}) collective-permute-start(f32[16,8,128]{2,1,0:T(8,128)S(1)} %get-tuple-element.458), channel_id=1, source_target_pairs={{1,0},{2,1},{3,2},{4,3},{5,4},{6,5},{7,6},{8,7},{9,8},{10,9},{11,1... | collective-permute-start | bytes 196616 | tf_op jit(solution)/shard_map/ppermute | solution.py:26
  44.5 0.9 copy-start.1
  44.6 0.9 copy-start.2
  45.8 6.2 %collective-permute-start.2 = (f32[16,8,128]{2,1,0:T(8,128)S(1)}, f32[16,8,128]{2,1,0:T(8,128)S(1)}, u32[]{:S(2)}, u32[]{:S(2)}) collective-permute-start(f32[16,8,128]{2,1,0:T(8,128)S(1)} %get-tuple-element.455), channel_id=1, source_target_pairs={{0,1},{1,2},{2,3},{3,4},{4,5},{5,6},{6,7},{7,8},{8,9},{9,10},{10,1... | collective-permute-start | bytes 196616 | tf_op jit(solution)/shard_map/ppermute | solution.py:25
  50.1 7.7 %collective-permute-start.3 = (f32[16,8,128]{2,1,0:T(8,128)S(1)}, f32[16,8,128]{2,1,0:T(8,128)S(1)}, u32[]{:S(2)}, u32[]{:S(2)}) collective-permute-start(f32[16,8,128]{2,1,0:T(8,128)S(1)} %get-tuple-element.456), channel_id=1, source_target_pairs={{1,0},{2,1},{3,2},{4,3},{5,4},{6,5},{7,6},{8,7},{9,8},{10,9},{11,1... | collective-permute-start | bytes 196616 | tf_op jit(solution)/shard_map/ppermute | solution.py:26
  89.2 7.0 %collective-permute-start.4 = (f32[16,8,128]{2,1,0:T(8,128)S(1)}, f32[16,8,128]{2,1,0:T(8,128)S(1)}, u32[]{:S(2)}, u32[]{:S(2)}) collective-permute-start(f32[16,8,128]{2,1,0:T(8,128)S(1)} %get-tuple-element.453), channel_id=1, source_target_pairs={{0,1},{1,2},{2,3},{3,4},{4,5},{5,6},{6,7},{7,8},{8,9},{9,10},{10,1... | collective-permute-start | bytes 196616 | tf_op jit(solution)/shard_map/ppermute | solution.py:25
  94.3 6.2 %collective-permute-start.5 = (f32[16,8,128]{2,1,0:T(8,128)S(1)}, f32[16,8,128]{2,1,0:T(8,128)S(1)}, u32[]{:S(2)}, u32[]{:S(2)}) collective-permute-start(f32[16,8,128]{2,1,0:T(8,128)S(1)} %get-tuple-element.454), channel_id=1, source_target_pairs={{1,0},{2,1},{3,2},{4,3},{5,4},{6,5},{7,6},{8,7},{9,8},{10,9},{11,1... | collective-permute-start | bytes 196616 | tf_op jit(solution)/shard_map/ppermute | solution.py:26
  131.8 5.8 %collective-permute-start.6 = (f32[16,8,128]{2,1,0:T(8,128)S(1)}, f32[16,8,128]{2,1,0:T(8,128)S(1)}, u32[]{:S(2)}, u32[]{:S(2)}) collective-permute-start(f32[16,8,128]{2,1,0:T(8,128)S(1)} %get-tuple-element.451), channel_id=1, source_target_pairs={{0,1},{1,2},{2,3},{3,4},{4,5},{5,6},{6,7},{7,8},{8,9},{9,10},{10,1... | collective-permute-start | bytes 196616 | tf_op jit(solution)/shard_map/ppermute | solution.py:25
  135.7 6.2 %collective-permute-start.7 = (f32[16,8,128]{2,1,0:T(8,128)S(1)}, f32[16,8,128]{2,1,0:T(8,128)S(1)}, u32[]{:S(2)}, u32[]{:S(2)}) collective-permute-start(f32[16,8,128]{2,1,0:T(8,128)S(1)} %get-tuple-element.452), channel_id=1, source_target_pairs={{1,0},{2,1},{3,2},{4,3},{5,4},{6,5},{7,6},{8,7},{9,8},{10,9},{11,1... | collective-permute-start | bytes 196616 | tf_op jit(solution)/shard_map/ppermute | solution.py:26
  190.5 7.9 %collective-permute-start.10 = (f32[8,1024]{1,0:T(8,128)S(1)}, f32[8,1024]{1,0:T(8,128)S(1)}, u32[]{:S(2)}, u32[]{:S(2)}) collective-permute-start(f32[8,1024]{1,0:T(8,128)S(1)} %maximum_maximum_fusion), channel_id=1, source_target_pairs={{0,96},{32,64},{64,32},{96,0},{128,224},{160,192},{192,160},{224,1... | collective-permute-start | bytes 98312 | tf_op jit(solution)/shard_map/ppermute | solution.py:39
  192.4 6.0 %collective-permute-start.8 = (f32[8,1024]{1,0:T(8,128)S(1)}, f32[8,1024]{1,0:T(8,128)S(1)}, u32[]{:S(2)}, u32[]{:S(2)}) collective-permute-start(f32[8,1024]{1,0:T(8,128)S(1)} %maximum_maximum_fusion), channel_id=1, source_target_pairs={{0,32},{32,0},{64,96},{96,64},{128,160},{160,128},{192,224},{224,1... | collective-permute-start | bytes 98312 | tf_op jit(solution)/shard_map/ppermute | solution.py:39
  195.9 5.8 %collective-permute-start.9 = (f32[8,1024]{1,0:T(8,128)S(1)}, f32[8,1024]{1,0:T(8,128)S(1)}, u32[]{:S(2)}, u32[]{:S(2)}) collective-permute-start(f32[8,1024]{1,0:T(8,128)S(1)} %maximum_maximum_fusion), channel_id=1, source_target_pairs={{0,64},{32,96},{64,0},{96,32},{128,192},{160,224},{192,128},{224,1... | collective-permute-start | bytes 98312 | tf_op jit(solution)/shard_map/ppermute | solution.py:39
  201.8 11.4 %collective-permute-start.11 = (f32[8,1024]{1,0:T(8,128)S(1)}, f32[8,1024]{1,0:T(8,128)S(1)}, u32[]{:S(2)}, u32[]{:S(2)}) collective-permute-start(f32[8,1024]{1,0:T(8,128)S(1)} %add_add_fusion.1), channel_id=1, source_target_pairs={{0,128},{32,160},{64,192},{96,224},{128,0},{160,32},{192,64},{224,... | collective-permute-start | bytes 98312 | tf_op jit(solution)/shard_map/ppermute | solution.py:39
  206.4 6.8 %collective-permute-start.12 = (f32[8,1024]{1,0:T(8,128)S(1)}, f32[8,1024]{1,0:T(8,128)S(1)}, u32[]{:S(2)}, u32[]{:S(2)}) collective-permute-start(f32[8,1024]{1,0:T(8,128)S(1)} %add_add_fusion.1), channel_id=1, source_target_pairs={{0,256},{32,288},{64,320},{96,352},{128,384},{160,416},{192,448},{... | collective-permute-start | bytes 98312 | tf_op jit(solution)/shard_map/ppermute | solution.py:39
  208.8 8.2 %collective-permute-start.13 = (f32[8,1024]{1,0:T(8,128)S(1)}, f32[8,1024]{1,0:T(8,128)S(1)}, u32[]{:S(2)}, u32[]{:S(2)}) collective-permute-start(f32[8,1024]{1,0:T(8,128)S(1)} %add_add_fusion.1), channel_id=1, source_target_pairs={{0,384},{32,416},{64,448},{96,480},{128,256},{160,288},{192,320},{... | collective-permute-start | bytes 98312 | tf_op jit(solution)/shard_map/ppermute | solution.py:39
  218.2 12.2 %collective-permute-start.14 = (f32[8,128]{1,0:T(8,128)S(1)}, f32[8,128]{1,0:T(8,128)S(1)}, u32[]{:S(2)}, u32[]{:S(2)}) collective-permute-start(f32[8,128]{1,0:T(8,128)S(1)} %broadcast_in_dim.74), channel_id=1, source_target_pairs={{0,1},{1,0},{2,3},{3,2},{4,5},{5,4},{6,7},{7,6},{8,9},{9,8},{10,11... | collective-permute-start | bytes 12296 | tf_op jit(solution)/shard_map/ppermute | solution.py:39
  221.6 8.8 %collective-permute-start.15 = (f32[8,128]{1,0:T(8,128)S(1)}, f32[8,128]{1,0:T(8,128)S(1)}, u32[]{:S(2)}, u32[]{:S(2)}) collective-permute-start(f32[8,128]{1,0:T(8,128)S(1)} %broadcast_in_dim.74), channel_id=1, source_target_pairs={{0,2},{1,3},{2,0},{3,1},{4,6},{5,7},{6,4},{7,5},{8,10},{9,11},{10,... | collective-permute-start | bytes 12296 | tf_op jit(solution)/shard_map/ppermute | solution.py:39
  228.4 7.3 %collective-permute-start.16 = (f32[8,128]{1,0:T(8,128)S(1)}, f32[8,128]{1,0:T(8,128)S(1)}, u32[]{:S(2)}, u32[]{:S(2)}) collective-permute-start(f32[8,128]{1,0:T(8,128)S(1)} %broadcast_in_dim.74), channel_id=1, source_target_pairs={{0,3},{1,2},{2,1},{3,0},{4,7},{5,6},{6,5},{7,4},{8,11},{9,10},{10,... | collective-permute-start | bytes 12296 | tf_op jit(solution)/shard_map/ppermute | solution.py:39
  236.3 42.0 %copy-start.5 = (f32[1,3,128]{2,0,1:T(1,128)S(1)}, f32[1,3,128]{2,0,1:T(1,128)}, u32[]{:S(2)}) copy-start(f32[1,3,128]{2,0,1:T(1,128)} %param.24) | copy-start | bytes 4612
  236.3 22.8 %collective-permute-start.17 = (f32[8,128]{1,0:T(8,128)S(1)}, f32[8,128]{1,0:T(8,128)S(1)}, u32[]{:S(2)}, u32[]{:S(2)}) collective-permute-start(f32[8,128]{1,0:T(8,128)S(1)} %add_add_fusion.3), channel_id=1, source_target_pairs={{0,4},{1,5},{2,6},{3,7},{4,0},{5,1},{6,2},{7,3},{8,12},{9,13},{10,... | collective-permute-start | bytes 12296 | tf_op jit(solution)/shard_map/ppermute | solution.py:39
  246.7 12.5 %collective-permute-start.18 = (f32[8,128]{1,0:T(8,128)S(1)}, f32[8,128]{1,0:T(8,128)S(1)}, u32[]{:S(2)}, u32[]{:S(2)}) collective-permute-start(f32[8,128]{1,0:T(8,128)S(1)} %add_add_fusion.3), channel_id=1, source_target_pairs={{0,8},{1,9},{2,10},{3,11},{4,12},{5,13},{6,14},{7,15},{8,0},{9,1},... | collective-permute-start | bytes 12296 | tf_op jit(solution)/shard_map/ppermute | solution.py:39
  256.5 11.2 %collective-permute-start.19 = (f32[8,128]{1,0:T(8,128)S(1)}, f32[8,128]{1,0:T(8,128)S(1)}, u32[]{:S(2)}, u32[]{:S(2)}) collective-permute-start(f32[8,128]{1,0:T(8,128)S(1)} %add_add_fusion.3), channel_id=1, source_target_pairs={{0,12},{1,13},{2,14},{3,15},{4,8},{5,9},{6,10},{7,11},{8,4},{9,5},... | collective-permute-start | bytes 12296 | tf_op jit(solution)/shard_map/ppermute | solution.py:39
  267.7 9.4 %collective-permute-start.20 = (f32[8,128]{1,0:T(8,128)S(1)}, f32[8,128]{1,0:T(8,128)S(1)}, u32[]{:S(2)}, u32[]{:S(2)}) collective-permute-start(f32[8,128]{1,0:T(8,128)S(1)} %add_add_fusion.2), channel_id=1, source_target_pairs={{0,16},{1,17},{2,18},{3,19},{4,20},{5,21},{6,22},{7,23},{8,24},{9,... | collective-permute-start | bytes 12296 | tf_op jit(solution)/shard_map/ppermute | solution.py:39

commit v2 on v1

--- a/solution.py
+++ b/solution.py
@@ -1,6 +1,10 @@
+import functools
+
 import jax
 import jax.numpy as jnp
 from jax import lax
+from jax.experimental import pallas as pl
+from jax.experimental.pallas import tpu as pltpu
 from jax.sharding import PartitionSpec as P
 
 HALO = 16
@@ -13,19 +17,6 @@
 NOISE_AMP = 0.25
 SPACING = 0.02
 TARGET_FLOW = 1.0
-
-
-def padded(value, sides, width):
-    for axis, dim in sides:
-        count, length = (lax.axis_size(axis), value.shape[dim])
-        up = [(i, (i + 1) % count) for i in range(count - 1)]
-        down = [(j, i) for i, j in up]
-        last = lax.slice_in_dim(value, length - width, length, axis=dim)
-        initial = lax.slice_in_dim(value, 0, width, axis=dim)
-        before = lax.ppermute(last, axis, up)
-        after = lax.ppermute(initial, axis, down)
-        value = jnp.concatenate([before, value, after], axis=dim)
-    return value
 
 
 def butterfly_sum(value, axis, radix=4):
@@ -44,51 +35,79 @@
     return value
 
 
-def bead_forces(own_tile, partners, shift_x):
-    offset_x = own_tile[0][None, :, None] - partners[:, 0][:, None, :] + shift_x[:, None, None]
-    offset_y = own_tile[1][None, :, None] - partners[:, 1][:, None, :]
-    offset_z = own_tile[2][None, :, None] - partners[:, 2][:, None, :]
-    closing = offset_x * (own_tile[3][None, :, None] - partners[:, 3][:, None, :])
-    closing = closing + offset_y * (own_tile[4][None, :, None] - partners[:, 4][:, None, :])
-    closing = closing + offset_z * (own_tile[5][None, :, None] - partners[:, 5][:, None, :])
-    weight = jnp.maximum(
-        1.0 - (offset_x * offset_x + offset_y * offset_y + offset_z * offset_z), 0.0
-    )
-    kicks = own_tile[7][None, :, None] + partners[:, 7][:, None, :]
-    factor = own_tile[6][None, :, None] * partners[:, 6][:, None, :] * weight
-    factor = factor * (REPULSION - FRICTION * weight * closing + NOISE_AMP * kicks)
-    return jnp.stack(
-        [
-            jnp.sum(factor * offset_x, axis=(0, 2)),
-            jnp.sum(factor * offset_y, axis=(0, 2)),
-            jnp.sum(factor * offset_z, axis=(0, 2)),
-        ]
-    )
+def force_kernel(links_ref, shifts_ref, src_ref, pos_ref, vel_ref, *, first, count, skip, origin, links):
+    width = src_ref.shape[-1]
+    rows = 8
+
+    def tile(i, carry):
+        t = first + i + jnp.where(i >= count // 2, skip, 0)
+        own = src_ref[t + HALO - origin]
+        own_rows = [jnp.broadcast_to(own[f : f + 1, :], (rows, width)) for f in range(6)]
+        kick_a = jnp.broadcast_to(REPULSION + NOISE_AMP * own[7:8, :], (rows, width))
+        acc = [jnp.zeros((rows, width), jnp.float32) for _ in range(3)]
+        for link in range(links):
+            p = links_ref[t * links + link] - origin
+            shift = shifts_ref[t * links + link]
+            part = src_ref[p]
+            fields = [part[0:1, :] - shift] + [part[f : f + 1, :] for f in range(1, 7)]
+            fields.append(NOISE_AMP * part[7:8, :])
+            spread = [jnp.broadcast_to(v, (rows, width)) for v in fields]
+            for j in range(width // rows):
+                xb, yb, zb, ub, vb, wb, sb, hb = [
+                    pltpu.roll(v, rows * j, 1, stride=1, stride_axis=0) for v in spread
+                ]
+                dx = own_rows[0] - xb
+                dy = own_rows[1] - yb
+                dz = own_rows[2] - zb
+                closing = dx * (own_rows[3] - ub) + dy * (own_rows[4] - vb) + dz * (own_rows[5] - wb)
+                weight = jnp.maximum(1.0 - (dx * dx + dy * dy + dz * dz), 0.0)
+                factor = sb * weight * (kick_a + hb - FRICTION * weight * closing)
+                acc[0] = acc[0] + factor * dx
+                acc[1] = acc[1] + factor * dy
+                acc[2] = acc[2] + factor * dz
+        strength_a = own[6:7, :]
+        force = jnp.concatenate([strength_a * jnp.sum(a, axis=0, keepdims=True) for a in acc], axis=0)
+        speed = own[3:6, :] + TIME_STEP * force
+        vel_ref[t] = speed
+        pos_ref[t] = own[0:3, :] + TIME_STEP * speed
+        return carry
+
+    lax.fori_loop(0, count, tile, 0)
 
 
-def slab_forces(extended, links):
-    tiles = links.shape[0]
-    margin = (extended.shape[0] - tiles) // 2
-    group = 8
-    width = extended.shape[-1]
-    own_index = jnp.arange(tiles, dtype=jnp.int32) + margin
-    own_tiles = extended[margin : margin + tiles]
+def substep_call(links, shifts, src, carry_out, *, first, count, skip, origin, tiles):
+    per_tile = links.shape[0] // tiles
+    width = src.shape[-1]
+    kernel = functools.partial(force_kernel, first=first, count=count, skip=skip, origin=origin, links=per_tile)
+    out_shape = (
+        jax.ShapeDtypeStruct((tiles, 3, width), jnp.float32),
+        jax.ShapeDtypeStruct((tiles, 3, width), jnp.float32),
+    )
+    pairs = count * per_tile * width * width
+    in_specs = [
+        pl.BlockSpec(memory_space=pltpu.SMEM),
+        pl.BlockSpec(memory_space=pltpu.SMEM),
+        pl.BlockSpec(memory_space=pltpu.VMEM),
+    ]
+    args = [links, shifts, src]
+    if carry_out is not None:
+        in_specs += [pl.BlockSpec(memory_space=pltpu.VMEM)] * 2
+        args += list(carry_out)
+        keep = slice(count // 2, tiles - count // 2)
 
-    def per_group(item):
-        own_group, link_group, index_group = item
-        partners = extended[link_group]
-        shifts = SPACING * (index_group[:, None] - link_group).astype(jnp.float32)
-        return jax.vmap(bead_forces)(own_group, partners, shifts)
-
-    result = lax.map(
-        per_group,
-        (
-            own_tiles.reshape(tiles // group, group, 8, width),
-            links.reshape(tiles // group, group, links.shape[1]),
-            own_index.reshape(tiles // group, group),
-        ),
-    )
-    return result.reshape(tiles, 3, width)
+        def body(l, s, x, p_in, v_in, p_out, v_out):
+            p_out[keep] = p_in[keep]
+            v_out[keep] = v_in[keep]
+            kernel(l, s, x, p_out, v_out)
+    else:
+        body = kernel
+    return pl.pallas_call(
+        body,
+        out_shape=out_shape,
+        in_specs=in_specs,
+        out_specs=(pl.BlockSpec(memory_space=pltpu.VMEM), pl.BlockSpec(memory_space=pltpu.VMEM)),
+        cost_estimate=pl.CostEstimate(flops=30 * pairs, transcendentals=0, bytes_accessed=src.size * 4),
+    )(*args)
 
 
 def shards(positions, velocities, strength, noise, neighbours, bins, thermal, slot_counts):
@@ -97,13 +116,27 @@
     weights = strength[0]
     links = neighbours[0]
     substeps = noise.shape[0]
+    tiles = links.shape[0]
+    count = lax.axis_size("space")
+    up = [(i, i + 1) for i in range(count - 1)]
+    down = [(i + 1, i) for i in range(count - 1)]
+    own_index = jnp.arange(tiles, dtype=jnp.int32)[:, None] + HALO
+    shifts = (SPACING * (own_index - links).astype(jnp.float32)).reshape(-1)
+    flat_links = links.reshape(-1)
+    edge = tiles - 2 * HALO
     for substep in range(substeps):
         packed = jnp.concatenate(
             [place, speed, weights[:, None, :], noise[substep, 0][:, None, :]], axis=1
         )
-        extended = padded(packed, (("space", 0),), HALO)
-        speed = speed + TIME_STEP * slab_forces(extended, links)
-        place = place + TIME_STEP * speed
+        before = lax.ppermute(packed[tiles - HALO :], "space", up)
+        after = lax.ppermute(packed[:HALO], "space", down)
+        inner = substep_call(
+            flat_links, shifts, packed, None, first=HALO, count=edge, skip=0, origin=HALO, tiles=tiles
+        )
+        extended = jnp.concatenate([before, packed, after], axis=0)
+        place, speed = substep_call(
+            flat_links, shifts, extended, inner, first=0, count=2 * HALO, skip=edge, origin=0, tiles=tiles
+        )
     tiles = speed.shape[0]
     width = speed.shape[-1]
     group = 8

time: 280 us -> 287 us (1.025)
  Pallas kernels: 0 us -> 141 us
  other arithmetic: 95.2 us -> 14.2 us
  local copies, waits for them, and re-layouts: 37.1 us -> 6.28 us
  waiting for transfers between devices: 48.6 us -> 27 us
  loops' own time: 6.34 us -> 0.32 us
  starting transfers between devices: 77.4 us -> 82.4 us
    pallas_call x0 -> x8, Pallas kernels: none -> 141 us  [substep_call(): pl.pallas_call(body, out_shape=out_shape, in_specs=in_specs, out_specs=(p...]
    reduce_sum x32 -> x0, other arithmetic: 84.4 us -> none  [bead_forces(): jnp.sum(factor * offset_x, axis=(0, 2))]
    ppermute x8, waiting for transfers between devices: 20.7 us -> 0.02 us  [the longest x4 0.01 us: shards(): before = lax.ppermute(packed[tiles - HALO:], 'space', up)]
    gather x32 -> x0, local copies, waits for them, and re-layouts: 18.5 us -> none  [per_group(): partners = extended[link_group]]
    another operation x4 -> x0, loops' own time: 6.03 us -> none  [slab_forces(): lax.map(per_group, (own_tiles.reshape(tiles // group, group, 8, width), l...]
    select_n x64 -> x0, local copies, waits for them, and re-layouts: 5.22 us -> none  [per_group(): partners = extended[link_group]]
    ppermute x8, starting transfers between devices: 22.8 us -> 25.8 us  [the longest x4 20.7 us: shards(): before = lax.ppermute(packed[tiles - HALO:], 'space', up)]
    mul x96 -> x0, local copies, waits for them, and re-layouts: 3.01 us -> none  [the longest x32 2.61 us: per_group(): shifts = SPACING * (index_group[:, None] - link_group).astype(jnp.float32)]
  transfers between devices with their start and end apart: 21 -> 21, of which waited for: 13 -> 5; matrix products, arithmetic and copies ran while one was open for 1% -> 1% of each run, Pallas kernels for 0% -> 25%
where the time goes in v2:
time: 287 us; the launch traced here: 286 us
  Pallas kernels  141 us (49%)
  starting transfers between devices  82.4 us (29%)
  waiting for transfers between devices  27 us (9%)
  other arithmetic  14.2 us (5%)
  matrix products  11.7 us (4%)
  local copies, waits for them, and re-layouts  6.28 us (2%)
    pallas_call x8, Pallas kernels, substep_call(): pl.pallas_call(body, out_shape=out_shape, in_specs=in_specs, out_specs=(p...  141 us
    ppermute x13, starting transfers between devices, butterfly_sum(): leaves.append(lax.ppermute(value, axis, pairs))  56.5 us
    ppermute x13, waiting for transfers between devices, butterfly_sum(): leaves.append(lax.ppermute(value, axis, pairs))  27 us
    ppermute x4, starting transfers between devices, shards(): before = lax.ppermute(packed[tiles - HALO:], 'space', up)  20.7 us
    dot_general x8, matrix products, accumulate(): jnp.dot(rows_now, table, precision=lax.Precision.HIGHEST, preferred_eleme...  11.7 us
  transfers between devices with their start and end apart: 21, of which 5 were waited for; matrix products, arithmetic and copies ran while one was open for 1% of the time, Pallas kernels for 25%

profile of v2, /device:TPU:8, one launch (start us, length us, event | category | flops | bytes accessed | tf_op | source)
XLA Modules:
  0.0 285.7 jit_solution(14628951932432043458)
XLA Ops:
  0.6 0.8 fusion.30
  1.5 1.1 copy_bitcast_fusion
  2.7 4.3 %collective-permute-start = (f32[16,8,128]{2,1,0:T(8,128)S(1)}, f32[16,8,128]{2,1,0:T(8,128)S(1)}, u32[]{:S(2)}, u32[]{:S(2)}) collective-permute-start(f32[16,8,128]{2,1,0:T(8,128)S(1)} %get-tuple-element.119), channel_id=1, source_target_pairs={{0,1},{1,2},{2,3},{3,4},{4,5},{5,6},{6,7},{7,8},{8,9},{9,10},{10,1... | collective-permute-start | bytes 196616 | tf_op jit(solution)/shard_map/ppermute | solution.py:131
  7.0 1.3 collective-permute-start.1
  8.8 0.6 convert_multiply_fusion.shifts_ref.s
  9.4 17.6 %shard_map.111 = (f32[64,3,128]{2,1,0:T(4,128)}, f32[64,3,128]{2,1,0:T(4,128)}) custom-call(s32[192]{0:T(256)} %copy-done.12, f32[192]{0:T(256)} %convert_multiply_fusion.shifts_ref.s, f32[64,8,128]{2,1,0:T(8,128)} %copy-done.1), custom_call_target="tpu_custom_call" | custom-call | flops 47185920 | bytes 262144 | tf_op jit(solution)/shard_map/pallas_call | solution.py:104
  27.0 0.9 fusion.12.x
  27.9 17.7 %shard_map.112 = (f32[64,3,128]{2,1,0:T(4,128)}, f32[64,3,128]{2,1,0:T(4,128)}) custom-call(s32[192]{0:T(256)} %copy-done.12, f32[192]{0:T(256)} %convert_multiply_fusion.shifts_ref.s, f32[96,8,128]{2,1,0:T(8,128)} %fusion.12.x, f32[64,3,128]{2,1,0:T(4,128)} %get-tuple-element.53.p_in, f32[64,3,128]{2,1,0:T(4,128)} %get-tuple-element.54.v_in), custom_call_target="tpu_custom_call" | custom-call | flops 47185920 | bytes 393216 | tf_op jit(solution)/shard_map/pallas_call | solution.py:104
  45.6 1.1 fusion.23.src_ref
  46.7 5.0 %collective-permute-start.2 = (f32[16,8,128]{2,1,0:T(8,128)S(1)}, f32[16,8,128]{2,1,0:T(8,128)S(1)}, u32[]{:S(2)}, u32[]{:S(2)}) collective-permute-start(f32[16,8,128]{2,1,0:T(8,128)S(1)} %get-tuple-element.117), channel_id=1, source_target_pairs={{0,1},{1,2},{2,3},{3,4},{4,5},{5,6},{6,7},{7,8},{8,9},{9,10},{10,1... | collective-permute-start | bytes 196616 | tf_op jit(solution)/shard_map/ppermute | solution.py:131
  51.8 1.3 collective-permute-start.3
  53.1 17.6 %shard_map.113 = (f32[64,3,128]{2,1,0:T(4,128)}, f32[64,3,128]{2,1,0:T(4,128)}) custom-call(s32[192]{0:T(256)} %copy-done.12, f32[192]{0:T(256)} %convert_multiply_fusion.shifts_ref.s, f32[64,8,128]{2,1,0:T(8,128)} %copy-done.3), custom_call_target="tpu_custom_call" | custom-call | flops 47185920 | bytes 262144 | tf_op jit(solution)/shard_map/pallas_call | solution.py:104
  70.7 0.9 fusion.15.x
  71.6 17.7 %shard_map.114 = (f32[64,3,128]{2,1,0:T(4,128)}, f32[64,3,128]{2,1,0:T(4,128)}) custom-call(s32[192]{0:T(256)} %copy-done.12, f32[192]{0:T(256)} %convert_multiply_fusion.shifts_ref.s, f32[96,8,128]{2,1,0:T(8,128)} %fusion.15.x, f32[64,3,128]{2,1,0:T(4,128)} %get-tuple-element.57.p_in, f32[64,3,128]{2,1,0:T(4,128)} %get-tuple-element.58.v_in), custom_call_target="tpu_custom_call" | custom-call | flops 47185920 | bytes 393216 | tf_op jit(solution)/shard_map/pallas_call | solution.py:104
  89.3 1.1 fusion.24.src_ref
  90.5 5.1 %collective-permute-start.4 = (f32[16,8,128]{2,1,0:T(8,128)S(1)}, f32[16,8,128]{2,1,0:T(8,128)S(1)}, u32[]{:S(2)}, u32[]{:S(2)}) collective-permute-start(f32[16,8,128]{2,1,0:T(8,128)S(1)} %get-tuple-element.115), channel_id=1, source_target_pairs={{0,1},{1,2},{2,3},{3,4},{4,5},{5,6},{6,7},{7,8},{8,9},{9,10},{10,1... | collective-permute-start | bytes 196616 | tf_op jit(solution)/shard_map/ppermute | solution.py:131
  95.5 1.3 collective-permute-start.5
  96.9 17.6 %shard_map.115 = (f32[64,3,128]{2,1,0:T(4,128)}, f32[64,3,128]{2,1,0:T(4,128)}) custom-call(s32[192]{0:T(256)} %copy-done.12, f32[192]{0:T(256)} %convert_multiply_fusion.shifts_ref.s, f32[64,8,128]{2,1,0:T(8,128)} %copy-done.4), custom_call_target="tpu_custom_call" | custom-call | flops 47185920 | bytes 262144 | tf_op jit(solution)/shard_map/pallas_call | solution.py:104
  114.5 0.9 fusion.18.x
  115.3 17.7 %shard_map.116 = (f32[64,3,128]{2,1,0:T(4,128)}, f32[64,3,128]{2,1,0:T(4,128)}) custom-call(s32[192]{0:T(256)} %copy-done.12, f32[192]{0:T(256)} %convert_multiply_fusion.shifts_ref.s, f32[96,8,128]{2,1,0:T(8,128)} %fusion.18.x, f32[64,3,128]{2,1,0:T(4,128)} %get-tuple-element.61.p_in, f32[64,3,128]{2,1,0:T(4,128)} %get-tuple-element.62.v_in), custom_call_target="tpu_custom_call" | custom-call | flops 47185920 | bytes 393216 | tf_op jit(solution)/shard_map/pallas_call | solution.py:104
  133.1 1.1 fusion.25.src_ref
  134.2 6.3 %collective-permute-start.6 = (f32[16,8,128]{2,1,0:T(8,128)S(1)}, f32[16,8,128]{2,1,0:T(8,128)S(1)}, u32[]{:S(2)}, u32[]{:S(2)}) collective-permute-start(f32[16,8,128]{2,1,0:T(8,128)S(1)} %get-tuple-element.113), channel_id=1, source_target_pairs={{0,1},{1,2},{2,3},{3,4},{4,5},{5,6},{6,7},{7,8},{8,9},{9,10},{10,1... | collective-permute-start | bytes 196616 | tf_op jit(solution)/shard_map/ppermute | solution.py:131
  140.5 1.3 collective-permute-start.7
  141.9 17.6 %shard_map.117 = (f32[64,3,128]{2,1,0:T(4,128)}, f32[64,3,128]{2,1,0:T(4,128)}) custom-call(s32[192]{0:T(256)} %copy-done.12, f32[192]{0:T(256)} %convert_multiply_fusion.shifts_ref.s, f32[64,8,128]{2,1,0:T(8,128)} %copy-done.2), custom_call_target="tpu_custom_call" | custom-call | flops 47185920 | bytes 262144 | tf_op jit(solution)/shard_map/pallas_call | solution.py:104
  159.5 0.9 fusion.21.x
  160.4 17.7 %shard_map.118 = (f32[64,3,128]{2,1,0:T(4,128)}, f32[64,3,128]{2,1,0:T(4,128)S(1)}) custom-call(s32[192]{0:T(256)} %copy-done.12, f32[192]{0:T(256)} %convert_multiply_fusion.shifts_ref.s, f32[96,8,128]{2,1,0:T(8,128)} %fusion.21.x, f32[64,3,128]{2,1,0:T(4,128)} %get-tuple-element.65.p_in, f32[64,3,128]{2,1,0:T(4,128)} %get-tuple-element.66.v_in), custom_call_target="tpu_custom_call" | custom-call | flops 47185920 | bytes 393216 | tf_op jit(solution)/shard_map/pallas_call | solution.py:104
  178.0 0.7 slice_reduce_fusion
  178.7 16.0 %while.13 = (s32[]{:T(128)}, f32[3,1024]{1,0:T(4,128)S(1)}, f32[1024]{0:T(1024)S(1)}, f32[8,8,3,128]{3,2,1,0:T(4,128)S(1)}, s32[8,1024]{1,0:T(8,128)S(1)}, /*index=5*/s32[]{:T(128)}, s32[]{:T(128)}) while((s32[]{:T(128)}, f32[3,1024]{1,0:T(4,128)S(1)}, f32[1024]{0:T(1024)S(1)}, f32[8,8,3,128]{3,2,1,0:T(4,128)S(1)}, ...), condition=%wide.region_2.3_spmd.clone, body=%wide.region_0.2_spmd.clone.sunk | while | flops 41950208 | bytes 77920 | solution.py:159
  178.7 1.5 fusion.35
  180.7 1.5 fusion.35
  182.2 0.5 fusion.36
  182.7 1.5 fusion.35
  184.7 1.5 fusion.35
  186.7 1.5 fusion.35
  188.8 1.5 fusion.35
  190.8 1.5 fusion.35
  192.8 1.5 fusion.35
  194.8 0.7 broadcast_in_dim.54
  195.6 1.9 collective-permute-start.10
  197.5 3.6 %collective-permute-start.8 = (f32[8,1024]{1,0:T(8,128)S(1)}, f32[8,1024]{1,0:T(8,128)S(1)}, u32[]{:S(2)}, u32[]{:S(2)}) collective-permute-start(f32[8,1024]{1,0:T(8,128)S(1)} %maximum_maximum_fusion), channel_id=1, source_target_pairs={{0,32},{32,0},{64,96},{96,64},{128,160},{160,128},{192,224},{224,1... | collective-permute-start | bytes 98312 | tf_op jit(solution)/shard_map/ppermute | solution.py:30
  201.1 2.4 collective-permute-start.9
  203.5 3.4 %collective-permute-done.9 = f32[8,1024]{1,0:T(8,128)S(1)} collective-permute-done((f32[8,1024]{1,0:T(8,128)S(1)}, f32[8,1024]{1,0:T(8,128)S(1)}, u32[]{:S(2)}, u32[]{:S(2)}) %collective-permute-start.9) | collective-permute-done | bytes 32800 | tf_op jit(solution)/shard_map/ppermute | solution.py:30
  207.0 4.7 %collective-permute-start.11 = (f32[8,1024]{1,0:T(8,128)S(1)}, f32[8,1024]{1,0:T(8,128)S(1)}, u32[]{:S(2)}, u32[]{:S(2)}) collective-permute-start(f32[8,1024]{1,0:T(8,128)S(1)} %add_add_fusion.1), channel_id=1, source_target_pairs={{0,128},{32,160},{64,192},{96,224},{128,0},{160,32},{192,64},{224,... | collective-permute-start | bytes 98312 | tf_op jit(solution)/shard_map/ppermute | solution.py:30
  211.7 2.4 collective-permute-start.12
  214.1 3.7 %collective-permute-start.13 = (f32[8,1024]{1,0:T(8,128)S(1)}, f32[8,1024]{1,0:T(8,128)S(1)}, u32[]{:S(2)}, u32[]{:S(2)}) collective-permute-start(f32[8,1024]{1,0:T(8,128)S(1)} %add_add_fusion.1), channel_id=1, source_target_pairs={{0,384},{32,416},{64,448},{96,480},{128,256},{160,288},{192,320},{... | collective-permute-start | bytes 98312 | tf_op jit(solution)/shard_map/ppermute | solution.py:30
  217.9 4.4 %collective-permute-done.13 = f32[8,1024]{1,0:T(8,128)S(1)} collective-permute-done((f32[8,1024]{1,0:T(8,128)S(1)}, f32[8,1024]{1,0:T(8,128)S(1)}, u32[]{:S(2)}, u32[]{:S(2)}) %collective-permute-start.13) | collective-permute-done | bytes 32800 | tf_op jit(solution)/shard_map/ppermute | solution.py:30
  222.3 0.5 slice.78
  222.8 0.6 broadcast_in_dim.56
  223.5 5.7 %collective-permute-start.14 = (f32[8,128]{1,0:T(8,128)S(1)}, f32[8,128]{1,0:T(8,128)S(1)}, u32[]{:S(2)}, u32[]{:S(2)}) collective-permute-start(f32[8,128]{1,0:T(8,128)S(1)} %broadcast_in_dim.56), channel_id=1, source_target_pairs={{0,1},{1,0},{2,3},{3,2},{4,5},{5,4},{6,7},{7,6},{8,9},{9,8},{10,11... | collective-permute-start | bytes 12296 | tf_op jit(solution)/shard_map/ppermute | solution.py:30
  229.2 7.7 %collective-permute-start.15 = (f32[8,128]{1,0:T(8,128)S(1)}, f32[8,128]{1,0:T(8,128)S(1)}, u32[]{:S(2)}, u32[]{:S(2)}) collective-permute-start(f32[8,128]{1,0:T(8,128)S(1)} %broadcast_in_dim.56), channel_id=1, source_target_pairs={{0,2},{1,3},{2,0},{3,1},{4,6},{5,7},{6,4},{7,5},{8,10},{9,11},{10,... | collective-permute-start | bytes 12296 | tf_op jit(solution)/shard_map/ppermute | solution.py:30
  237.0 1.9 collective-permute-start.16
  239.6 4.7 %collective-permute-done.16 = f32[8,128]{1,0:T(8,128)S(1)} collective-permute-done((f32[8,128]{1,0:T(8,128)S(1)}, f32[8,128]{1,0:T(8,128)S(1)}, u32[]{:S(2)}, u32[]{:S(2)}) %collective-permute-start.16) | collective-permute-done | bytes 4128 | tf_op jit(solution)/shard_map/ppermute | solution.py:30
  244.3 0.6 add_add_fusion.3
  244.9 10.1 %collective-permute-start.17 = (f32[8,128]{1,0:T(8,128)S(1)}, f32[8,128]{1,0:T(8,128)S(1)}, u32[]{:S(2)}, u32[]{:S(2)}) collective-permute-start(f32[8,128]{1,0:T(8,128)S(1)} %add_add_fusion.3), channel_id=1, source_target_pairs={{0,4},{1,5},{2,6},{3,7},{4,0},{5,1},{6,2},{7,3},{8,12},{9,13},{10,... | collective-permute-start | bytes 12296 | tf_op jit(solution)/shard_map/ppermute | solution.py:30
  255.1 8.1 %collective-permute-start.18 = (f32[8,128]{1,0:T(8,128)S(1)}, f32[8,128]{1,0:T(8,128)S(1)}, u32[]{:S(2)}, u32[]{:S(2)}) collective-permute-start(f32[8,128]{1,0:T(8,128)S(1)} %add_add_fusion.3), channel_id=1, source_target_pairs={{0,8},{1,9},{2,10},{3,11},{4,12},{5,13},{6,14},{7,15},{8,0},{9,1},... | collective-permute-start | bytes 12296 | tf_op jit(solution)/shard_map/ppermute | solution.py:30
  263.2 1.9 collective-permute-start.19
  265.2 0.6 copy.24
  265.8 0.6 copy.25
  266.5 7.9 %collective-permute-done.19 = f32[8,128]{1,0:T(8,128)S(1)} collective-permute-done((f32[8,128]{1,0:T(8,128)S(1)}, f32[8,128]{1,0:T(8,128)S(1)}, u32[]{:S(2)}, u32[]{:S(2)}) %collective-permute-start.19) | collective-permute-done | bytes 4128 | tf_op jit(solution)/shard_map/ppermute | solution.py:30
  274.4 2.2 collective-permute-start.20
  276.7 0.6 slice_divide_fusion
  277.3 6.5 %collective-permute-done.20 = f32[8,128]{1,0:T(8,128)S(1)} collective-permute-done((f32[8,128]{1,0:T(8,128)S(1)}, f32[8,128]{1,0:T(8,128)S(1)}, u32[]{:S(2)}, u32[]{:S(2)}) %collective-permute-start.20) | collective-permute-done | bytes 4128 | tf_op jit(solution)/shard_map/ppermute | solution.py:30
  283.8 0.5 slice.67
  285.0 0.6 broadcast_select_fusion
  (93 shorter events, 4.5 us)
Async XLA Ops:
  0.6 1.9 copy-start
  2.6 5.8 %copy-start.14 = (s32[1,64,3]{1,0,2:T(1,128)S(1)}, s32[1,64,3]{1,0,2:T(1,128)}, u32[]{:S(2)}) copy-start(s32[1,64,3]{1,0,2:T(1,128)} %param.14) | copy-start | bytes 2308
  2.7 6.7 %copy-start.1 = (f32[64,8,128]{2,1,0:T(8,128)}, f32[64,8,128]{2,1,0:T(8,128)S(1)}, u32[]{:S(2)}) copy-start(f32[64,8,128]{2,1,0:T(8,128)S(1)} %fusion.22.src_ref) | copy-start | bytes 786436
  2.7 24.2 %collective-permute-start = (f32[16,8,128]{2,1,0:T(8,128)S(1)}, f32[16,8,128]{2,1,0:T(8,128)S(1)}, u32[]{:S(2)}, u32[]{:S(2)}) collective-permute-start(f32[16,8,128]{2,1,0:T(8,128)S(1)} %get-tuple-element.119), channel_id=1, source_target_pairs={{0,1},{1,2},{2,3},{3,4},{4,5},{5,6},{6,7},{7,8},{8,9},{9,10},{10,1... | collective-permute-start | bytes 196616 | tf_op jit(solution)/shard_map/ppermute | solution.py:131
  7.0 19.9 %collective-permute-start.1 = (f32[16,8,128]{2,1,0:T(8,128)S(1)}, f32[16,8,128]{2,1,0:T(8,128)S(1)}, u32[]{:S(2)}, u32[]{:S(2)}) collective-permute-start(f32[16,8,128]{2,1,0:T(8,128)S(1)} %get-tuple-element.120), channel_id=1, source_target_pairs={{1,0},{2,1},{3,2},{4,3},{5,4},{6,5},{7,6},{8,7},{9,8},{10,9},{11,1... | collective-permute-start | bytes 196616 | tf_op jit(solution)/shard_map/ppermute | solution.py:132
  8.6 0.8 copy-start.12
  46.7 6.4 %copy-start.3 = (f32[64,8,128]{2,1,0:T(8,128)}, f32[64,8,128]{2,1,0:T(8,128)S(1)}, u32[]{:S(2)}) copy-start(f32[64,8,128]{2,1,0:T(8,128)S(1)} %fusion.23.src_ref) | copy-start | bytes 786436
  46.7 24.0 %copy-start.7 = (f32[64,3,128]{2,1,0:T(4,128)S(1)}, f32[64,3,128]{2,1,0:T(4,128)}, u32[]{:S(2)}) copy-start(f32[64,3,128]{2,1,0:T(4,128)} %get-tuple-element.55) | copy-start | bytes 294916
  46.7 24.0 %copy-start.8 = (f32[64,3,128]{2,1,0:T(4,128)S(1)}, f32[64,3,128]{2,1,0:T(4,128)}, u32[]{:S(2)}) copy-start(f32[64,3,128]{2,1,0:T(4,128)} %get-tuple-element.56) | copy-start | bytes 294916
  46.7 24.0 %collective-permute-start.2 = (f32[16,8,128]{2,1,0:T(8,128)S(1)}, f32[16,8,128]{2,1,0:T(8,128)S(1)}, u32[]{:S(2)}, u32[]{:S(2)}) collective-permute-start(f32[16,8,128]{2,1,0:T(8,128)S(1)} %get-tuple-element.117), channel_id=1, source_target_pairs={{0,1},{1,2},{2,3},{3,4},{4,5},{5,6},{6,7},{7,8},{8,9},{9,10},{10,1... | collective-permute-start | bytes 196616 | tf_op jit(solution)/shard_map/ppermute | solution.py:131
  51.8 18.9 %collective-permute-start.3 = (f32[16,8,128]{2,1,0:T(8,128)S(1)}, f32[16,8,128]{2,1,0:T(8,128)S(1)}, u32[]{:S(2)}, u32[]{:S(2)}) collective-permute-start(f32[16,8,128]{2,1,0:T(8,128)S(1)} %get-tuple-element.118), channel_id=1, source_target_pairs={{1,0},{2,1},{3,2},{4,3},{5,4},{6,5},{7,6},{8,7},{9,8},{10,9},{11,1... | collective-permute-start | bytes 196616 | tf_op jit(solution)/shard_map/ppermute | solution.py:132
  90.4 6.4 %copy-start.4 = (f32[64,8,128]{2,1,0:T(8,128)}, f32[64,8,128]{2,1,0:T(8,128)S(1)}, u32[]{:S(2)}) copy-start(f32[64,8,128]{2,1,0:T(8,128)S(1)} %fusion.24.src_ref) | copy-start | bytes 786436
  90.4 24.0 %copy-start.9 = (f32[64,3,128]{2,1,0:T(4,128)S(1)}, f32[64,3,128]{2,1,0:T(4,128)}, u32[]{:S(2)}) copy-start(f32[64,3,128]{2,1,0:T(4,128)} %get-tuple-element.59) | copy-start | bytes 294916
  90.4 24.0 %copy-start.10 = (f32[64,3,128]{2,1,0:T(4,128)S(1)}, f32[64,3,128]{2,1,0:T(4,128)}, u32[]{:S(2)}) copy-start(f32[64,3,128]{2,1,0:T(4,128)} %get-tuple-element.60) | copy-start | bytes 294916
  90.5 24.0 %collective-permute-start.4 = (f32[16,8,128]{2,1,0:T(8,128)S(1)}, f32[16,8,128]{2,1,0:T(8,128)S(1)}, u32[]{:S(2)}, u32[]{:S(2)}) collective-permute-start(f32[16,8,128]{2,1,0:T(8,128)S(1)} %get-tuple-element.115), channel_id=1, source_target_pairs={{0,1},{1,2},{2,3},{3,4},{4,5},{5,6},{6,7},{7,8},{8,9},{9,10},{10,1... | collective-permute-start | bytes 196616 | tf_op jit(solution)/shard_map/ppermute | solution.py:131
  95.5 18.9 %collective-permute-start.5 = (f32[16,8,128]{2,1,0:T(8,128)S(1)}, f32[16,8,128]{2,1,0:T(8,128)S(1)}, u32[]{:S(2)}, u32[]{:S(2)}) collective-permute-start(f32[16,8,128]{2,1,0:T(8,128)S(1)} %get-tuple-element.116), channel_id=1, source_target_pairs={{1,0},{2,1},{3,2},{4,3},{5,4},{6,5},{7,6},{8,7},{9,8},{10,9},{11,1... | collective-permute-start | bytes 196616 | tf_op jit(solution)/shard_map/ppermute | solution.py:132
  133.1 8.7 %copy-start.13 = (s32[1,64,128]{2,1,0:T(8,128)S(1)}, s32[1,64,128]{2,1,0:T(8,128)}, u32[]{:S(2)}) copy-start(s32[1,64,128]{2,1,0:T(8,128)} %param.15) | copy-start | bytes 98308
  134.2 7.7 %copy-start.2 = (f32[64,8,128]{2,1,0:T(8,128)}, f32[64,8,128]{2,1,0:T(8,128)S(1)}, u32[]{:S(2)}) copy-start(f32[64,8,128]{2,1,0:T(8,128)S(1)} %fusion.25.src_ref) | copy-start | bytes 786436
  134.2 25.3 %copy-start.5 = (f32[64,3,128]{2,1,0:T(4,128)S(1)}, f32[64,3,128]{2,1,0:T(4,128)}, u32[]{:S(2)}) copy-start(f32[64,3,128]{2,1,0:T(4,128)} %get-tuple-element.63) | copy-start | bytes 294916
  134.2 25.3 %copy-start.6 = (f32[64,3,128]{2,1,0:T(4,128)S(1)}, f32[64,3,128]{2,1,0:T(4,128)}, u32[]{:S(2)}) copy-start(f32[64,3,128]{2,1,0:T(4,128)} %get-tuple-element.64) | copy-start | bytes 294916
  134.2 25.2 %collective-permute-start.6 = (f32[16,8,128]{2,1,0:T(8,128)S(1)}, f32[16,8,128]{2,1,0:T(8,128)S(1)}, u32[]{:S(2)}, u32[]{:S(2)}) collective-permute-start(f32[16,8,128]{2,1,0:T(8,128)S(1)} %get-tuple-element.113), channel_id=1, source_target_pairs={{0,1},{1,2},{2,3},{3,4},{4,5},{5,6},{6,7},{7,8},{8,9},{9,10},{10,1... | collective-permute-start | bytes 196616 | tf_op jit(solution)/shard_map/ppermute | solution.py:131
  140.5 18.9 %collective-permute-start.7 = (f32[16,8,128]{2,1,0:T(8,128)S(1)}, f32[16,8,128]{2,1,0:T(8,128)S(1)}, u32[]{:S(2)}, u32[]{:S(2)}) collective-permute-start(f32[16,8,128]{2,1,0:T(8,128)S(1)} %get-tuple-element.114), channel_id=1, source_target_pairs={{1,0},{2,1},{3,2},{4,3},{5,4},{6,5},{7,6},{8,7},{9,8},{10,9},{11,1... | collective-permute-start | bytes 196616 | tf_op jit(solution)/shard_map/ppermute | solution.py:132
  194.8 70.4 %copy-start.11 = (f32[64,3,128]{2,1,0:T(4,128)S(1)}, f32[64,3,128]{2,1,0:T(4,128)}, u32[]{:S(2)}) copy-start(f32[64,3,128]{2,1,0:T(4,128)} %get-tuple-element.67) | copy-start | bytes 294916
  195.6 7.9 %collective-permute-start.10 = (f32[8,1024]{1,0:T(8,128)S(1)}, f32[8,1024]{1,0:T(8,128)S(1)}, u32[]{:S(2)}, u32[]{:S(2)}) collective-permute-start(f32[8,1024]{1,0:T(8,128)S(1)} %maximum_maximum_fusion), channel_id=1, source_target_pairs={{0,96},{32,64},{64,32},{96,0},{128,224},{160,192},{192,160},{224,1... | collective-permute-start | bytes 98312 | tf_op jit(solution)/shard_map/ppermute | solution.py:30
  197.5 6.0 %collective-permute-start.8 = (f32[8,1024]{1,0:T(8,128)S(1)}, f32[8,1024]{1,0:T(8,128)S(1)}, u32[]{:S(2)}, u32[]{:S(2)}) collective-permute-start(f32[8,1024]{1,0:T(8,128)S(1)} %maximum_maximum_fusion), channel_id=1, source_target_pairs={{0,32},{32,0},{64,96},{96,64},{128,160},{160,128},{192,224},{224,1... | collective-permute-start | bytes 98312 | tf_op jit(solution)/shard_map/ppermute | solution.py:30
  201.1 5.8 %collective-permute-start.9 = (f32[8,1024]{1,0:T(8,128)S(1)}, f32[8,1024]{1,0:T(8,128)S(1)}, u32[]{:S(2)}, u32[]{:S(2)}) collective-permute-start(f32[8,1024]{1,0:T(8,128)S(1)} %maximum_maximum_fusion), channel_id=1, source_target_pairs={{0,64},{32,96},{64,0},{96,32},{128,192},{160,224},{192,128},{224,1... | collective-permute-start | bytes 98312 | tf_op jit(solution)/shard_map/ppermute | solution.py:30
  207.0 78.0 %copy-start.15 = (f32[1,3,128]{2,0,1:T(1,128)S(1)}, f32[1,3,128]{2,0,1:T(1,128)}, u32[]{:S(2)}) copy-start(f32[1,3,128]{2,0,1:T(1,128)} %param.16) | copy-start | bytes 4612
  207.0 10.9 %collective-permute-start.11 = (f32[8,1024]{1,0:T(8,128)S(1)}, f32[8,1024]{1,0:T(8,128)S(1)}, u32[]{:S(2)}, u32[]{:S(2)}) collective-permute-start(f32[8,1024]{1,0:T(8,128)S(1)} %add_add_fusion.1), channel_id=1, source_target_pairs={{0,128},{32,160},{64,192},{96,224},{128,0},{160,32},{192,64},{224,... | collective-permute-start | bytes 98312 | tf_op jit(solution)/shard_map/ppermute | solution.py:30
  211.7 6.1 %collective-permute-start.12 = (f32[8,1024]{1,0:T(8,128)S(1)}, f32[8,1024]{1,0:T(8,128)S(1)}, u32[]{:S(2)}, u32[]{:S(2)}) collective-permute-start(f32[8,1024]{1,0:T(8,128)S(1)} %add_add_fusion.1), channel_id=1, source_target_pairs={{0,256},{32,288},{64,320},{96,352},{128,384},{160,416},{192,448},{... | collective-permute-start | bytes 98312 | tf_op jit(solution)/shard_map/ppermute | solution.py:30
  214.1 8.2 %collective-permute-start.13 = (f32[8,1024]{1,0:T(8,128)S(1)}, f32[8,1024]{1,0:T(8,128)S(1)}, u32[]{:S(2)}, u32[]{:S(2)}) collective-permute-start(f32[8,1024]{1,0:T(8,128)S(1)} %add_add_fusion.1), channel_id=1, source_target_pairs={{0,384},{32,416},{64,448},{96,480},{128,256},{160,288},{192,320},{... | collective-permute-start | bytes 98312 | tf_op jit(solution)/shard_map/ppermute | solution.py:30
  223.5 16.1 %collective-permute-start.14 = (f32[8,128]{1,0:T(8,128)S(1)}, f32[8,128]{1,0:T(8,128)S(1)}, u32[]{:S(2)}, u32[]{:S(2)}) collective-permute-start(f32[8,128]{1,0:T(8,128)S(1)} %broadcast_in_dim.56), channel_id=1, source_target_pairs={{0,1},{1,0},{2,3},{3,2},{4,5},{5,4},{6,7},{7,6},{8,9},{9,8},{10,11... | collective-permute-start | bytes 12296 | tf_op jit(solution)/shard_map/ppermute | solution.py:30
  229.2 10.3 %collective-permute-start.15 = (f32[8,128]{1,0:T(8,128)S(1)}, f32[8,128]{1,0:T(8,128)S(1)}, u32[]{:S(2)}, u32[]{:S(2)}) collective-permute-start(f32[8,128]{1,0:T(8,128)S(1)} %broadcast_in_dim.56), channel_id=1, source_target_pairs={{0,2},{1,3},{2,0},{3,1},{4,6},{5,7},{6,4},{7,5},{8,10},{9,11},{10,... | collective-permute-start | bytes 12296 | tf_op jit(solution)/shard_map/ppermute | solution.py:30
  237.0 7.3 %collective-permute-start.16 = (f32[8,128]{1,0:T(8,128)S(1)}, f32[8,128]{1,0:T(8,128)S(1)}, u32[]{:S(2)}, u32[]{:S(2)}) collective-permute-start(f32[8,128]{1,0:T(8,128)S(1)} %broadcast_in_dim.56), channel_id=1, source_target_pairs={{0,3},{1,2},{2,1},{3,0},{4,7},{5,6},{6,5},{7,4},{8,11},{9,10},{10,... | collective-permute-start | bytes 12296 | tf_op jit(solution)/shard_map/ppermute | solution.py:30
  244.9 21.5 %collective-permute-start.17 = (f32[8,128]{1,0:T(8,128)S(1)}, f32[8,128]{1,0:T(8,128)S(1)}, u32[]{:S(2)}, u32[]{:S(2)}) collective-permute-start(f32[8,128]{1,0:T(8,128)S(1)} %add_add_fusion.3), channel_id=1, source_target_pairs={{0,4},{1,5},{2,6},{3,7},{4,0},{5,1},{6,2},{7,3},{8,12},{9,13},{10,... | collective-permute-start | bytes 12296 | tf_op jit(solution)/shard_map/ppermute | solution.py:30
  255.1 11.4 %collective-permute-start.18 = (f32[8,128]{1,0:T(8,128)S(1)}, f32[8,128]{1,0:T(8,128)S(1)}, u32[]{:S(2)}, u32[]{:S(2)}) collective-permute-start(f32[8,128]{1,0:T(8,128)S(1)} %add_add_fusion.3), channel_id=1, source_target_pairs={{0,8},{1,9},{2,10},{3,11},{4,12},{5,13},{6,14},{7,15},{8,0},{9,1},... | collective-permute-start | bytes 12296 | tf_op jit(solution)/shard_map/ppermute | solution.py:30
  263.2 11.2 %collective-permute-start.19 = (f32[8,128]{1,0:T(8,128)S(1)}, f32[8,128]{1,0:T(8,128)S(1)}, u32[]{:S(2)}, u32[]{:S(2)}) collective-permute-start(f32[8,128]{1,0:T(8,128)S(1)} %add_add_fusion.3), channel_id=1, source_target_pairs={{0,12},{1,13},{2,14},{3,15},{4,8},{5,9},{6,10},{7,11},{8,4},{9,5},... | collective-permute-start | bytes 12296 | tf_op jit(solution)/shard_map/ppermute | solution.py:30
  274.4 9.4 %collective-permute-start.20 = (f32[8,128]{1,0:T(8,128)S(1)}, f32[8,128]{1,0:T(8,128)S(1)}, u32[]{:S(2)}, u32[]{:S(2)}) collective-permute-start(f32[8,128]{1,0:T(8,128)S(1)} %add_add_fusion.2), channel_id=1, source_target_pairs={{0,16},{1,17},{2,18},{3,19},{4,20},{5,21},{6,22},{7,23},{8,24},{9,... | collective-permute-start | bytes 12296 | tf_op jit(solution)/shard_map/ppermute | solution.py:30

commit v3 on v1

--- a/solution.py
+++ b/solution.py
@@ -28,7 +28,7 @@
     return value
 
 
-def butterfly_sum(value, axis, radix=4):
+def butterfly_sum(value, axis, radix=2):
     count = lax.axis_size(axis)
     stride = 1
     while stride < count:

time: 280 us -> 264 us (0.943)
  the two profiles are of different devices: /device:TPU:8 before, /device:TPU:36 now
where the time goes in v3:
time: 264 us
  other arithmetic  95.9 us (36%)
  starting transfers between devices  63.8 us (24%)
  waiting for transfers between devices  46.3 us (18%)
  local copies, waits for them, and re-layouts  37.1 us (14%)
  matrix products  11.7 us (4%)
  loops' own time  6.34 us (2%)
    reduce_sum x32, other arithmetic, bead_forces(): jnp.sum(factor * offset_x, axis=(0, 2))  84.4 us
    ppermute x9, waiting for transfers between devices, butterfly_sum(): leaves.append(lax.ppermute(value, axis, pairs))  38.1 us
    ppermute x4, starting transfers between devices, padded(): after = lax.ppermute(initial, axis, down)  34.7 us
    ppermute x9, starting transfers between devices, butterfly_sum(): leaves.append(lax.ppermute(value, axis, pairs))  19 us
    gather x32, local copies, waits for them, and re-layouts, per_group(): partners = extended[link_group]  18.5 us
    dot_general x8, matrix products, accumulate(): jnp.dot(rows_now, table, precision=lax.Precision.HIGHEST, preferred_eleme...  11.7 us
    ppermute x4, starting transfers between devices, padded(): before = lax.ppermute(last, axis, up)  10 us
    ppermute x4, waiting for transfers between devices, padded(): after = lax.ppermute(initial, axis, down)  6.39 us
  transfers between devices with their start and end apart: 17, of which 17 were waited for; matrix products, arithmetic and copies ran while one was open for 1% of the time, Pallas kernels for 0%

profile of v3, /device:TPU:36, one launch (start us, length us, event | category | flops | bytes accessed | tf_op | source)
XLA Modules:
  0.0 263.5 jit_solution(14045872509171920186)
XLA Ops:
  2.8 4.3 %collective-permute-start = (f32[16,8,128]{2,1,0:T(8,128)S(1)}, f32[16,8,128]{2,1,0:T(8,128)S(1)}, u32[]{:S(2)}, u32[]{:S(2)}) collective-permute-start(f32[16,8,128]{2,1,0:T(8,128)S(1)} %get-tuple-element.457), channel_id=1, source_target_pairs={{0,1},{1,2},{2,3},{3,4},{4,5},{5,6},{6,7},{7,8},{8,9},{9,10},{10,1... | collective-permute-start | bytes 196616 | tf_op jit(solution)/shard_map/ppermute | solution.py:25
  7.1 8.4 %collective-permute-start.1 = (f32[16,8,128]{2,1,0:T(8,128)S(1)}, f32[16,8,128]{2,1,0:T(8,128)S(1)}, u32[]{:S(2)}, u32[]{:S(2)}) collective-permute-start(f32[16,8,128]{2,1,0:T(8,128)S(1)} %get-tuple-element.458), channel_id=1, source_target_pairs={{1,0},{2,1},{3,2},{4,3},{5,4},{6,5},{7,6},{8,7},{9,8},{10,9},{11,1... | collective-permute-start | bytes 196616 | tf_op jit(solution)/shard_map/ppermute | solution.py:26
  18.0 30.8 %while.53 = (s32[]{:T(128)}, f32[8,8,3,128]{3,1,2,0:T(8,128)S(1)}, f32[8,8,8,128]{3,2,1,0:T(8,128)S(1)}, s32[8,8,3]{1,2,0:T(4,128)S(1)}, f32[96,8,128]{2,1,0:T(8,128)S(1)}, /*index=5*/s32[8,8]{1,0:T(8,128)S(1)}, s32[]{:T(128)}) while((s32[]{:T(128)}, f32[8,8,3,128]{3,1,2,0:T(8,128)S(1)}, f32[8,8,8,128]{3,2,1,0:T(8,128)S(1)}, ...), condition=%wide.region_4.5_spmd, body=%wide.region_0.4_spmd.sunk | while | flops 12980370 | bytes 1156605 | solution.py:83
  19.2 2.6 %multiply_reduce_fusion.8 = (f32[8,128]{1,0:T(8,128)S(1)}, f32[8,128]{1,0:T(8,128)S(1)}, f32[8,128]{1,0:T(8,128)S(1)}) fusion(f32[8,3]{1,0:T(8,128)S(1)} %copy.420, f32[8,3,128]{2,1,0:T(4,128)S(1)} %copy.422, f32[8,128]{1,0:T(8,128)S(1)} %get-tuple-element.751, f32[8,3,128]{2,1,0:T(4,128)S(1)} %copy.424, f32[8,128]{1,0:T(8,128)S(1)} %get-tuple-element.755, ...), kind=kLoop, calls=%fused_computation.23.clone.1 | loop fusion | flops 12973056 | bytes 143456 | tf_op jit(solution)/shard_map/while/body/eval_jaxpr/vmap()/reduce_sum | solution.py:62
  23.1 2.6 %multiply_reduce_fusion.8 = (f32[8,128]{1,0:T(8,128)S(1)}, f32[8,128]{1,0:T(8,128)S(1)}, f32[8,128]{1,0:T(8,128)S(1)}) fusion(f32[8,3]{1,0:T(8,128)S(1)} %copy.420, f32[8,3,128]{2,1,0:T(4,128)S(1)} %copy.422, f32[8,128]{1,0:T(8,128)S(1)} %get-tuple-element.751, f32[8,3,128]{2,1,0:T(4,128)S(1)} %copy.424, f32[8,128]{1,0:T(8,128)S(1)} %get-tuple-element.755, ...), kind=kLoop, calls=%fused_computation.23.clone.1 | loop fusion | flops 12973056 | bytes 143456 | tf_op jit(solution)/shard_map/while/body/eval_jaxpr/vmap()/reduce_sum | solution.py:62
  26.9 2.6 %multiply_reduce_fusion.8 = (f32[8,128]{1,0:T(8,128)S(1)}, f32[8,128]{1,0:T(8,128)S(1)}, f32[8,128]{1,0:T(8,128)S(1)}) fusion(f32[8,3]{1,0:T(8,128)S(1)} %copy.420, f32[8,3,128]{2,1,0:T(4,128)S(1)} %copy.422, f32[8,128]{1,0:T(8,128)S(1)} %get-tuple-element.751, f32[8,3,128]{2,1,0:T(4,128)S(1)} %copy.424, f32[8,128]{1,0:T(8,128)S(1)} %get-tuple-element.755, ...), kind=kLoop, calls=%fused_computation.23.clone.1 | loop fusion | flops 12973056 | bytes 143456 | tf_op jit(solution)/shard_map/while/body/eval_jaxpr/vmap()/reduce_sum | solution.py:62
  30.8 2.6 %multiply_reduce_fusion.8 = (f32[8,128]{1,0:T(8,128)S(1)}, f32[8,128]{1,0:T(8,128)S(1)}, f32[8,128]{1,0:T(8,128)S(1)}) fusion(f32[8,3]{1,0:T(8,128)S(1)} %copy.420, f32[8,3,128]{2,1,0:T(4,128)S(1)} %copy.422, f32[8,128]{1,0:T(8,128)S(1)} %get-tuple-element.751, f32[8,3,128]{2,1,0:T(4,128)S(1)} %copy.424, f32[8,128]{1,0:T(8,128)S(1)} %get-tuple-element.755, ...), kind=kLoop, calls=%fused_computation.23.clone.1 | loop fusion | flops 12973056 | bytes 143456 | tf_op jit(solution)/shard_map/while/body/eval_jaxpr/vmap()/reduce_sum | solution.py:62
  34.6 2.6 %multiply_reduce_fusion.8 = (f32[8,128]{1,0:T(8,128)S(1)}, f32[8,128]{1,0:T(8,128)S(1)}, f32[8,128]{1,0:T(8,128)S(1)}) fusion(f32[8,3]{1,0:T(8,128)S(1)} %copy.420, f32[8,3,128]{2,1,0:T(4,128)S(1)} %copy.422, f32[8,128]{1,0:T(8,128)S(1)} %get-tuple-element.751, f32[8,3,128]{2,1,0:T(4,128)S(1)} %copy.424, f32[8,128]{1,0:T(8,128)S(1)} %get-tuple-element.755, ...), kind=kLoop, calls=%fused_computation.23.clone.1 | loop fusion | flops 12973056 | bytes 143456 | tf_op jit(solution)/shard_map/while/body/eval_jaxpr/vmap()/reduce_sum | solution.py:62
  38.5 2.6 %multiply_reduce_fusion.8 = (f32[8,128]{1,0:T(8,128)S(1)}, f32[8,128]{1,0:T(8,128)S(1)}, f32[8,128]{1,0:T(8,128)S(1)}) fusion(f32[8,3]{1,0:T(8,128)S(1)} %copy.420, f32[8,3,128]{2,1,0:T(4,128)S(1)} %copy.422, f32[8,128]{1,0:T(8,128)S(1)} %get-tuple-element.751, f32[8,3,128]{2,1,0:T(4,128)S(1)} %copy.424, f32[8,128]{1,0:T(8,128)S(1)} %get-tuple-element.755, ...), kind=kLoop, calls=%fused_computation.23.clone.1 | loop fusion | flops 12973056 | bytes 143456 | tf_op jit(solution)/shard_map/while/body/eval_jaxpr/vmap()/reduce_sum | solution.py:62
  42.3 2.6 %multiply_reduce_fusion.8 = (f32[8,128]{1,0:T(8,128)S(1)}, f32[8,128]{1,0:T(8,128)S(1)}, f32[8,128]{1,0:T(8,128)S(1)}) fusion(f32[8,3]{1,0:T(8,128)S(1)} %copy.420, f32[8,3,128]{2,1,0:T(4,128)S(1)} %copy.422, f32[8,128]{1,0:T(8,128)S(1)} %get-tuple-element.751, f32[8,3,128]{2,1,0:T(4,128)S(1)} %copy.424, f32[8,128]{1,0:T(8,128)S(1)} %get-tuple-element.755, ...), kind=kLoop, calls=%fused_computation.23.clone.1 | loop fusion | flops 12973056 | bytes 143456 | tf_op jit(solution)/shard_map/while/body/eval_jaxpr/vmap()/reduce_sum | solution.py:62
  46.2 2.6 %multiply_reduce_fusion.8 = (f32[8,128]{1,0:T(8,128)S(1)}, f32[8,128]{1,0:T(8,128)S(1)}, f32[8,128]{1,0:T(8,128)S(1)}) fusion(f32[8,3]{1,0:T(8,128)S(1)} %copy.420, f32[8,3,128]{2,1,0:T(4,128)S(1)} %copy.422, f32[8,128]{1,0:T(8,128)S(1)} %get-tuple-element.751, f32[8,3,128]{2,1,0:T(4,128)S(1)} %copy.424, f32[8,128]{1,0:T(8,128)S(1)} %get-tuple-element.755, ...), kind=kLoop, calls=%fused_computation.23.clone.1 | loop fusion | flops 12973056 | bytes 143456 | tf_op jit(solution)/shard_map/while/body/eval_jaxpr/vmap()/reduce_sum | solution.py:62
  50.1 1.9 collective-permute-start.2
  52.1 9.2 %collective-permute-start.3 = (f32[16,8,128]{2,1,0:T(8,128)S(1)}, f32[16,8,128]{2,1,0:T(8,128)S(1)}, u32[]{:S(2)}, u32[]{:S(2)}) collective-permute-start(f32[16,8,128]{2,1,0:T(8,128)S(1)} %get-tuple-element.456), channel_id=1, source_target_pairs={{1,0},{2,1},{3,2},{4,3},{5,4},{6,5},{7,6},{8,7},{9,8},{10,9},{11,1... | collective-permute-start | bytes 196616 | tf_op jit(solution)/shard_map/ppermute | solution.py:26
  61.5 2.0 collective-permute-done.3
  63.7 30.8 %while.54 = (s32[]{:T(128)}, f32[8,8,3,128]{3,1,2,0:T(8,128)S(1)}, f32[8,8,8,128]{3,2,1,0:T(8,128)S(1)}, s32[8,8,3]{1,2,0:T(4,128)S(1)}, f32[96,8,128]{2,1,0:T(8,128)S(1)}, /*index=5*/s32[8,8]{1,0:T(8,128)S(1)}, s32[]{:T(128)}) while((s32[]{:T(128)}, f32[8,8,3,128]{3,1,2,0:T(8,128)S(1)}, f32[8,8,8,128]{3,2,1,0:T(8,128)S(1)}, ...), condition=%wide.region_9.10_spmd, body=%wide.region_5.9_spmd.sunk | while | flops 12980370 | bytes 1156605 | solution.py:83
  64.9 2.6 %multiply_reduce_fusion.9 = (f32[8,128]{1,0:T(8,128)S(1)}, f32[8,128]{1,0:T(8,128)S(1)}, f32[8,128]{1,0:T(8,128)S(1)}) fusion(f32[8,3]{1,0:T(8,128)S(1)} %copy.435, f32[8,3,128]{2,1,0:T(4,128)S(1)} %copy.437, f32[8,128]{1,0:T(8,128)S(1)} %get-tuple-element.786, f32[8,3,128]{2,1,0:T(4,128)S(1)} %copy.439, f32[8,128]{1,0:T(8,128)S(1)} %get-tuple-element.790, ...), kind=kLoop, calls=%fused_computation.71.clone.1 | loop fusion | flops 12973056 | bytes 143456 | tf_op jit(solution)/shard_map/while/body/eval_jaxpr/vmap()/reduce_sum | solution.py:62
  68.8 2.6 %multiply_reduce_fusion.9 = (f32[8,128]{1,0:T(8,128)S(1)}, f32[8,128]{1,0:T(8,128)S(1)}, f32[8,128]{1,0:T(8,128)S(1)}) fusion(f32[8,3]{1,0:T(8,128)S(1)} %copy.435, f32[8,3,128]{2,1,0:T(4,128)S(1)} %copy.437, f32[8,128]{1,0:T(8,128)S(1)} %get-tuple-element.786, f32[8,3,128]{2,1,0:T(4,128)S(1)} %copy.439, f32[8,128]{1,0:T(8,128)S(1)} %get-tuple-element.790, ...), kind=kLoop, calls=%fused_computation.71.clone.1 | loop fusion | flops 12973056 | bytes 143456 | tf_op jit(solution)/shard_map/while/body/eval_jaxpr/vmap()/reduce_sum | solution.py:62
  72.6 2.6 %multiply_reduce_fusion.9 = (f32[8,128]{1,0:T(8,128)S(1)}, f32[8,128]{1,0:T(8,128)S(1)}, f32[8,128]{1,0:T(8,128)S(1)}) fusion(f32[8,3]{1,0:T(8,128)S(1)} %copy.435, f32[8,3,128]{2,1,0:T(4,128)S(1)} %copy.437, f32[8,128]{1,0:T(8,128)S(1)} %get-tuple-element.786, f32[8,3,128]{2,1,0:T(4,128)S(1)} %copy.439, f32[8,128]{1,0:T(8,128)S(1)} %get-tuple-element.790, ...), kind=kLoop, calls=%fused_computation.71.clone.1 | loop fusion | flops 12973056 | bytes 143456 | tf_op jit(solution)/shard_map/while/body/eval_jaxpr/vmap()/reduce_sum | solution.py:62
  76.5 2.6 %multiply_reduce_fusion.9 = (f32[8,128]{1,0:T(8,128)S(1)}, f32[8,128]{1,0:T(8,128)S(1)}, f32[8,128]{1,0:T(8,128)S(1)}) fusion(f32[8,3]{1,0:T(8,128)S(1)} %copy.435, f32[8,3,128]{2,1,0:T(4,128)S(1)} %copy.437, f32[8,128]{1,0:T(8,128)S(1)} %get-tuple-element.786, f32[8,3,128]{2,1,0:T(4,128)S(1)} %copy.439, f32[8,128]{1,0:T(8,128)S(1)} %get-tuple-element.790, ...), kind=kLoop, calls=%fused_computation.71.clone.1 | loop fusion | flops 12973056 | bytes 143456 | tf_op jit(solution)/shard_map/while/body/eval_jaxpr/vmap()/reduce_sum | solution.py:62
  80.3 2.6 %multiply_reduce_fusion.9 = (f32[8,128]{1,0:T(8,128)S(1)}, f32[8,128]{1,0:T(8,128)S(1)}, f32[8,128]{1,0:T(8,128)S(1)}) fusion(f32[8,3]{1,0:T(8,128)S(1)} %copy.435, f32[8,3,128]{2,1,0:T(4,128)S(1)} %copy.437, f32[8,128]{1,0:T(8,128)S(1)} %get-tuple-element.786, f32[8,3,128]{2,1,0:T(4,128)S(1)} %copy.439, f32[8,128]{1,0:T(8,128)S(1)} %get-tuple-element.790, ...), kind=kLoop, calls=%fused_computation.71.clone.1 | loop fusion | flops 12973056 | bytes 143456 | tf_op jit(solution)/shard_map/while/body/eval_jaxpr/vmap()/reduce_sum | solution.py:62
  84.2 2.6 %multiply_reduce_fusion.9 = (f32[8,128]{1,0:T(8,128)S(1)}, f32[8,128]{1,0:T(8,128)S(1)}, f32[8,128]{1,0:T(8,128)S(1)}) fusion(f32[8,3]{1,0:T(8,128)S(1)} %copy.435, f32[8,3,128]{2,1,0:T(4,128)S(1)} %copy.437, f32[8,128]{1,0:T(8,128)S(1)} %get-tuple-element.786, f32[8,3,128]{2,1,0:T(4,128)S(1)} %copy.439, f32[8,128]{1,0:T(8,128)S(1)} %get-tuple-element.790, ...), kind=kLoop, calls=%fused_computation.71.clone.1 | loop fusion | flops 12973056 | bytes 143456 | tf_op jit(solution)/shard_map/while/body/eval_jaxpr/vmap()/reduce_sum | solution.py:62
  88.0 2.6 %multiply_reduce_fusion.9 = (f32[8,128]{1,0:T(8,128)S(1)}, f32[8,128]{1,0:T(8,128)S(1)}, f32[8,128]{1,0:T(8,128)S(1)}) fusion(f32[8,3]{1,0:T(8,128)S(1)} %copy.435, f32[8,3,128]{2,1,0:T(4,128)S(1)} %copy.437, f32[8,128]{1,0:T(8,128)S(1)} %get-tuple-element.786, f32[8,3,128]{2,1,0:T(4,128)S(1)} %copy.439, f32[8,128]{1,0:T(8,128)S(1)} %get-tuple-element.790, ...), kind=kLoop, calls=%fused_computation.71.clone.1 | loop fusion | flops 12973056 | bytes 143456 | tf_op jit(solution)/shard_map/while/body/eval_jaxpr/vmap()/reduce_sum | solution.py:62
  91.9 2.6 %multiply_reduce_fusion.9 = (f32[8,128]{1,0:T(8,128)S(1)}, f32[8,128]{1,0:T(8,128)S(1)}, f32[8,128]{1,0:T(8,128)S(1)}) fusion(f32[8,3]{1,0:T(8,128)S(1)} %copy.435, f32[8,3,128]{2,1,0:T(4,128)S(1)} %copy.437, f32[8,128]{1,0:T(8,128)S(1)} %get-tuple-element.786, f32[8,3,128]{2,1,0:T(4,128)S(1)} %copy.439, f32[8,128]{1,0:T(8,128)S(1)} %get-tuple-element.790, ...), kind=kLoop, calls=%fused_computation.71.clone.1 | loop fusion | flops 12973056 | bytes 143456 | tf_op jit(solution)/shard_map/while/body/eval_jaxpr/vmap()/reduce_sum | solution.py:62
  94.9 1.9 collective-permute-start.4
  96.8 8.6 %collective-permute-start.5 = (f32[16,8,128]{2,1,0:T(8,128)S(1)}, f32[16,8,128]{2,1,0:T(8,128)S(1)}, u32[]{:S(2)}, u32[]{:S(2)}) collective-permute-start(f32[16,8,128]{2,1,0:T(8,128)S(1)} %get-tuple-element.454), channel_id=1, source_target_pairs={{1,0},{2,1},{3,2},{4,3},{5,4},{6,5},{7,6},{8,7},{9,8},{10,9},{11,1... | collective-permute-start | bytes 196616 | tf_op jit(solution)/shard_map/ppermute | solution.py:26
  105.7 1.9 collective-permute-done.5
  107.7 30.8 %while.55 = (s32[]{:T(128)}, f32[8,8,3,128]{3,1,2,0:T(8,128)S(1)}, f32[8,8,8,128]{3,2,1,0:T(8,128)S(1)}, s32[8,8,3]{1,2,0:T(4,128)S(1)}, f32[96,8,128]{2,1,0:T(8,128)S(1)}, /*index=5*/s32[8,8]{1,0:T(8,128)S(1)}, s32[]{:T(128)}) while((s32[]{:T(128)}, f32[8,8,3,128]{3,1,2,0:T(8,128)S(1)}, f32[8,8,8,128]{3,2,1,0:T(8,128)S(1)}, ...), condition=%wide.region_14.15_spmd, body=%wide.region_10.14_spmd.sunk | while | flops 12980370 | bytes 1156605 | solution.py:83
  108.9 2.6 %multiply_reduce_fusion.10 = (f32[8,128]{1,0:T(8,128)S(1)}, f32[8,128]{1,0:T(8,128)S(1)}, f32[8,128]{1,0:T(8,128)S(1)}) fusion(f32[8,3]{1,0:T(8,128)S(1)} %copy.450, f32[8,3,128]{2,1,0:T(4,128)S(1)} %copy.452, f32[8,128]{1,0:T(8,128)S(1)} %get-tuple-element.821, f32[8,3,128]{2,1,0:T(4,128)S(1)} %copy.454, f32[8,128]{1,0:T(8,128)S(1)} %get-tuple-element.825, ...), kind=kLoop, calls=%fused_computation.119.clone.1 | loop fusion | flops 12973056 | bytes 143456 | tf_op jit(solution)/shard_map/while/body/eval_jaxpr/vmap()/reduce_sum | solution.py:62
  112.8 2.6 %multiply_reduce_fusion.10 = (f32[8,128]{1,0:T(8,128)S(1)}, f32[8,128]{1,0:T(8,128)S(1)}, f32[8,128]{1,0:T(8,128)S(1)}) fusion(f32[8,3]{1,0:T(8,128)S(1)} %copy.450, f32[8,3,128]{2,1,0:T(4,128)S(1)} %copy.452, f32[8,128]{1,0:T(8,128)S(1)} %get-tuple-element.821, f32[8,3,128]{2,1,0:T(4,128)S(1)} %copy.454, f32[8,128]{1,0:T(8,128)S(1)} %get-tuple-element.825, ...), kind=kLoop, calls=%fused_computation.119.clone.1 | loop fusion | flops 12973056 | bytes 143456 | tf_op jit(solution)/shard_map/while/body/eval_jaxpr/vmap()/reduce_sum | solution.py:62
  116.6 2.6 %multiply_reduce_fusion.10 = (f32[8,128]{1,0:T(8,128)S(1)}, f32[8,128]{1,0:T(8,128)S(1)}, f32[8,128]{1,0:T(8,128)S(1)}) fusion(f32[8,3]{1,0:T(8,128)S(1)} %copy.450, f32[8,3,128]{2,1,0:T(4,128)S(1)} %copy.452, f32[8,128]{1,0:T(8,128)S(1)} %get-tuple-element.821, f32[8,3,128]{2,1,0:T(4,128)S(1)} %copy.454, f32[8,128]{1,0:T(8,128)S(1)} %get-tuple-element.825, ...), kind=kLoop, calls=%fused_computation.119.clone.1 | loop fusion | flops 12973056 | bytes 143456 | tf_op jit(solution)/shard_map/while/body/eval_jaxpr/vmap()/reduce_sum | solution.py:62
  120.5 2.6 %multiply_reduce_fusion.10 = (f32[8,128]{1,0:T(8,128)S(1)}, f32[8,128]{1,0:T(8,128)S(1)}, f32[8,128]{1,0:T(8,128)S(1)}) fusion(f32[8,3]{1,0:T(8,128)S(1)} %copy.450, f32[8,3,128]{2,1,0:T(4,128)S(1)} %copy.452, f32[8,128]{1,0:T(8,128)S(1)} %get-tuple-element.821, f32[8,3,128]{2,1,0:T(4,128)S(1)} %copy.454, f32[8,128]{1,0:T(8,128)S(1)} %get-tuple-element.825, ...), kind=kLoop, calls=%fused_computation.119.clone.1 | loop fusion | flops 12973056 | bytes 143456 | tf_op jit(solution)/shard_map/while/body/eval_jaxpr/vmap()/reduce_sum | solution.py:62
  124.3 2.6 %multiply_reduce_fusion.10 = (f32[8,128]{1,0:T(8,128)S(1)}, f32[8,128]{1,0:T(8,128)S(1)}, f32[8,128]{1,0:T(8,128)S(1)}) fusion(f32[8,3]{1,0:T(8,128)S(1)} %copy.450, f32[8,3,128]{2,1,0:T(4,128)S(1)} %copy.452, f32[8,128]{1,0:T(8,128)S(1)} %get-tuple-element.821, f32[8,3,128]{2,1,0:T(4,128)S(1)} %copy.454, f32[8,128]{1,0:T(8,128)S(1)} %get-tuple-element.825, ...), kind=kLoop, calls=%fused_computation.119.clone.1 | loop fusion | flops 12973056 | bytes 143456 | tf_op jit(solution)/shard_map/while/body/eval_jaxpr/vmap()/reduce_sum | solution.py:62
  128.2 2.6 %multiply_reduce_fusion.10 = (f32[8,128]{1,0:T(8,128)S(1)}, f32[8,128]{1,0:T(8,128)S(1)}, f32[8,128]{1,0:T(8,128)S(1)}) fusion(f32[8,3]{1,0:T(8,128)S(1)} %copy.450, f32[8,3,128]{2,1,0:T(4,128)S(1)} %copy.452, f32[8,128]{1,0:T(8,128)S(1)} %get-tuple-element.821, f32[8,3,128]{2,1,0:T(4,128)S(1)} %copy.454, f32[8,128]{1,0:T(8,128)S(1)} %get-tuple-element.825, ...), kind=kLoop, calls=%fused_computation.119.clone.1 | loop fusion | flops 12973056 | bytes 143456 | tf_op jit(solution)/shard_map/while/body/eval_jaxpr/vmap()/reduce_sum | solution.py:62
  132.0 2.6 %multiply_reduce_fusion.10 = (f32[8,128]{1,0:T(8,128)S(1)}, f32[8,128]{1,0:T(8,128)S(1)}, f32[8,128]{1,0:T(8,128)S(1)}) fusion(f32[8,3]{1,0:T(8,128)S(1)} %copy.450, f32[8,3,128]{2,1,0:T(4,128)S(1)} %copy.452, f32[8,128]{1,0:T(8,128)S(1)} %get-tuple-element.821, f32[8,3,128]{2,1,0:T(4,128)S(1)} %copy.454, f32[8,128]{1,0:T(8,128)S(1)} %get-tuple-element.825, ...), kind=kLoop, calls=%fused_computation.119.clone.1 | loop fusion | flops 12973056 | bytes 143456 | tf_op jit(solution)/shard_map/while/body/eval_jaxpr/vmap()/reduce_sum | solution.py:62
  135.9 2.6 %multiply_reduce_fusion.10 = (f32[8,128]{1,0:T(8,128)S(1)}, f32[8,128]{1,0:T(8,128)S(1)}, f32[8,128]{1,0:T(8,128)S(1)}) fusion(f32[8,3]{1,0:T(8,128)S(1)} %copy.450, f32[8,3,128]{2,1,0:T(4,128)S(1)} %copy.452, f32[8,128]{1,0:T(8,128)S(1)} %get-tuple-element.821, f32[8,3,128]{2,1,0:T(4,128)S(1)} %copy.454, f32[8,128]{1,0:T(8,128)S(1)} %get-tuple-element.825, ...), kind=kLoop, calls=%fused_computation.119.clone.1 | loop fusion | flops 12973056 | bytes 143456 | tf_op jit(solution)/shard_map/while/body/eval_jaxpr/vmap()/reduce_sum | solution.py:62
  138.9 1.9 collective-permute-start.6
  140.8 8.6 %collective-permute-start.7 = (f32[16,8,128]{2,1,0:T(8,128)S(1)}, f32[16,8,128]{2,1,0:T(8,128)S(1)}, u32[]{:S(2)}, u32[]{:S(2)}) collective-permute-start(f32[16,8,128]{2,1,0:T(8,128)S(1)} %get-tuple-element.452), channel_id=1, source_target_pairs={{1,0},{2,1},{3,2},{4,3},{5,4},{6,5},{7,6},{8,7},{9,8},{10,9},{11,1... | collective-permute-start | bytes 196616 | tf_op jit(solution)/shard_map/ppermute | solution.py:26
  151.5 30.8 %while.56 = (s32[]{:T(128)}, f32[8,8,3,128]{3,1,2,0:T(8,128)S(1)}, f32[8,8,8,128]{3,2,1,0:T(8,128)S(1)}, s32[8,8,3]{1,2,0:T(4,128)S(1)}, f32[96,8,128]{2,1,0:T(8,128)S(1)}, /*index=5*/s32[8,8]{1,0:T(8,128)S(1)}, s32[]{:T(128)}) while((s32[]{:T(128)}, f32[8,8,3,128]{3,1,2,0:T(8,128)S(1)}, f32[8,8,8,128]{3,2,1,0:T(8,128)S(1)}, ...), condition=%wide.region_19.20_spmd, body=%wide.region_15.19_spmd.sunk | while | flops 12980370 | bytes 1156605 | solution.py:83
  152.6 2.6 %multiply_reduce_fusion.11 = (f32[8,128]{1,0:T(8,128)S(1)}, f32[8,128]{1,0:T(8,128)S(1)}, f32[8,128]{1,0:T(8,128)S(1)}) fusion(f32[8,3]{1,0:T(8,128)S(1)} %copy.465, f32[8,3,128]{2,1,0:T(4,128)S(1)} %copy.467, f32[8,128]{1,0:T(8,128)S(1)} %get-tuple-element.856, f32[8,3,128]{2,1,0:T(4,128)S(1)} %copy.469, f32[8,128]{1,0:T(8,128)S(1)} %get-tuple-element.860, ...), kind=kLoop, calls=%fused_computation.167.clone.1 | loop fusion | flops 12973056 | bytes 143456 | tf_op jit(solution)/shard_map/while/body/eval_jaxpr/vmap()/reduce_sum | solution.py:62
  156.5 2.6 %multiply_reduce_fusion.11 = (f32[8,128]{1,0:T(8,128)S(1)}, f32[8,128]{1,0:T(8,128)S(1)}, f32[8,128]{1,0:T(8,128)S(1)}) fusion(f32[8,3]{1,0:T(8,128)S(1)} %copy.465, f32[8,3,128]{2,1,0:T(4,128)S(1)} %copy.467, f32[8,128]{1,0:T(8,128)S(1)} %get-tuple-element.856, f32[8,3,128]{2,1,0:T(4,128)S(1)} %copy.469, f32[8,128]{1,0:T(8,128)S(1)} %get-tuple-element.860, ...), kind=kLoop, calls=%fused_computation.167.clone.1 | loop fusion | flops 12973056 | bytes 143456 | tf_op jit(solution)/shard_map/while/body/eval_jaxpr/vmap()/reduce_sum | solution.py:62
  160.3 2.6 %multiply_reduce_fusion.11 = (f32[8,128]{1,0:T(8,128)S(1)}, f32[8,128]{1,0:T(8,128)S(1)}, f32[8,128]{1,0:T(8,128)S(1)}) fusion(f32[8,3]{1,0:T(8,128)S(1)} %copy.465, f32[8,3,128]{2,1,0:T(4,128)S(1)} %copy.467, f32[8,128]{1,0:T(8,128)S(1)} %get-tuple-element.856, f32[8,3,128]{2,1,0:T(4,128)S(1)} %copy.469, f32[8,128]{1,0:T(8,128)S(1)} %get-tuple-element.860, ...), kind=kLoop, calls=%fused_computation.167.clone.1 | loop fusion | flops 12973056 | bytes 143456 | tf_op jit(solution)/shard_map/while/body/eval_jaxpr/vmap()/reduce_sum | solution.py:62
  164.2 2.6 %multiply_reduce_fusion.11 = (f32[8,128]{1,0:T(8,128)S(1)}, f32[8,128]{1,0:T(8,128)S(1)}, f32[8,128]{1,0:T(8,128)S(1)}) fusion(f32[8,3]{1,0:T(8,128)S(1)} %copy.465, f32[8,3,128]{2,1,0:T(4,128)S(1)} %copy.467, f32[8,128]{1,0:T(8,128)S(1)} %get-tuple-element.856, f32[8,3,128]{2,1,0:T(4,128)S(1)} %copy.469, f32[8,128]{1,0:T(8,128)S(1)} %get-tuple-element.860, ...), kind=kLoop, calls=%fused_computation.167.clone.1 | loop fusion | flops 12973056 | bytes 143456 | tf_op jit(solution)/shard_map/while/body/eval_jaxpr/vmap()/reduce_sum | solution.py:62
  168.1 2.6 %multiply_reduce_fusion.11 = (f32[8,128]{1,0:T(8,128)S(1)}, f32[8,128]{1,0:T(8,128)S(1)}, f32[8,128]{1,0:T(8,128)S(1)}) fusion(f32[8,3]{1,0:T(8,128)S(1)} %copy.465, f32[8,3,128]{2,1,0:T(4,128)S(1)} %copy.467, f32[8,128]{1,0:T(8,128)S(1)} %get-tuple-element.856, f32[8,3,128]{2,1,0:T(4,128)S(1)} %copy.469, f32[8,128]{1,0:T(8,128)S(1)} %get-tuple-element.860, ...), kind=kLoop, calls=%fused_computation.167.clone.1 | loop fusion | flops 12973056 | bytes 143456 | tf_op jit(solution)/shard_map/while/body/eval_jaxpr/vmap()/reduce_sum | solution.py:62
  171.9 2.6 %multiply_reduce_fusion.11 = (f32[8,128]{1,0:T(8,128)S(1)}, f32[8,128]{1,0:T(8,128)S(1)}, f32[8,128]{1,0:T(8,128)S(1)}) fusion(f32[8,3]{1,0:T(8,128)S(1)} %copy.465, f32[8,3,128]{2,1,0:T(4,128)S(1)} %copy.467, f32[8,128]{1,0:T(8,128)S(1)} %get-tuple-element.856, f32[8,3,128]{2,1,0:T(4,128)S(1)} %copy.469, f32[8,128]{1,0:T(8,128)S(1)} %get-tuple-element.860, ...), kind=kLoop, calls=%fused_computation.167.clone.1 | loop fusion | flops 12973056 | bytes 143456 | tf_op jit(solution)/shard_map/while/body/eval_jaxpr/vmap()/reduce_sum | solution.py:62
  175.8 2.6 %multiply_reduce_fusion.11 = (f32[8,128]{1,0:T(8,128)S(1)}, f32[8,128]{1,0:T(8,128)S(1)}, f32[8,128]{1,0:T(8,128)S(1)}) fusion(f32[8,3]{1,0:T(8,128)S(1)} %copy.465, f32[8,3,128]{2,1,0:T(4,128)S(1)} %copy.467, f32[8,128]{1,0:T(8,128)S(1)} %get-tuple-element.856, f32[8,3,128]{2,1,0:T(4,128)S(1)} %copy.469, f32[8,128]{1,0:T(8,128)S(1)} %get-tuple-element.860, ...), kind=kLoop, calls=%fused_computation.167.clone.1 | loop fusion | flops 12973056 | bytes 143456 | tf_op jit(solution)/shard_map/while/body/eval_jaxpr/vmap()/reduce_sum | solution.py:62
  179.6 2.6 %multiply_reduce_fusion.11 = (f32[8,128]{1,0:T(8,128)S(1)}, f32[8,128]{1,0:T(8,128)S(1)}, f32[8,128]{1,0:T(8,128)S(1)}) fusion(f32[8,3]{1,0:T(8,128)S(1)} %copy.465, f32[8,3,128]{2,1,0:T(4,128)S(1)} %copy.467, f32[8,128]{1,0:T(8,128)S(1)} %get-tuple-element.856, f32[8,3,128]{2,1,0:T(4,128)S(1)} %copy.469, f32[8,128]{1,0:T(8,128)S(1)} %get-tuple-element.860, ...), kind=kLoop, calls=%fused_computation.167.clone.1 | loop fusion | flops 12973056 | bytes 143456 | tf_op jit(solution)/shard_map/while/body/eval_jaxpr/vmap()/reduce_sum | solution.py:62
  183.0 16.0 %while.57 = (s32[]{:T(128)}, f32[3,1024]{1,0:T(4,128)S(1)}, f32[1024]{0:T(1024)S(1)}, f32[8,8,3,128]{3,2,1,0:T(4,128)S(1)}, s32[8,1024]{1,0:T(8,128)S(1)}, /*index=5*/s32[]{:T(128)}, s32[]{:T(128)}) while((s32[]{:T(128)}, f32[3,1024]{1,0:T(4,128)S(1)}, f32[1024]{0:T(1024)S(1)}, f32[8,8,3,128]{3,2,1,0:T(4,128)S(1)}, ...), condition=%wide.region_22.23_spmd.clone, body=%wide.region_20.22_spmd.clone.sunk | while | flops 41950208 | bytes 77920 | solution.py:126
  199.9 1.9 collective-permute-start.8
  203.1 3.1 %collective-permute-start.9 = (f32[8,1024]{1,0:T(8,128)S(1)}, f32[8,1024]{1,0:T(8,128)S(1)}, u32[]{:S(2)}, u32[]{:S(2)}) collective-permute-start(f32[8,1024]{1,0:T(8,128)S(1)} %fusion.95), channel_id=1, source_target_pairs={{0,64},{32,96},{64,0},{96,32},{128,192},{160,224},{192,128},{224,1... | collective-permute-start | bytes 98312 | tf_op jit(solution)/shard_map/ppermute | solution.py:39
  206.2 2.7 %collective-permute-done.9 = f32[8,1024]{1,0:T(8,128)S(1)} collective-permute-done((f32[8,1024]{1,0:T(8,128)S(1)}, f32[8,1024]{1,0:T(8,128)S(1)}, u32[]{:S(2)}, u32[]{:S(2)}) %collective-permute-start.9) | collective-permute-done | bytes 32800 | tf_op jit(solution)/shard_map/ppermute | solution.py:39
  208.9 2.4 collective-permute-start.10
  211.3 4.9 %collective-permute-done.10 = f32[8,1024]{1,0:T(8,128)S(1)} collective-permute-done((f32[8,1024]{1,0:T(8,128)S(1)}, f32[8,1024]{1,0:T(8,128)S(1)}, u32[]{:S(2)}, u32[]{:S(2)}) %collective-permute-start.10) | collective-permute-done | bytes 32800 | tf_op jit(solution)/shard_map/ppermute | solution.py:39
  216.2 1.9 collective-permute-start.11
  218.1 3.9 %collective-permute-done.11 = f32[8,1024]{1,0:T(8,128)S(1)} collective-permute-done((f32[8,1024]{1,0:T(8,128)S(1)}, f32[8,1024]{1,0:T(8,128)S(1)}, u32[]{:S(2)}, u32[]{:S(2)}) %collective-permute-start.11) | collective-permute-done | bytes 32800 | tf_op jit(solution)/shard_map/ppermute | solution.py:39
  223.1 1.9 collective-permute-start.12
  225.1 3.6 %collective-permute-done.12 = f32[8,128]{1,0:T(8,128)S(1)} collective-permute-done((f32[8,128]{1,0:T(8,128)S(1)}, f32[8,128]{1,0:T(8,128)S(1)}, u32[]{:S(2)}, u32[]{:S(2)}) %collective-permute-start.12) | collective-permute-done | bytes 4128 | tf_op jit(solution)/shard_map/ppermute | solution.py:39
  229.3 1.9 collective-permute-start.13
  231.9 3.8 %collective-permute-done.13 = f32[8,128]{1,0:T(8,128)S(1)} collective-permute-done((f32[8,128]{1,0:T(8,128)S(1)}, f32[8,128]{1,0:T(8,128)S(1)}, u32[]{:S(2)}, u32[]{:S(2)}) %collective-permute-start.13) | collective-permute-done | bytes 4128 | tf_op jit(solution)/shard_map/ppermute | solution.py:39
  236.4 1.9 collective-permute-start.14
  238.3 7.5 %collective-permute-done.14 = f32[8,128]{1,0:T(8,128)S(1)} collective-permute-done((f32[8,128]{1,0:T(8,128)S(1)}, f32[8,128]{1,0:T(8,128)S(1)}, u32[]{:S(2)}, u32[]{:S(2)}) %collective-permute-start.14) | collective-permute-done | bytes 4128 | tf_op jit(solution)/shard_map/ppermute | solution.py:39
  245.8 2.0 collective-permute-start.15
  248.5 3.7 %collective-permute-done.15 = f32[8,128]{1,0:T(8,128)S(1)} collective-permute-done((f32[8,128]{1,0:T(8,128)S(1)}, f32[8,128]{1,0:T(8,128)S(1)}, u32[]{:S(2)}, u32[]{:S(2)}) %collective-permute-start.15) | collective-permute-done | bytes 4128 | tf_op jit(solution)/shard_map/ppermute | solution.py:39
  252.3 1.9 collective-permute-start.16
  254.8 6.9 %collective-permute-done.16 = f32[8,128]{1,0:T(8,128)S(1)} collective-permute-done((f32[8,128]{1,0:T(8,128)S(1)}, f32[8,128]{1,0:T(8,128)S(1)}, u32[]{:S(2)}, u32[]{:S(2)}) %collective-permute-start.16) | collective-permute-done | bytes 4128 | tf_op jit(solution)/shard_map/ppermute | solution.py:39
  (909 shorter events, 65.8 us)
Async XLA Ops:
  1.5 1.1 copy-start
  2.6 12.9 %copy-start.4 = (s32[1,64,3]{1,0,2:T(1,128)S(1)}, s32[1,64,3]{1,0,2:T(1,128)}, u32[]{:S(2)}) copy-start(s32[1,64,3]{1,0,2:T(1,128)} %param.22) | copy-start | bytes 2308
  2.6 13.0 %copy-start.3 = (s32[1,64,128]{2,1,0:T(8,128)S(1)}, s32[1,64,128]{2,1,0:T(8,128)}, u32[]{:S(2)}) copy-start(s32[1,64,128]{2,1,0:T(8,128)} %param.23) | copy-start | bytes 98308
  2.8 14.2 %collective-permute-start = (f32[16,8,128]{2,1,0:T(8,128)S(1)}, f32[16,8,128]{2,1,0:T(8,128)S(1)}, u32[]{:S(2)}, u32[]{:S(2)}) collective-permute-start(f32[16,8,128]{2,1,0:T(8,128)S(1)} %get-tuple-element.457), channel_id=1, source_target_pairs={{0,1},{1,2},{2,3},{3,4},{4,5},{5,6},{6,7},{7,8},{8,9},{9,10},{10,1... | collective-permute-start | bytes 196616 | tf_op jit(solution)/shard_map/ppermute | solution.py:25
  7.1 10.8 %collective-permute-start.1 = (f32[16,8,128]{2,1,0:T(8,128)S(1)}, f32[16,8,128]{2,1,0:T(8,128)S(1)}, u32[]{:S(2)}, u32[]{:S(2)}) collective-permute-start(f32[16,8,128]{2,1,0:T(8,128)S(1)} %get-tuple-element.458), channel_id=1, source_target_pairs={{1,0},{2,1},{3,2},{4,3},{5,4},{6,5},{7,6},{8,7},{9,8},{10,9},{11,1... | collective-permute-start | bytes 196616 | tf_op jit(solution)/shard_map/ppermute | solution.py:26
  48.9 0.9 copy-start.1
  48.9 0.9 copy-start.2
  50.1 11.4 %collective-permute-start.2 = (f32[16,8,128]{2,1,0:T(8,128)S(1)}, f32[16,8,128]{2,1,0:T(8,128)S(1)}, u32[]{:S(2)}, u32[]{:S(2)}) collective-permute-start(f32[16,8,128]{2,1,0:T(8,128)S(1)} %get-tuple-element.455), channel_id=1, source_target_pairs={{0,1},{1,2},{2,3},{3,4},{4,5},{5,6},{6,7},{7,8},{8,9},{9,10},{10,1... | collective-permute-start | bytes 196616 | tf_op jit(solution)/shard_map/ppermute | solution.py:25
  52.1 11.5 %collective-permute-start.3 = (f32[16,8,128]{2,1,0:T(8,128)S(1)}, f32[16,8,128]{2,1,0:T(8,128)S(1)}, u32[]{:S(2)}, u32[]{:S(2)}) collective-permute-start(f32[16,8,128]{2,1,0:T(8,128)S(1)} %get-tuple-element.456), channel_id=1, source_target_pairs={{1,0},{2,1},{3,2},{4,3},{5,4},{6,5},{7,6},{8,7},{9,8},{10,9},{11,1... | collective-permute-start | bytes 196616 | tf_op jit(solution)/shard_map/ppermute | solution.py:26
  94.9 10.8 %collective-permute-start.4 = (f32[16,8,128]{2,1,0:T(8,128)S(1)}, f32[16,8,128]{2,1,0:T(8,128)S(1)}, u32[]{:S(2)}, u32[]{:S(2)}) collective-permute-start(f32[16,8,128]{2,1,0:T(8,128)S(1)} %get-tuple-element.453), channel_id=1, source_target_pairs={{0,1},{1,2},{2,3},{3,4},{4,5},{5,6},{6,7},{7,8},{8,9},{9,10},{10,1... | collective-permute-start | bytes 196616 | tf_op jit(solution)/shard_map/ppermute | solution.py:25
  96.8 10.7 %collective-permute-start.5 = (f32[16,8,128]{2,1,0:T(8,128)S(1)}, f32[16,8,128]{2,1,0:T(8,128)S(1)}, u32[]{:S(2)}, u32[]{:S(2)}) collective-permute-start(f32[16,8,128]{2,1,0:T(8,128)S(1)} %get-tuple-element.454), channel_id=1, source_target_pairs={{1,0},{2,1},{3,2},{4,3},{5,4},{6,5},{7,6},{8,7},{9,8},{10,9},{11,1... | collective-permute-start | bytes 196616 | tf_op jit(solution)/shard_map/ppermute | solution.py:26
  138.9 10.8 %collective-permute-start.6 = (f32[16,8,128]{2,1,0:T(8,128)S(1)}, f32[16,8,128]{2,1,0:T(8,128)S(1)}, u32[]{:S(2)}, u32[]{:S(2)}) collective-permute-start(f32[16,8,128]{2,1,0:T(8,128)S(1)} %get-tuple-element.451), channel_id=1, source_target_pairs={{0,1},{1,2},{2,3},{3,4},{4,5},{5,6},{6,7},{7,8},{8,9},{9,10},{10,1... | collective-permute-start | bytes 196616 | tf_op jit(solution)/shard_map/ppermute | solution.py:25
  140.8 10.5 %collective-permute-start.7 = (f32[16,8,128]{2,1,0:T(8,128)S(1)}, f32[16,8,128]{2,1,0:T(8,128)S(1)}, u32[]{:S(2)}, u32[]{:S(2)}) collective-permute-start(f32[16,8,128]{2,1,0:T(8,128)S(1)} %get-tuple-element.452), channel_id=1, source_target_pairs={{1,0},{2,1},{3,2},{4,3},{5,4},{6,5},{7,6},{8,7},{9,8},{10,9},{11,1... | collective-permute-start | bytes 196616 | tf_op jit(solution)/shard_map/ppermute | solution.py:26
  199.9 3.1 %collective-permute-start.8 = (f32[8,1024]{1,0:T(8,128)S(1)}, f32[8,1024]{1,0:T(8,128)S(1)}, u32[]{:S(2)}, u32[]{:S(2)}) collective-permute-start(f32[8,1024]{1,0:T(8,128)S(1)} %maximum_maximum_fusion), channel_id=1, source_target_pairs={{0,32},{32,0},{64,96},{96,64},{128,160},{160,128},{192,224},{224,1... | collective-permute-start | bytes 98312 | tf_op jit(solution)/shard_map/ppermute | solution.py:39
  203.1 5.8 %collective-permute-start.9 = (f32[8,1024]{1,0:T(8,128)S(1)}, f32[8,1024]{1,0:T(8,128)S(1)}, u32[]{:S(2)}, u32[]{:S(2)}) collective-permute-start(f32[8,1024]{1,0:T(8,128)S(1)} %fusion.95), channel_id=1, source_target_pairs={{0,64},{32,96},{64,0},{96,32},{128,192},{160,224},{192,128},{224,1... | collective-permute-start | bytes 98312 | tf_op jit(solution)/shard_map/ppermute | solution.py:39
  208.9 7.3 %collective-permute-start.10 = (f32[8,1024]{1,0:T(8,128)S(1)}, f32[8,1024]{1,0:T(8,128)S(1)}, u32[]{:S(2)}, u32[]{:S(2)}) collective-permute-start(f32[8,1024]{1,0:T(8,128)S(1)} %add.380), channel_id=1, source_target_pairs={{0,128},{32,160},{64,192},{96,224},{128,0},{160,32},{192,64},{224,... | collective-permute-start | bytes 98312 | tf_op jit(solution)/shard_map/ppermute | solution.py:39
  216.2 5.8 %collective-permute-start.11 = (f32[8,1024]{1,0:T(8,128)S(1)}, f32[8,1024]{1,0:T(8,128)S(1)}, u32[]{:S(2)}, u32[]{:S(2)}) collective-permute-start(f32[8,1024]{1,0:T(8,128)S(1)} %add.381), channel_id=1, source_target_pairs={{0,256},{32,288},{64,320},{96,352},{128,384},{160,416},{192,448},{... | collective-permute-start | bytes 98312 | tf_op jit(solution)/shard_map/ppermute | solution.py:39
  223.1 5.5 %collective-permute-start.12 = (f32[8,128]{1,0:T(8,128)S(1)}, f32[8,128]{1,0:T(8,128)S(1)}, u32[]{:S(2)}, u32[]{:S(2)}) collective-permute-start(f32[8,128]{1,0:T(8,128)S(1)} %broadcast_in_dim.74), channel_id=1, source_target_pairs={{0,1},{1,0},{2,3},{3,2},{4,5},{5,4},{6,7},{7,6},{8,9},{9,8},{10,11... | collective-permute-start | bytes 12296 | tf_op jit(solution)/shard_map/ppermute | solution.py:39
  229.3 6.4 %collective-permute-start.13 = (f32[8,128]{1,0:T(8,128)S(1)}, f32[8,128]{1,0:T(8,128)S(1)}, u32[]{:S(2)}, u32[]{:S(2)}) collective-permute-start(f32[8,128]{1,0:T(8,128)S(1)} %broadcast_add_fusion), channel_id=1, source_target_pairs={{0,2},{1,3},{2,0},{3,1},{4,6},{5,7},{6,4},{7,5},{8,10},{9,11},{10,... | collective-permute-start | bytes 12296 | tf_op jit(solution)/shard_map/ppermute | solution.py:39
  236.4 9.4 %collective-permute-start.14 = (f32[8,128]{1,0:T(8,128)S(1)}, f32[8,128]{1,0:T(8,128)S(1)}, u32[]{:S(2)}, u32[]{:S(2)}) collective-permute-start(f32[8,128]{1,0:T(8,128)S(1)} %fusion.112), channel_id=1, source_target_pairs={{0,4},{1,5},{2,6},{3,7},{4,0},{5,1},{6,2},{7,3},{8,12},{9,13},{10,... | collective-permute-start | bytes 12296 | tf_op jit(solution)/shard_map/ppermute | solution.py:39
  245.8 17.1 %copy-start.5 = (f32[1,3,128]{2,0,1:T(1,128)S(1)}, f32[1,3,128]{2,0,1:T(1,128)}, u32[]{:S(2)}) copy-start(f32[1,3,128]{2,0,1:T(1,128)} %param.24) | copy-start | bytes 4612
  245.8 6.5 %collective-permute-start.15 = (f32[8,128]{1,0:T(8,128)S(1)}, f32[8,128]{1,0:T(8,128)S(1)}, u32[]{:S(2)}, u32[]{:S(2)}) collective-permute-start(f32[8,128]{1,0:T(8,128)S(1)} %add.385), channel_id=1, source_target_pairs={{0,8},{1,9},{2,10},{3,11},{4,12},{5,13},{6,14},{7,15},{8,0},{9,1},... | collective-permute-start | bytes 12296 | tf_op jit(solution)/shard_map/ppermute | solution.py:39
  252.3 9.4 %collective-permute-start.16 = (f32[8,128]{1,0:T(8,128)S(1)}, f32[8,128]{1,0:T(8,128)S(1)}, u32[]{:S(2)}, u32[]{:S(2)}) collective-permute-start(f32[8,128]{1,0:T(8,128)S(1)} %add.386), channel_id=1, source_target_pairs={{0,16},{1,17},{2,18},{3,19},{4,20},{5,21},{6,22},{7,23},{8,24},{9,... | collective-permute-start | bytes 12296 | tf_op jit(solution)/shard_map/ppermute | solution.py:39

commit v4 on v3

--- a/solution.py
+++ b/solution.py
@@ -66,17 +66,15 @@
     )
 
 
-def slab_forces(extended, links):
-    tiles = links.shape[0]
-    margin = (extended.shape[0] - tiles) // 2
+def tile_forces(source, own_index, link_index):
+    tiles = own_index.shape[0]
     group = 8
-    width = extended.shape[-1]
-    own_index = jnp.arange(tiles, dtype=jnp.int32) + margin
-    own_tiles = extended[margin : margin + tiles]
+    width = source.shape[-1]
+    own_tiles = source[own_index]
 
     def per_group(item):
         own_group, link_group, index_group = item
-        partners = extended[link_group]
+        partners = source[link_group]
         shifts = SPACING * (index_group[:, None] - link_group).astype(jnp.float32)
         return jax.vmap(bead_forces)(own_group, partners, shifts)
 
@@ -84,7 +82,7 @@
         per_group,
         (
             own_tiles.reshape(tiles // group, group, 8, width),
-            links.reshape(tiles // group, group, links.shape[1]),
+            link_index.reshape(tiles // group, group, link_index.shape[1]),
             own_index.reshape(tiles // group, group),
         ),
     )
@@ -97,12 +95,28 @@
     weights = strength[0]
     links = neighbours[0]
     substeps = noise.shape[0]
+    tiles = links.shape[0]
+    count = lax.axis_size("space")
+    up = [(i, i + 1) for i in range(count - 1)]
+    down = [(i + 1, i) for i in range(count - 1)]
+    local = jnp.arange(tiles, dtype=jnp.int32)
+    inner = local[HALO : tiles - HALO]
+    outer = jnp.concatenate([local[:HALO], local[tiles - HALO :]])
+    inner_links = links[HALO : tiles - HALO] - HALO
+    outer_links = jnp.concatenate([links[:HALO], links[tiles - HALO :]], axis=0)
     for substep in range(substeps):
         packed = jnp.concatenate(
             [place, speed, weights[:, None, :], noise[substep, 0][:, None, :]], axis=1
         )
-        extended = padded(packed, (("space", 0),), HALO)
-        speed = speed + TIME_STEP * slab_forces(extended, links)
+        before = lax.ppermute(packed[tiles - HALO :], "space", up)
+        after = lax.ppermute(packed[:HALO], "space", down)
+        inner_force = tile_forces(packed, inner, inner_links)
+        extended = jnp.concatenate([before, packed, after], axis=0)
+        outer_force = tile_forces(extended, outer + HALO, outer_links)
+        force = jnp.concatenate(
+            [outer_force[:HALO], inner_force, outer_force[HALO:]], axis=0
+        )
+        speed = speed + TIME_STEP * force
         place = place + TIME_STEP * speed
     tiles = speed.shape[0]
     width = speed.shape[-1]

time: 264 us -> 260 us (0.985)
  the two profiles are of different devices: /device:TPU:36 before, /device:TPU:46 now
where the time goes in v4:
time: 260 us; the launch traced here: 259 us
  other arithmetic  95.5 us (37%)
  starting transfers between devices  63.8 us (25%)
  local copies, waits for them, and re-layouts  41.7 us (16%)
  waiting for transfers between devices  37 us (14%)
  matrix products  11.7 us (4%)
  loops' own time  6.37 us (2%)
  between operations  2.85 us (1%)
    reduce_sum x32, other arithmetic, bead_forces(): jnp.sum(factor * offset_x, axis=(0, 2))  84.4 us
    ppermute x9, waiting for transfers between devices, butterfly_sum(): leaves.append(lax.ppermute(value, axis, pairs))  37 us
    ppermute x4, starting transfers between devices, shards(): after = lax.ppermute(packed[:HALO], 'space', down)  33.9 us
    ppermute x9, starting transfers between devices, butterfly_sum(): leaves.append(lax.ppermute(value, axis, pairs))  19.9 us
    gather x32, local copies, waits for them, and re-layouts, per_group(): partners = source[link_group]  18.5 us
    dot_general x8, matrix products, accumulate(): jnp.dot(rows_now, table, precision=lax.Precision.HIGHEST, preferred_eleme...  11.7 us
    ppermute x4, starting transfers between devices, shards(): before = lax.ppermute(packed[tiles - HALO:], 'space', up)  10 us
    another operation x8, loops' own time, tile_forces(): lax.map(per_group, (own_tiles.reshape(tiles // group, group, 8, width), l...  6.02 us
  transfers between devices with their start and end apart: 17, of which 9 were waited for; matrix products, arithmetic and copies ran while one was open for 24% of the time, Pallas kernels for 0%

profile of v4, /device:TPU:46, one launch (start us, length us, event | category | flops | bytes accessed | tf_op | source)
XLA Modules:
  0.0 258.9 jit_solution(10354151709683170167)
XLA Ops:
  2.7 4.3 %collective-permute-start = (f32[16,8,128]{2,1,0:T(8,128)S(1)}, f32[16,8,128]{2,1,0:T(8,128)S(1)}, u32[]{:S(2)}, u32[]{:S(2)}) collective-permute-start(f32[16,8,128]{2,1,0:T(8,128)S(1)} %get-tuple-element.963), channel_id=1, source_target_pairs={{0,1},{1,2},{2,3},{3,4},{4,5},{5,6},{6,7},{7,8},{8,9},{9,10},{10,1... | collective-permute-start | bytes 196616 | tf_op jit(solution)/shard_map/ppermute | solution.py:111
  7.0 9.3 %collective-permute-start.1 = (f32[16,8,128]{2,1,0:T(8,128)S(1)}, f32[16,8,128]{2,1,0:T(8,128)S(1)}, u32[]{:S(2)}, u32[]{:S(2)}) collective-permute-start(f32[16,8,128]{2,1,0:T(8,128)S(1)} %get-tuple-element.964), channel_id=1, source_target_pairs={{1,0},{2,1},{3,2},{4,3},{5,4},{6,5},{7,6},{8,7},{9,8},{10,9},{11,1... | collective-permute-start | bytes 196616 | tf_op jit(solution)/shard_map/ppermute | solution.py:112
  17.9 15.4 %while.94 = (s32[]{:T(128)}, f32[4,8,3,128]{3,1,2,0:T(8,128)S(1)}, f32[4,8,8,128]{3,2,1,0:T(8,128)S(1)}, s32[4,8,3]{1,2,0:T(4,128)S(1)}, f32[64,8,128]{2,1,0:T(8,128)S(1)}, /*index=5*/s32[4,8]{1,0:T(4,128)S(1)}, s32[]{:T(128)}) while((s32[]{:T(128)}, f32[4,8,3,128]{3,1,2,0:T(8,128)S(1)}, f32[4,8,8,128]{3,2,1,0:T(8,128)S(1)}, ...), condition=%wide.region_9.10_spmd, body=%wide.region_5.9_spmd.sunk | while | flops 12980370 | bytes 1156605 | solution.py:81
  19.1 2.6 %multiply_reduce_fusion.17 = (f32[8,128]{1,0:T(8,128)S(1)}, f32[8,128]{1,0:T(8,128)S(1)}, f32[8,128]{1,0:T(8,128)S(1)}) fusion(f32[8,3]{1,0:T(8,128)S(1)} %copy.1157, f32[8,3,128]{2,1,0:T(4,128)S(1)} %copy.1159, f32[8,128]{1,0:T(8,128)S(1)} %get-tuple-element.1546, f32[8,3,128]{2,1,0:T(4,128)S(1)} %copy.1161, f32[8,128]{1,0:T(8,128)S(1)} %get-tuple-element.1550, ...), kind=kLoop, calls=%fused_computation.83.clone.1 | loop fusion | flops 12973056 | bytes 143456 | tf_op jit(solution)/shard_map/while/body/eval_jaxpr/vmap()/reduce_sum | solution.py:62
  22.9 2.6 %multiply_reduce_fusion.17 = (f32[8,128]{1,0:T(8,128)S(1)}, f32[8,128]{1,0:T(8,128)S(1)}, f32[8,128]{1,0:T(8,128)S(1)}) fusion(f32[8,3]{1,0:T(8,128)S(1)} %copy.1157, f32[8,3,128]{2,1,0:T(4,128)S(1)} %copy.1159, f32[8,128]{1,0:T(8,128)S(1)} %get-tuple-element.1546, f32[8,3,128]{2,1,0:T(4,128)S(1)} %copy.1161, f32[8,128]{1,0:T(8,128)S(1)} %get-tuple-element.1550, ...), kind=kLoop, calls=%fused_computation.83.clone.1 | loop fusion | flops 12973056 | bytes 143456 | tf_op jit(solution)/shard_map/while/body/eval_jaxpr/vmap()/reduce_sum | solution.py:62
  26.8 2.6 %multiply_reduce_fusion.17 = (f32[8,128]{1,0:T(8,128)S(1)}, f32[8,128]{1,0:T(8,128)S(1)}, f32[8,128]{1,0:T(8,128)S(1)}) fusion(f32[8,3]{1,0:T(8,128)S(1)} %copy.1157, f32[8,3,128]{2,1,0:T(4,128)S(1)} %copy.1159, f32[8,128]{1,0:T(8,128)S(1)} %get-tuple-element.1546, f32[8,3,128]{2,1,0:T(4,128)S(1)} %copy.1161, f32[8,128]{1,0:T(8,128)S(1)} %get-tuple-element.1550, ...), kind=kLoop, calls=%fused_computation.83.clone.1 | loop fusion | flops 12973056 | bytes 143456 | tf_op jit(solution)/shard_map/while/body/eval_jaxpr/vmap()/reduce_sum | solution.py:62
  30.6 2.6 %multiply_reduce_fusion.17 = (f32[8,128]{1,0:T(8,128)S(1)}, f32[8,128]{1,0:T(8,128)S(1)}, f32[8,128]{1,0:T(8,128)S(1)}) fusion(f32[8,3]{1,0:T(8,128)S(1)} %copy.1157, f32[8,3,128]{2,1,0:T(4,128)S(1)} %copy.1159, f32[8,128]{1,0:T(8,128)S(1)} %get-tuple-element.1546, f32[8,3,128]{2,1,0:T(4,128)S(1)} %copy.1161, f32[8,128]{1,0:T(8,128)S(1)} %get-tuple-element.1550, ...), kind=kLoop, calls=%fused_computation.83.clone.1 | loop fusion | flops 12973056 | bytes 143456 | tf_op jit(solution)/shard_map/while/body/eval_jaxpr/vmap()/reduce_sum | solution.py:62
  34.1 15.4 %while.93 = (s32[]{:T(128)}, f32[4,8,3,128]{3,1,2,0:T(8,128)S(1)}, f32[4,8,8,128]{3,2,1,0:T(8,128)S(1)}, s32[4,8,3]{1,2,0:T(4,128)S(1)}, f32[96,8,128]{2,1,0:T(8,128)S(1)}, /*index=5*/s32[4,8]{1,0:T(4,128)S(1)}, s32[]{:T(128)}) while((s32[]{:T(128)}, f32[4,8,3,128]{3,1,2,0:T(8,128)S(1)}, f32[4,8,8,128]{3,2,1,0:T(8,128)S(1)}, ...), condition=%wide.region_4.5_spmd, body=%wide.region_0.4_spmd.sunk | while | flops 12980370 | bytes 1156605 | solution.py:81
  35.3 2.6 %multiply_reduce_fusion.16 = (f32[8,128]{1,0:T(8,128)S(1)}, f32[8,128]{1,0:T(8,128)S(1)}, f32[8,128]{1,0:T(8,128)S(1)}) fusion(f32[8,3]{1,0:T(8,128)S(1)} %copy.1142, f32[8,3,128]{2,1,0:T(4,128)S(1)} %copy.1144, f32[8,128]{1,0:T(8,128)S(1)} %get-tuple-element.1511, f32[8,3,128]{2,1,0:T(4,128)S(1)} %copy.1146, f32[8,128]{1,0:T(8,128)S(1)} %get-tuple-element.1515, ...), kind=kLoop, calls=%fused_computation.35.clone.1 | loop fusion | flops 12973056 | bytes 143456 | tf_op jit(solution)/shard_map/while/body/eval_jaxpr/vmap()/reduce_sum | solution.py:62
  39.2 2.6 %multiply_reduce_fusion.16 = (f32[8,128]{1,0:T(8,128)S(1)}, f32[8,128]{1,0:T(8,128)S(1)}, f32[8,128]{1,0:T(8,128)S(1)}) fusion(f32[8,3]{1,0:T(8,128)S(1)} %copy.1142, f32[8,3,128]{2,1,0:T(4,128)S(1)} %copy.1144, f32[8,128]{1,0:T(8,128)S(1)} %get-tuple-element.1511, f32[8,3,128]{2,1,0:T(4,128)S(1)} %copy.1146, f32[8,128]{1,0:T(8,128)S(1)} %get-tuple-element.1515, ...), kind=kLoop, calls=%fused_computation.35.clone.1 | loop fusion | flops 12973056 | bytes 143456 | tf_op jit(solution)/shard_map/while/body/eval_jaxpr/vmap()/reduce_sum | solution.py:62
  43.0 2.6 %multiply_reduce_fusion.16 = (f32[8,128]{1,0:T(8,128)S(1)}, f32[8,128]{1,0:T(8,128)S(1)}, f32[8,128]{1,0:T(8,128)S(1)}) fusion(f32[8,3]{1,0:T(8,128)S(1)} %copy.1142, f32[8,3,128]{2,1,0:T(4,128)S(1)} %copy.1144, f32[8,128]{1,0:T(8,128)S(1)} %get-tuple-element.1511, f32[8,3,128]{2,1,0:T(4,128)S(1)} %copy.1146, f32[8,128]{1,0:T(8,128)S(1)} %get-tuple-element.1515, ...), kind=kLoop, calls=%fused_computation.35.clone.1 | loop fusion | flops 12973056 | bytes 143456 | tf_op jit(solution)/shard_map/while/body/eval_jaxpr/vmap()/reduce_sum | solution.py:62
  46.9 2.6 %multiply_reduce_fusion.16 = (f32[8,128]{1,0:T(8,128)S(1)}, f32[8,128]{1,0:T(8,128)S(1)}, f32[8,128]{1,0:T(8,128)S(1)}) fusion(f32[8,3]{1,0:T(8,128)S(1)} %copy.1142, f32[8,3,128]{2,1,0:T(4,128)S(1)} %copy.1144, f32[8,128]{1,0:T(8,128)S(1)} %get-tuple-element.1511, f32[8,3,128]{2,1,0:T(4,128)S(1)} %copy.1146, f32[8,128]{1,0:T(8,128)S(1)} %get-tuple-element.1515, ...), kind=kLoop, calls=%fused_computation.35.clone.1 | loop fusion | flops 12973056 | bytes 143456 | tf_op jit(solution)/shard_map/while/body/eval_jaxpr/vmap()/reduce_sum | solution.py:62
  50.6 1.9 collective-permute-start.2
  52.5 8.1 %collective-permute-start.3 = (f32[16,8,128]{2,1,0:T(8,128)S(1)}, f32[16,8,128]{2,1,0:T(8,128)S(1)}, u32[]{:S(2)}, u32[]{:S(2)}) collective-permute-start(f32[16,8,128]{2,1,0:T(8,128)S(1)} %get-tuple-element.962), channel_id=1, source_target_pairs={{1,0},{2,1},{3,2},{4,3},{5,4},{6,5},{7,6},{8,7},{9,8},{10,9},{11,1... | collective-permute-start | bytes 196616 | tf_op jit(solution)/shard_map/ppermute | solution.py:112
  60.6 15.4 %while.96 = (s32[]{:T(128)}, f32[4,8,3,128]{3,1,2,0:T(8,128)S(1)}, f32[4,8,8,128]{3,2,1,0:T(8,128)S(1)}, s32[4,8,3]{1,2,0:T(4,128)S(1)}, f32[64,8,128]{2,1,0:T(8,128)S(1)}, /*index=5*/s32[4,8]{1,0:T(4,128)S(1)}, s32[]{:T(128)}) while((s32[]{:T(128)}, f32[4,8,3,128]{3,1,2,0:T(8,128)S(1)}, f32[4,8,8,128]{3,2,1,0:T(8,128)S(1)}, ...), condition=%wide.region_19.20_spmd, body=%wide.region_15.19_spmd.sunk | while | flops 12980370 | bytes 1156605 | solution.py:81
  61.8 2.6 %multiply_reduce_fusion.19 = (f32[8,128]{1,0:T(8,128)S(1)}, f32[8,128]{1,0:T(8,128)S(1)}, f32[8,128]{1,0:T(8,128)S(1)}) fusion(f32[8,3]{1,0:T(8,128)S(1)} %copy.1187, f32[8,3,128]{2,1,0:T(4,128)S(1)} %copy.1189, f32[8,128]{1,0:T(8,128)S(1)} %get-tuple-element.1616, f32[8,3,128]{2,1,0:T(4,128)S(1)} %copy.1191, f32[8,128]{1,0:T(8,128)S(1)} %get-tuple-element.1620, ...), kind=kLoop, calls=%fused_computation.179.clone.1 | loop fusion | flops 12973056 | bytes 143456 | tf_op jit(solution)/shard_map/while/body/eval_jaxpr/vmap()/reduce_sum | solution.py:62
  65.7 2.6 %multiply_reduce_fusion.19 = (f32[8,128]{1,0:T(8,128)S(1)}, f32[8,128]{1,0:T(8,128)S(1)}, f32[8,128]{1,0:T(8,128)S(1)}) fusion(f32[8,3]{1,0:T(8,128)S(1)} %copy.1187, f32[8,3,128]{2,1,0:T(4,128)S(1)} %copy.1189, f32[8,128]{1,0:T(8,128)S(1)} %get-tuple-element.1616, f32[8,3,128]{2,1,0:T(4,128)S(1)} %copy.1191, f32[8,128]{1,0:T(8,128)S(1)} %get-tuple-element.1620, ...), kind=kLoop, calls=%fused_computation.179.clone.1 | loop fusion | flops 12973056 | bytes 143456 | tf_op jit(solution)/shard_map/while/body/eval_jaxpr/vmap()/reduce_sum | solution.py:62
  69.5 2.6 %multiply_reduce_fusion.19 = (f32[8,128]{1,0:T(8,128)S(1)}, f32[8,128]{1,0:T(8,128)S(1)}, f32[8,128]{1,0:T(8,128)S(1)}) fusion(f32[8,3]{1,0:T(8,128)S(1)} %copy.1187, f32[8,3,128]{2,1,0:T(4,128)S(1)} %copy.1189, f32[8,128]{1,0:T(8,128)S(1)} %get-tuple-element.1616, f32[8,3,128]{2,1,0:T(4,128)S(1)} %copy.1191, f32[8,128]{1,0:T(8,128)S(1)} %get-tuple-element.1620, ...), kind=kLoop, calls=%fused_computation.179.clone.1 | loop fusion | flops 12973056 | bytes 143456 | tf_op jit(solution)/shard_map/while/body/eval_jaxpr/vmap()/reduce_sum | solution.py:62
  73.4 2.6 %multiply_reduce_fusion.19 = (f32[8,128]{1,0:T(8,128)S(1)}, f32[8,128]{1,0:T(8,128)S(1)}, f32[8,128]{1,0:T(8,128)S(1)}) fusion(f32[8,3]{1,0:T(8,128)S(1)} %copy.1187, f32[8,3,128]{2,1,0:T(4,128)S(1)} %copy.1189, f32[8,128]{1,0:T(8,128)S(1)} %get-tuple-element.1616, f32[8,3,128]{2,1,0:T(4,128)S(1)} %copy.1191, f32[8,128]{1,0:T(8,128)S(1)} %get-tuple-element.1620, ...), kind=kLoop, calls=%fused_computation.179.clone.1 | loop fusion | flops 12973056 | bytes 143456 | tf_op jit(solution)/shard_map/while/body/eval_jaxpr/vmap()/reduce_sum | solution.py:62
  76.9 15.4 %while.95 = (s32[]{:T(128)}, f32[4,8,3,128]{3,1,2,0:T(8,128)S(1)}, f32[4,8,8,128]{3,2,1,0:T(8,128)S(1)}, s32[4,8,3]{1,2,0:T(4,128)S(1)}, f32[96,8,128]{2,1,0:T(8,128)S(1)}, /*index=5*/s32[4,8]{1,0:T(4,128)S(1)}, s32[]{:T(128)}) while((s32[]{:T(128)}, f32[4,8,3,128]{3,1,2,0:T(8,128)S(1)}, f32[4,8,8,128]{3,2,1,0:T(8,128)S(1)}, ...), condition=%wide.region_14.15_spmd, body=%wide.region_10.14_spmd.sunk | while | flops 12980370 | bytes 1156605 | solution.py:81
  78.0 2.6 %multiply_reduce_fusion.18 = (f32[8,128]{1,0:T(8,128)S(1)}, f32[8,128]{1,0:T(8,128)S(1)}, f32[8,128]{1,0:T(8,128)S(1)}) fusion(f32[8,3]{1,0:T(8,128)S(1)} %copy.1172, f32[8,3,128]{2,1,0:T(4,128)S(1)} %copy.1174, f32[8,128]{1,0:T(8,128)S(1)} %get-tuple-element.1581, f32[8,3,128]{2,1,0:T(4,128)S(1)} %copy.1176, f32[8,128]{1,0:T(8,128)S(1)} %get-tuple-element.1585, ...), kind=kLoop, calls=%fused_computation.131.clone.1 | loop fusion | flops 12973056 | bytes 143456 | tf_op jit(solution)/shard_map/while/body/eval_jaxpr/vmap()/reduce_sum | solution.py:62
  81.9 2.6 %multiply_reduce_fusion.18 = (f32[8,128]{1,0:T(8,128)S(1)}, f32[8,128]{1,0:T(8,128)S(1)}, f32[8,128]{1,0:T(8,128)S(1)}) fusion(f32[8,3]{1,0:T(8,128)S(1)} %copy.1172, f32[8,3,128]{2,1,0:T(4,128)S(1)} %copy.1174, f32[8,128]{1,0:T(8,128)S(1)} %get-tuple-element.1581, f32[8,3,128]{2,1,0:T(4,128)S(1)} %copy.1176, f32[8,128]{1,0:T(8,128)S(1)} %get-tuple-element.1585, ...), kind=kLoop, calls=%fused_computation.131.clone.1 | loop fusion | flops 12973056 | bytes 143456 | tf_op jit(solution)/shard_map/while/body/eval_jaxpr/vmap()/reduce_sum | solution.py:62
  85.7 2.6 %multiply_reduce_fusion.18 = (f32[8,128]{1,0:T(8,128)S(1)}, f32[8,128]{1,0:T(8,128)S(1)}, f32[8,128]{1,0:T(8,128)S(1)}) fusion(f32[8,3]{1,0:T(8,128)S(1)} %copy.1172, f32[8,3,128]{2,1,0:T(4,128)S(1)} %copy.1174, f32[8,128]{1,0:T(8,128)S(1)} %get-tuple-element.1581, f32[8,3,128]{2,1,0:T(4,128)S(1)} %copy.1176, f32[8,128]{1,0:T(8,128)S(1)} %get-tuple-element.1585, ...), kind=kLoop, calls=%fused_computation.131.clone.1 | loop fusion | flops 12973056 | bytes 143456 | tf_op jit(solution)/shard_map/while/body/eval_jaxpr/vmap()/reduce_sum | solution.py:62
  89.6 2.6 %multiply_reduce_fusion.18 = (f32[8,128]{1,0:T(8,128)S(1)}, f32[8,128]{1,0:T(8,128)S(1)}, f32[8,128]{1,0:T(8,128)S(1)}) fusion(f32[8,3]{1,0:T(8,128)S(1)} %copy.1172, f32[8,3,128]{2,1,0:T(4,128)S(1)} %copy.1174, f32[8,128]{1,0:T(8,128)S(1)} %get-tuple-element.1581, f32[8,3,128]{2,1,0:T(4,128)S(1)} %copy.1176, f32[8,128]{1,0:T(8,128)S(1)} %get-tuple-element.1585, ...), kind=kLoop, calls=%fused_computation.131.clone.1 | loop fusion | flops 12973056 | bytes 143456 | tf_op jit(solution)/shard_map/while/body/eval_jaxpr/vmap()/reduce_sum | solution.py:62
  93.2 1.9 collective-permute-start.4
  95.1 8.1 %collective-permute-start.5 = (f32[16,8,128]{2,1,0:T(8,128)S(1)}, f32[16,8,128]{2,1,0:T(8,128)S(1)}, u32[]{:S(2)}, u32[]{:S(2)}) collective-permute-start(f32[16,8,128]{2,1,0:T(8,128)S(1)} %get-tuple-element.960), channel_id=1, source_target_pairs={{1,0},{2,1},{3,2},{4,3},{5,4},{6,5},{7,6},{8,7},{9,8},{10,9},{11,1... | collective-permute-start | bytes 196616 | tf_op jit(solution)/shard_map/ppermute | solution.py:112
  103.3 15.4 %while.98 = (s32[]{:T(128)}, f32[4,8,3,128]{3,1,2,0:T(8,128)S(1)}, f32[4,8,8,128]{3,2,1,0:T(8,128)S(1)}, s32[4,8,3]{1,2,0:T(4,128)S(1)}, f32[64,8,128]{2,1,0:T(8,128)S(1)}, /*index=5*/s32[4,8]{1,0:T(4,128)S(1)}, s32[]{:T(128)}) while((s32[]{:T(128)}, f32[4,8,3,128]{3,1,2,0:T(8,128)S(1)}, f32[4,8,8,128]{3,2,1,0:T(8,128)S(1)}, ...), condition=%wide.region_29.30_spmd, body=%wide.region_25.29_spmd.sunk | while | flops 12980370 | bytes 1156605 | solution.py:81
  104.5 2.6 %multiply_reduce_fusion.21 = (f32[8,128]{1,0:T(8,128)S(1)}, f32[8,128]{1,0:T(8,128)S(1)}, f32[8,128]{1,0:T(8,128)S(1)}) fusion(f32[8,3]{1,0:T(8,128)S(1)} %copy.1217, f32[8,3,128]{2,1,0:T(4,128)S(1)} %copy.1219, f32[8,128]{1,0:T(8,128)S(1)} %get-tuple-element.1686, f32[8,3,128]{2,1,0:T(4,128)S(1)} %copy.1221, f32[8,128]{1,0:T(8,128)S(1)} %get-tuple-element.1690, ...), kind=kLoop, calls=%fused_computation.275.clone.1 | loop fusion | flops 12973056 | bytes 143456 | tf_op jit(solution)/shard_map/while/body/eval_jaxpr/vmap()/reduce_sum | solution.py:62
  108.3 2.6 %multiply_reduce_fusion.21 = (f32[8,128]{1,0:T(8,128)S(1)}, f32[8,128]{1,0:T(8,128)S(1)}, f32[8,128]{1,0:T(8,128)S(1)}) fusion(f32[8,3]{1,0:T(8,128)S(1)} %copy.1217, f32[8,3,128]{2,1,0:T(4,128)S(1)} %copy.1219, f32[8,128]{1,0:T(8,128)S(1)} %get-tuple-element.1686, f32[8,3,128]{2,1,0:T(4,128)S(1)} %copy.1221, f32[8,128]{1,0:T(8,128)S(1)} %get-tuple-element.1690, ...), kind=kLoop, calls=%fused_computation.275.clone.1 | loop fusion | flops 12973056 | bytes 143456 | tf_op jit(solution)/shard_map/while/body/eval_jaxpr/vmap()/reduce_sum | solution.py:62
  112.2 2.6 %multiply_reduce_fusion.21 = (f32[8,128]{1,0:T(8,128)S(1)}, f32[8,128]{1,0:T(8,128)S(1)}, f32[8,128]{1,0:T(8,128)S(1)}) fusion(f32[8,3]{1,0:T(8,128)S(1)} %copy.1217, f32[8,3,128]{2,1,0:T(4,128)S(1)} %copy.1219, f32[8,128]{1,0:T(8,128)S(1)} %get-tuple-element.1686, f32[8,3,128]{2,1,0:T(4,128)S(1)} %copy.1221, f32[8,128]{1,0:T(8,128)S(1)} %get-tuple-element.1690, ...), kind=kLoop, calls=%fused_computation.275.clone.1 | loop fusion | flops 12973056 | bytes 143456 | tf_op jit(solution)/shard_map/while/body/eval_jaxpr/vmap()/reduce_sum | solution.py:62
  116.0 2.6 %multiply_reduce_fusion.21 = (f32[8,128]{1,0:T(8,128)S(1)}, f32[8,128]{1,0:T(8,128)S(1)}, f32[8,128]{1,0:T(8,128)S(1)}) fusion(f32[8,3]{1,0:T(8,128)S(1)} %copy.1217, f32[8,3,128]{2,1,0:T(4,128)S(1)} %copy.1219, f32[8,128]{1,0:T(8,128)S(1)} %get-tuple-element.1686, f32[8,3,128]{2,1,0:T(4,128)S(1)} %copy.1221, f32[8,128]{1,0:T(8,128)S(1)} %get-tuple-element.1690, ...), kind=kLoop, calls=%fused_computation.275.clone.1 | loop fusion | flops 12973056 | bytes 143456 | tf_op jit(solution)/shard_map/while/body/eval_jaxpr/vmap()/reduce_sum | solution.py:62
  119.5 15.4 %while.97 = (s32[]{:T(128)}, f32[4,8,3,128]{3,1,2,0:T(8,128)S(1)}, f32[4,8,8,128]{3,2,1,0:T(8,128)S(1)}, s32[4,8,3]{1,2,0:T(4,128)S(1)}, f32[96,8,128]{2,1,0:T(8,128)S(1)}, /*index=5*/s32[4,8]{1,0:T(4,128)S(1)}, s32[]{:T(128)}) while((s32[]{:T(128)}, f32[4,8,3,128]{3,1,2,0:T(8,128)S(1)}, f32[4,8,8,128]{3,2,1,0:T(8,128)S(1)}, ...), condition=%wide.region_24.25_spmd, body=%wide.region_20.24_spmd.sunk | while | flops 12980370 | bytes 1156605 | solution.py:81
  120.7 2.6 %multiply_reduce_fusion.20 = (f32[8,128]{1,0:T(8,128)S(1)}, f32[8,128]{1,0:T(8,128)S(1)}, f32[8,128]{1,0:T(8,128)S(1)}) fusion(f32[8,3]{1,0:T(8,128)S(1)} %copy.1202, f32[8,3,128]{2,1,0:T(4,128)S(1)} %copy.1204, f32[8,128]{1,0:T(8,128)S(1)} %get-tuple-element.1651, f32[8,3,128]{2,1,0:T(4,128)S(1)} %copy.1206, f32[8,128]{1,0:T(8,128)S(1)} %get-tuple-element.1655, ...), kind=kLoop, calls=%fused_computation.227.clone.1 | loop fusion | flops 12973056 | bytes 143456 | tf_op jit(solution)/shard_map/while/body/eval_jaxpr/vmap()/reduce_sum | solution.py:62
  124.5 2.6 %multiply_reduce_fusion.20 = (f32[8,128]{1,0:T(8,128)S(1)}, f32[8,128]{1,0:T(8,128)S(1)}, f32[8,128]{1,0:T(8,128)S(1)}) fusion(f32[8,3]{1,0:T(8,128)S(1)} %copy.1202, f32[8,3,128]{2,1,0:T(4,128)S(1)} %copy.1204, f32[8,128]{1,0:T(8,128)S(1)} %get-tuple-element.1651, f32[8,3,128]{2,1,0:T(4,128)S(1)} %copy.1206, f32[8,128]{1,0:T(8,128)S(1)} %get-tuple-element.1655, ...), kind=kLoop, calls=%fused_computation.227.clone.1 | loop fusion | flops 12973056 | bytes 143456 | tf_op jit(solution)/shard_map/while/body/eval_jaxpr/vmap()/reduce_sum | solution.py:62
  128.4 2.6 %multiply_reduce_fusion.20 = (f32[8,128]{1,0:T(8,128)S(1)}, f32[8,128]{1,0:T(8,128)S(1)}, f32[8,128]{1,0:T(8,128)S(1)}) fusion(f32[8,3]{1,0:T(8,128)S(1)} %copy.1202, f32[8,3,128]{2,1,0:T(4,128)S(1)} %copy.1204, f32[8,128]{1,0:T(8,128)S(1)} %get-tuple-element.1651, f32[8,3,128]{2,1,0:T(4,128)S(1)} %copy.1206, f32[8,128]{1,0:T(8,128)S(1)} %get-tuple-element.1655, ...), kind=kLoop, calls=%fused_computation.227.clone.1 | loop fusion | flops 12973056 | bytes 143456 | tf_op jit(solution)/shard_map/while/body/eval_jaxpr/vmap()/reduce_sum | solution.py:62
  132.2 2.6 %multiply_reduce_fusion.20 = (f32[8,128]{1,0:T(8,128)S(1)}, f32[8,128]{1,0:T(8,128)S(1)}, f32[8,128]{1,0:T(8,128)S(1)}) fusion(f32[8,3]{1,0:T(8,128)S(1)} %copy.1202, f32[8,3,128]{2,1,0:T(4,128)S(1)} %copy.1204, f32[8,128]{1,0:T(8,128)S(1)} %get-tuple-element.1651, f32[8,3,128]{2,1,0:T(4,128)S(1)} %copy.1206, f32[8,128]{1,0:T(8,128)S(1)} %get-tuple-element.1655, ...), kind=kLoop, calls=%fused_computation.227.clone.1 | loop fusion | flops 12973056 | bytes 143456 | tf_op jit(solution)/shard_map/while/body/eval_jaxpr/vmap()/reduce_sum | solution.py:62
  135.8 1.9 collective-permute-start.6
  137.7 8.3 %collective-permute-start.7 = (f32[16,8,128]{2,1,0:T(8,128)S(1)}, f32[16,8,128]{2,1,0:T(8,128)S(1)}, u32[]{:S(2)}, u32[]{:S(2)}) collective-permute-start(f32[16,8,128]{2,1,0:T(8,128)S(1)} %get-tuple-element.958), channel_id=1, source_target_pairs={{1,0},{2,1},{3,2},{4,3},{5,4},{6,5},{7,6},{8,7},{9,8},{10,9},{11,1... | collective-permute-start | bytes 196616 | tf_op jit(solution)/shard_map/ppermute | solution.py:112
  146.0 15.4 %while.100 = (s32[]{:T(128)}, f32[4,8,3,128]{3,1,0,2:T(8,128)S(1)}, f32[4,8,8,128]{3,2,1,0:T(8,128)S(1)}, s32[4,8,3]{1,2,0:T(4,128)S(1)}, f32[64,8,128]{2,1,0:T(8,128)S(1)}, /*index=5*/s32[4,8]{1,0:T(4,128)S(1)}, s32[]{:T(128)}) while((s32[]{:T(128)}, f32[4,8,3,128]{3,1,0,2:T(8,128)S(1)}, f32[4,8,8,128]{3,2,1,0:T(8,128)S(1)}, ...), condition=%wide.region_39.40_spmd, body=%wide.region_35.39_spmd.sunk | while | flops 12980370 | bytes 1156605 | solution.py:81
  147.2 2.6 %multiply_reduce_fusion.23 = (f32[8,128]{1,0:T(8,128)S(1)}, f32[8,128]{1,0:T(8,128)S(1)}, f32[8,128]{1,0:T(8,128)S(1)}) fusion(f32[8,3]{1,0:T(8,128)S(1)} %copy.1247, f32[8,3,128]{2,1,0:T(4,128)S(1)} %copy.1249, f32[8,128]{1,0:T(8,128)S(1)} %get-tuple-element.1756, f32[8,3,128]{2,1,0:T(4,128)S(1)} %copy.1251, f32[8,128]{1,0:T(8,128)S(1)} %get-tuple-element.1760, ...), kind=kLoop, calls=%fused_computation.371.clone.1 | loop fusion | flops 12973056 | bytes 143456 | tf_op jit(solution)/shard_map/while/body/eval_jaxpr/vmap()/reduce_sum | solution.py:62
  151.1 2.6 %multiply_reduce_fusion.23 = (f32[8,128]{1,0:T(8,128)S(1)}, f32[8,128]{1,0:T(8,128)S(1)}, f32[8,128]{1,0:T(8,128)S(1)}) fusion(f32[8,3]{1,0:T(8,128)S(1)} %copy.1247, f32[8,3,128]{2,1,0:T(4,128)S(1)} %copy.1249, f32[8,128]{1,0:T(8,128)S(1)} %get-tuple-element.1756, f32[8,3,128]{2,1,0:T(4,128)S(1)} %copy.1251, f32[8,128]{1,0:T(8,128)S(1)} %get-tuple-element.1760, ...), kind=kLoop, calls=%fused_computation.371.clone.1 | loop fusion | flops 12973056 | bytes 143456 | tf_op jit(solution)/shard_map/while/body/eval_jaxpr/vmap()/reduce_sum | solution.py:62
  154.9 2.6 %multiply_reduce_fusion.23 = (f32[8,128]{1,0:T(8,128)S(1)}, f32[8,128]{1,0:T(8,128)S(1)}, f32[8,128]{1,0:T(8,128)S(1)}) fusion(f32[8,3]{1,0:T(8,128)S(1)} %copy.1247, f32[8,3,128]{2,1,0:T(4,128)S(1)} %copy.1249, f32[8,128]{1,0:T(8,128)S(1)} %get-tuple-element.1756, f32[8,3,128]{2,1,0:T(4,128)S(1)} %copy.1251, f32[8,128]{1,0:T(8,128)S(1)} %get-tuple-element.1760, ...), kind=kLoop, calls=%fused_computation.371.clone.1 | loop fusion | flops 12973056 | bytes 143456 | tf_op jit(solution)/shard_map/while/body/eval_jaxpr/vmap()/reduce_sum | solution.py:62
  158.8 2.6 %multiply_reduce_fusion.23 = (f32[8,128]{1,0:T(8,128)S(1)}, f32[8,128]{1,0:T(8,128)S(1)}, f32[8,128]{1,0:T(8,128)S(1)}) fusion(f32[8,3]{1,0:T(8,128)S(1)} %copy.1247, f32[8,3,128]{2,1,0:T(4,128)S(1)} %copy.1249, f32[8,128]{1,0:T(8,128)S(1)} %get-tuple-element.1756, f32[8,3,128]{2,1,0:T(4,128)S(1)} %copy.1251, f32[8,128]{1,0:T(8,128)S(1)} %get-tuple-element.1760, ...), kind=kLoop, calls=%fused_computation.371.clone.1 | loop fusion | flops 12973056 | bytes 143456 | tf_op jit(solution)/shard_map/while/body/eval_jaxpr/vmap()/reduce_sum | solution.py:62
  162.3 15.4 %while.99 = (s32[]{:T(128)}, f32[4,8,3,128]{3,1,2,0:T(8,128)S(1)}, f32[4,8,8,128]{3,2,1,0:T(8,128)S(1)}, s32[4,8,3]{1,2,0:T(4,128)S(1)}, f32[96,8,128]{2,1,0:T(8,128)S(1)}, /*index=5*/s32[4,8]{1,0:T(4,128)S(1)}, s32[]{:T(128)}) while((s32[]{:T(128)}, f32[4,8,3,128]{3,1,2,0:T(8,128)S(1)}, f32[4,8,8,128]{3,2,1,0:T(8,128)S(1)}, ...), condition=%wide.region_34.35_spmd, body=%wide.region_30.34_spmd.sunk | while | flops 12980370 | bytes 1156605 | solution.py:81
  163.5 2.6 %multiply_reduce_fusion.22 = (f32[8,128]{1,0:T(8,128)S(1)}, f32[8,128]{1,0:T(8,128)S(1)}, f32[8,128]{1,0:T(8,128)S(1)}) fusion(f32[8,3]{1,0:T(8,128)S(1)} %copy.1232, f32[8,3,128]{2,1,0:T(4,128)S(1)} %copy.1234, f32[8,128]{1,0:T(8,128)S(1)} %get-tuple-element.1721, f32[8,3,128]{2,1,0:T(4,128)S(1)} %copy.1236, f32[8,128]{1,0:T(8,128)S(1)} %get-tuple-element.1725, ...), kind=kLoop, calls=%fused_computation.323.clone.1 | loop fusion | flops 12973056 | bytes 143456 | tf_op jit(solution)/shard_map/while/body/eval_jaxpr/vmap()/reduce_sum | solution.py:62
  167.3 2.6 %multiply_reduce_fusion.22 = (f32[8,128]{1,0:T(8,128)S(1)}, f32[8,128]{1,0:T(8,128)S(1)}, f32[8,128]{1,0:T(8,128)S(1)}) fusion(f32[8,3]{1,0:T(8,128)S(1)} %copy.1232, f32[8,3,128]{2,1,0:T(4,128)S(1)} %copy.1234, f32[8,128]{1,0:T(8,128)S(1)} %get-tuple-element.1721, f32[8,3,128]{2,1,0:T(4,128)S(1)} %copy.1236, f32[8,128]{1,0:T(8,128)S(1)} %get-tuple-element.1725, ...), kind=kLoop, calls=%fused_computation.323.clone.1 | loop fusion | flops 12973056 | bytes 143456 | tf_op jit(solution)/shard_map/while/body/eval_jaxpr/vmap()/reduce_sum | solution.py:62
  171.2 2.6 %multiply_reduce_fusion.22 = (f32[8,128]{1,0:T(8,128)S(1)}, f32[8,128]{1,0:T(8,128)S(1)}, f32[8,128]{1,0:T(8,128)S(1)}) fusion(f32[8,3]{1,0:T(8,128)S(1)} %copy.1232, f32[8,3,128]{2,1,0:T(4,128)S(1)} %copy.1234, f32[8,128]{1,0:T(8,128)S(1)} %get-tuple-element.1721, f32[8,3,128]{2,1,0:T(4,128)S(1)} %copy.1236, f32[8,128]{1,0:T(8,128)S(1)} %get-tuple-element.1725, ...), kind=kLoop, calls=%fused_computation.323.clone.1 | loop fusion | flops 12973056 | bytes 143456 | tf_op jit(solution)/shard_map/while/body/eval_jaxpr/vmap()/reduce_sum | solution.py:62
  175.0 2.6 %multiply_reduce_fusion.22 = (f32[8,128]{1,0:T(8,128)S(1)}, f32[8,128]{1,0:T(8,128)S(1)}, f32[8,128]{1,0:T(8,128)S(1)}) fusion(f32[8,3]{1,0:T(8,128)S(1)} %copy.1232, f32[8,3,128]{2,1,0:T(4,128)S(1)} %copy.1234, f32[8,128]{1,0:T(8,128)S(1)} %get-tuple-element.1721, f32[8,3,128]{2,1,0:T(4,128)S(1)} %copy.1236, f32[8,128]{1,0:T(8,128)S(1)} %get-tuple-element.1725, ...), kind=kLoop, calls=%fused_computation.323.clone.1 | loop fusion | flops 12973056 | bytes 143456 | tf_op jit(solution)/shard_map/while/body/eval_jaxpr/vmap()/reduce_sum | solution.py:62
  178.5 16.1 %while.101 = (s32[]{:T(128)}, f32[3,1024]{1,0:T(4,128)S(1)}, f32[1024]{0:T(1024)S(1)}, f32[8,8,3,128]{3,2,1,0:T(4,128)S(1)}, s32[8,1024]{1,0:T(8,128)S(1)}, /*index=5*/s32[]{:T(128)}, s32[]{:T(128)}) while((s32[]{:T(128)}, f32[3,1024]{1,0:T(4,128)S(1)}, f32[1024]{0:T(1024)S(1)}, f32[8,8,3,128]{3,2,1,0:T(4,128)S(1)}, ...), condition=%wide.region_42.43_spmd.clone, body=%wide.region_40.42_spmd.clone.sunk | while | flops 41950208 | bytes 77920 | solution.py:140
  195.4 1.9 collective-permute-start.8
  198.6 2.7 %collective-permute-start.9 = (f32[8,1024]{1,0:T(8,128)S(1)}, f32[8,1024]{1,0:T(8,128)S(1)}, u32[]{:S(2)}, u32[]{:S(2)}) collective-permute-start(f32[8,1024]{1,0:T(8,128)S(1)} %fusion.161), channel_id=1, source_target_pairs={{0,64},{32,96},{64,0},{96,32},{128,192},{160,224},{192,128},{224,1... | collective-permute-start | bytes 98312 | tf_op jit(solution)/shard_map/ppermute | solution.py:39
  201.3 3.1 %collective-permute-done.9 = f32[8,1024]{1,0:T(8,128)S(1)} collective-permute-done((f32[8,1024]{1,0:T(8,128)S(1)}, f32[8,1024]{1,0:T(8,128)S(1)}, u32[]{:S(2)}, u32[]{:S(2)}) %collective-permute-start.9) | collective-permute-done | bytes 32800 | tf_op jit(solution)/shard_map/ppermute | solution.py:39
  204.4 3.3 %collective-permute-start.10 = (f32[8,1024]{1,0:T(8,128)S(1)}, f32[8,1024]{1,0:T(8,128)S(1)}, u32[]{:S(2)}, u32[]{:S(2)}) collective-permute-start(f32[8,1024]{1,0:T(8,128)S(1)} %add.603), channel_id=1, source_target_pairs={{0,128},{32,160},{64,192},{96,224},{128,0},{160,32},{192,64},{224,... | collective-permute-start | bytes 98312 | tf_op jit(solution)/shard_map/ppermute | solution.py:39
  207.7 4.0 %collective-permute-done.10 = f32[8,1024]{1,0:T(8,128)S(1)} collective-permute-done((f32[8,1024]{1,0:T(8,128)S(1)}, f32[8,1024]{1,0:T(8,128)S(1)}, u32[]{:S(2)}, u32[]{:S(2)}) %collective-permute-start.10) | collective-permute-done | bytes 32800 | tf_op jit(solution)/shard_map/ppermute | solution.py:39
  211.7 2.3 collective-permute-start.11
  214.1 3.4 %collective-permute-done.11 = f32[8,1024]{1,0:T(8,128)S(1)} collective-permute-done((f32[8,1024]{1,0:T(8,128)S(1)}, f32[8,1024]{1,0:T(8,128)S(1)}, u32[]{:S(2)}, u32[]{:S(2)}) %collective-permute-start.11) | collective-permute-done | bytes 32800 | tf_op jit(solution)/shard_map/ppermute | solution.py:39
  218.7 1.9 collective-permute-start.12
  220.6 3.6 %collective-permute-done.12 = f32[8,128]{1,0:T(8,128)S(1)} collective-permute-done((f32[8,128]{1,0:T(8,128)S(1)}, f32[8,128]{1,0:T(8,128)S(1)}, u32[]{:S(2)}, u32[]{:S(2)}) %collective-permute-start.12) | collective-permute-done | bytes 4128 | tf_op jit(solution)/shard_map/ppermute | solution.py:39
  224.8 1.9 collective-permute-start.13
  227.4 3.8 %collective-permute-done.13 = f32[8,128]{1,0:T(8,128)S(1)} collective-permute-done((f32[8,128]{1,0:T(8,128)S(1)}, f32[8,128]{1,0:T(8,128)S(1)}, u32[]{:S(2)}, u32[]{:S(2)}) %collective-permute-start.13) | collective-permute-done | bytes 4128 | tf_op jit(solution)/shard_map/ppermute | solution.py:39
  231.9 1.9 collective-permute-start.14
  234.0 7.3 %collective-permute-done.14 = f32[8,128]{1,0:T(8,128)S(1)} collective-permute-done((f32[8,128]{1,0:T(8,128)S(1)}, f32[8,128]{1,0:T(8,128)S(1)}, u32[]{:S(2)}, u32[]{:S(2)}) %collective-permute-start.14) | collective-permute-done | bytes 4128 | tf_op jit(solution)/shard_map/ppermute | solution.py:39
  244.0 3.7 %collective-permute-done.15 = f32[8,128]{1,0:T(8,128)S(1)} collective-permute-done((f32[8,128]{1,0:T(8,128)S(1)}, f32[8,128]{1,0:T(8,128)S(1)}, u32[]{:S(2)}, u32[]{:S(2)}) %collective-permute-start.15) | collective-permute-done | bytes 4128 | tf_op jit(solution)/shard_map/ppermute | solution.py:39
  250.2 6.9 %collective-permute-done.16 = f32[8,128]{1,0:T(8,128)S(1)} collective-permute-done((f32[8,128]{1,0:T(8,128)S(1)}, f32[8,128]{1,0:T(8,128)S(1)}, u32[]{:S(2)}, u32[]{:S(2)}) %collective-permute-start.16) | collective-permute-done | bytes 4128 | tf_op jit(solution)/shard_map/ppermute | solution.py:39
  (963 shorter events, 69.6 us)
Async XLA Ops:
  0.6 1.8 copy-start.1
  0.6 1.9 copy-start
  2.6 13.7 %copy-start.4 = (s32[1,64,3]{1,0,2:T(1,128)S(1)}, s32[1,64,3]{1,0,2:T(1,128)}, u32[]{:S(2)}) copy-start(s32[1,64,3]{1,0,2:T(1,128)} %param.30) | copy-start | bytes 2308
  2.7 30.6 %collective-permute-start = (f32[16,8,128]{2,1,0:T(8,128)S(1)}, f32[16,8,128]{2,1,0:T(8,128)S(1)}, u32[]{:S(2)}, u32[]{:S(2)}) collective-permute-start(f32[16,8,128]{2,1,0:T(8,128)S(1)} %get-tuple-element.963), channel_id=1, source_target_pairs={{0,1},{1,2},{2,3},{3,4},{4,5},{5,6},{6,7},{7,8},{8,9},{9,10},{10,1... | collective-permute-start | bytes 196616 | tf_op jit(solution)/shard_map/ppermute | solution.py:111
  7.0 26.3 %collective-permute-start.1 = (f32[16,8,128]{2,1,0:T(8,128)S(1)}, f32[16,8,128]{2,1,0:T(8,128)S(1)}, u32[]{:S(2)}, u32[]{:S(2)}) collective-permute-start(f32[16,8,128]{2,1,0:T(8,128)S(1)} %get-tuple-element.964), channel_id=1, source_target_pairs={{1,0},{2,1},{3,2},{4,3},{5,4},{6,5},{7,6},{8,7},{9,8},{10,9},{11,1... | collective-permute-start | bytes 196616 | tf_op jit(solution)/shard_map/ppermute | solution.py:112
  17.9 15.5 %copy-start.3 = (s32[1,64,128]{2,1,0:T(8,128)S(1)}, s32[1,64,128]{2,1,0:T(8,128)}, u32[]{:S(2)}) copy-start(s32[1,64,128]{2,1,0:T(8,128)} %param.31) | copy-start | bytes 98308
  34.1 15.5 %copy-start.2 = (f32[1,64,3,128]{3,1,2,0:T(8,128)S(1)}, f32[1,64,3,128]{3,1,2,0:T(8,128)}, u32[]{:S(2)}) copy-start(f32[1,64,3,128]{3,1,2,0:T(8,128)} %param.27) | copy-start | bytes 294916
  50.6 25.5 %collective-permute-start.2 = (f32[16,8,128]{2,1,0:T(8,128)S(1)}, f32[16,8,128]{2,1,0:T(8,128)S(1)}, u32[]{:S(2)}, u32[]{:S(2)}) collective-permute-start(f32[16,8,128]{2,1,0:T(8,128)S(1)} %get-tuple-element.961), channel_id=1, source_target_pairs={{0,1},{1,2},{2,3},{3,4},{4,5},{5,6},{6,7},{7,8},{8,9},{9,10},{10,1... | collective-permute-start | bytes 196616 | tf_op jit(solution)/shard_map/ppermute | solution.py:111
  52.5 23.6 %collective-permute-start.3 = (f32[16,8,128]{2,1,0:T(8,128)S(1)}, f32[16,8,128]{2,1,0:T(8,128)S(1)}, u32[]{:S(2)}, u32[]{:S(2)}) collective-permute-start(f32[16,8,128]{2,1,0:T(8,128)S(1)} %get-tuple-element.962), channel_id=1, source_target_pairs={{1,0},{2,1},{3,2},{4,3},{5,4},{6,5},{7,6},{8,7},{9,8},{10,9},{11,1... | collective-permute-start | bytes 196616 | tf_op jit(solution)/shard_map/ppermute | solution.py:112
  93.2 25.5 %collective-permute-start.4 = (f32[16,8,128]{2,1,0:T(8,128)S(1)}, f32[16,8,128]{2,1,0:T(8,128)S(1)}, u32[]{:S(2)}, u32[]{:S(2)}) collective-permute-start(f32[16,8,128]{2,1,0:T(8,128)S(1)} %get-tuple-element.959), channel_id=1, source_target_pairs={{0,1},{1,2},{2,3},{3,4},{4,5},{5,6},{6,7},{7,8},{8,9},{9,10},{10,1... | collective-permute-start | bytes 196616 | tf_op jit(solution)/shard_map/ppermute | solution.py:111
  95.1 23.6 %collective-permute-start.5 = (f32[16,8,128]{2,1,0:T(8,128)S(1)}, f32[16,8,128]{2,1,0:T(8,128)S(1)}, u32[]{:S(2)}, u32[]{:S(2)}) collective-permute-start(f32[16,8,128]{2,1,0:T(8,128)S(1)} %get-tuple-element.960), channel_id=1, source_target_pairs={{1,0},{2,1},{3,2},{4,3},{5,4},{6,5},{7,6},{8,7},{9,8},{10,9},{11,1... | collective-permute-start | bytes 196616 | tf_op jit(solution)/shard_map/ppermute | solution.py:112
  135.8 25.7 %collective-permute-start.6 = (f32[16,8,128]{2,1,0:T(8,128)S(1)}, f32[16,8,128]{2,1,0:T(8,128)S(1)}, u32[]{:S(2)}, u32[]{:S(2)}) collective-permute-start(f32[16,8,128]{2,1,0:T(8,128)S(1)} %get-tuple-element.957), channel_id=1, source_target_pairs={{0,1},{1,2},{2,3},{3,4},{4,5},{5,6},{6,7},{7,8},{8,9},{9,10},{10,1... | collective-permute-start | bytes 196616 | tf_op jit(solution)/shard_map/ppermute | solution.py:111
  137.7 23.8 %collective-permute-start.7 = (f32[16,8,128]{2,1,0:T(8,128)S(1)}, f32[16,8,128]{2,1,0:T(8,128)S(1)}, u32[]{:S(2)}, u32[]{:S(2)}) collective-permute-start(f32[16,8,128]{2,1,0:T(8,128)S(1)} %get-tuple-element.958), channel_id=1, source_target_pairs={{1,0},{2,1},{3,2},{4,3},{5,4},{6,5},{7,6},{8,7},{9,8},{10,9},{11,1... | collective-permute-start | bytes 196616 | tf_op jit(solution)/shard_map/ppermute | solution.py:112
  195.4 3.1 %collective-permute-start.8 = (f32[8,1024]{1,0:T(8,128)S(1)}, f32[8,1024]{1,0:T(8,128)S(1)}, u32[]{:S(2)}, u32[]{:S(2)}) collective-permute-start(f32[8,1024]{1,0:T(8,128)S(1)} %maximum_maximum_fusion), channel_id=1, source_target_pairs={{0,32},{32,0},{64,96},{96,64},{128,160},{160,128},{192,224},{224,1... | collective-permute-start | bytes 98312 | tf_op jit(solution)/shard_map/ppermute | solution.py:39
  198.6 5.8 %collective-permute-start.9 = (f32[8,1024]{1,0:T(8,128)S(1)}, f32[8,1024]{1,0:T(8,128)S(1)}, u32[]{:S(2)}, u32[]{:S(2)}) collective-permute-start(f32[8,1024]{1,0:T(8,128)S(1)} %fusion.161), channel_id=1, source_target_pairs={{0,64},{32,96},{64,0},{96,32},{128,192},{160,224},{192,128},{224,1... | collective-permute-start | bytes 98312 | tf_op jit(solution)/shard_map/ppermute | solution.py:39
  204.4 7.3 %collective-permute-start.10 = (f32[8,1024]{1,0:T(8,128)S(1)}, f32[8,1024]{1,0:T(8,128)S(1)}, u32[]{:S(2)}, u32[]{:S(2)}) collective-permute-start(f32[8,1024]{1,0:T(8,128)S(1)} %add.603), channel_id=1, source_target_pairs={{0,128},{32,160},{64,192},{96,224},{128,0},{160,32},{192,64},{224,... | collective-permute-start | bytes 98312 | tf_op jit(solution)/shard_map/ppermute | solution.py:39
  211.7 5.8 %collective-permute-start.11 = (f32[8,1024]{1,0:T(8,128)S(1)}, f32[8,1024]{1,0:T(8,128)S(1)}, u32[]{:S(2)}, u32[]{:S(2)}) collective-permute-start(f32[8,1024]{1,0:T(8,128)S(1)} %add.604), channel_id=1, source_target_pairs={{0,256},{32,288},{64,320},{96,352},{128,384},{160,416},{192,448},{... | collective-permute-start | bytes 98312 | tf_op jit(solution)/shard_map/ppermute | solution.py:39
  218.7 5.5 %collective-permute-start.12 = (f32[8,128]{1,0:T(8,128)S(1)}, f32[8,128]{1,0:T(8,128)S(1)}, u32[]{:S(2)}, u32[]{:S(2)}) collective-permute-start(f32[8,128]{1,0:T(8,128)S(1)} %broadcast_in_dim.115), channel_id=1, source_target_pairs={{0,1},{1,0},{2,3},{3,2},{4,5},{5,4},{6,7},{7,6},{8,9},{9,8},{10,11... | collective-permute-start | bytes 12296 | tf_op jit(solution)/shard_map/ppermute | solution.py:39
  224.8 6.4 %collective-permute-start.13 = (f32[8,128]{1,0:T(8,128)S(1)}, f32[8,128]{1,0:T(8,128)S(1)}, u32[]{:S(2)}, u32[]{:S(2)}) collective-permute-start(f32[8,128]{1,0:T(8,128)S(1)} %broadcast_add_fusion), channel_id=1, source_target_pairs={{0,2},{1,3},{2,0},{3,1},{4,6},{5,7},{6,4},{7,5},{8,10},{9,11},{10,... | collective-permute-start | bytes 12296 | tf_op jit(solution)/shard_map/ppermute | solution.py:39
  231.9 9.4 %collective-permute-start.14 = (f32[8,128]{1,0:T(8,128)S(1)}, f32[8,128]{1,0:T(8,128)S(1)}, u32[]{:S(2)}, u32[]{:S(2)}) collective-permute-start(f32[8,128]{1,0:T(8,128)S(1)} %fusion.190), channel_id=1, source_target_pairs={{0,4},{1,5},{2,6},{3,7},{4,0},{5,1},{6,2},{7,3},{8,12},{9,13},{10,... | collective-permute-start | bytes 12296 | tf_op jit(solution)/shard_map/ppermute | solution.py:39
  241.3 6.4 %collective-permute-start.15 = (f32[8,128]{1,0:T(8,128)S(1)}, f32[8,128]{1,0:T(8,128)S(1)}, u32[]{:S(2)}, u32[]{:S(2)}) collective-permute-start(f32[8,128]{1,0:T(8,128)S(1)} %add.608), channel_id=1, source_target_pairs={{0,8},{1,9},{2,10},{3,11},{4,12},{5,13},{6,14},{7,15},{8,0},{9,1},... | collective-permute-start | bytes 12296 | tf_op jit(solution)/shard_map/ppermute | solution.py:39
  243.2 15.1 %copy-start.5 = (f32[1,3,128]{2,0,1:T(1,128)S(1)}, f32[1,3,128]{2,0,1:T(1,128)}, u32[]{:S(2)}) copy-start(f32[1,3,128]{2,0,1:T(1,128)} %param.32) | copy-start | bytes 4612
  247.7 9.4 %collective-permute-start.16 = (f32[8,128]{1,0:T(8,128)S(1)}, f32[8,128]{1,0:T(8,128)S(1)}, u32[]{:S(2)}, u32[]{:S(2)}) collective-permute-start(f32[8,128]{1,0:T(8,128)S(1)} %add.609), channel_id=1, source_target_pairs={{0,16},{1,17},{2,18},{3,19},{4,20},{5,21},{6,22},{7,23},{8,24},{9,... | collective-permute-start | bytes 12296 | tf_op jit(solution)/shard_map/ppermute | solution.py:39

commit v5 on v4

--- a/solution.py
+++ b/solution.py
@@ -136,16 +136,25 @@
         counts = counts + jnp.sum(table, axis=0)
         return ((momentum, counts), None)
 
+    local_flux = jnp.sum(speed[:, 0, :])
+    slab_flux = butterfly_sum(jnp.full((8, 128), local_flux, jnp.float32), "space")
     start = (jnp.zeros((3, BINS_DEV), jnp.float32), jnp.zeros((BINS_DEV,), jnp.float32))
-    (momentum, counts), unused = lax.scan(accumulate, start, (grouped_speed, grouped_bins))
-    local_flux = jnp.sum(speed[:, 0, :])
+    chunks = 4
+    steps = tiles // group // chunks
+    momentum, counts = start
+    for chunk in range(chunks):
+        piece = slice(chunk * steps, (chunk + 1) * steps)
+        (part_momentum, part_counts), unused = lax.scan(
+            accumulate, start, (grouped_speed[piece], grouped_bins[piece])
+        )
+        momentum = momentum + part_momentum
+        counts = counts + part_counts
     packed = jnp.concatenate(
-        [momentum, counts[None, :], jnp.full((4, BINS_DEV), local_flux, jnp.float32)], axis=0
+        [momentum, counts[None, :], jnp.full((4, BINS_DEV), slab_flux[0, 0], jnp.float32)], axis=0
     )
     packed = butterfly_sum(packed, "rep")
     momentum, counts = packed[0:3], packed[3]
-    slab_flux = jnp.full((8, 128), packed[4, 0], jnp.float32)
-    flux_sum = butterfly_sum(slab_flux, "space")[0, 0]
+    flux_sum = packed[4, 0]
     bin_velocity = momentum / counts[None, :]
     total_beads = lax.axis_size("rep") * lax.axis_size("space") * tiles * width
     inflow = 2.0 * TARGET_FLOW - flux_sum / total_beads

time: 260 us -> 249 us (0.958)
  waiting for transfers between devices: 37 us -> 26 us
    ppermute x9, waiting for transfers between devices: 37 us -> 25.9 us  [butterfly_sum(): leaves.append(lax.ppermute(value, axis, pairs))]
  transfers between devices with their start and end apart: 17 -> 17, of which waited for: 9 -> 8; matrix products, arithmetic and copies ran while one was open for 24% -> 31% of each run, Pallas kernels for 0% -> 0%
where the time goes in v5:
time: 249 us; the launch traced here: 248 us
  other arithmetic  95.4 us (38%)
  starting transfers between devices  63.8 us (26%)
  local copies, waits for them, and re-layouts  41.8 us (17%)
  waiting for transfers between devices  26 us (10%)
  matrix products  11.7 us (5%)
  loops' own time  6.36 us (3%)
  between operations  2.96 us (1%)
    reduce_sum x32, other arithmetic, bead_forces(): jnp.sum(factor * offset_x, axis=(0, 2))  84.4 us
    ppermute x4, starting transfers between devices, shards(): after = lax.ppermute(packed[:HALO], 'space', down)  33.7 us
    ppermute x9, waiting for transfers between devices, butterfly_sum(): leaves.append(lax.ppermute(value, axis, pairs))  25.9 us
    ppermute x9, starting transfers between devices, butterfly_sum(): leaves.append(lax.ppermute(value, axis, pairs))  20 us
    gather x32, local copies, waits for them, and re-layouts, per_group(): partners = source[link_group]  18.5 us
    dot_general x8, matrix products, accumulate(): jnp.dot(rows_now, table, precision=lax.Precision.HIGHEST, preferred_eleme...  11.7 us
    ppermute x4, starting transfers between devices, shards(): before = lax.ppermute(packed[tiles - HALO:], 'space', up)  10 us
    another operation x8, loops' own time, tile_forces(): lax.map(per_group, (own_tiles.reshape(tiles // group, group, 8, width), l...  6.02 us
  transfers between devices with their start and end apart: 17, of which 8 were waited for; matrix products, arithmetic and copies ran while one was open for 31% of the time, Pallas kernels for 0%

profile of v5, /device:TPU:46, one launch (start us, length us, event | category | flops | bytes accessed | tf_op | source)
XLA Modules:
  0.0 248.0 jit_solution(7257707094485350079)
XLA Ops:
  2.7 4.3 %collective-permute-start = (f32[16,8,128]{2,1,0:T(8,128)S(1)}, f32[16,8,128]{2,1,0:T(8,128)S(1)}, u32[]{:S(2)}, u32[]{:S(2)}) collective-permute-start(f32[16,8,128]{2,1,0:T(8,128)S(1)} %get-tuple-element.1178), channel_id=1, source_target_pairs={{0,1},{1,2},{2,3},{3,4},{4,5},{5,6},{6,7},{7,8},{8,9},{9,10},{10,1... | collective-permute-start | bytes 196616 | tf_op jit(solution)/shard_map/ppermute | solution.py:111
  7.0 9.3 %collective-permute-start.1 = (f32[16,8,128]{2,1,0:T(8,128)S(1)}, f32[16,8,128]{2,1,0:T(8,128)S(1)}, u32[]{:S(2)}, u32[]{:S(2)}) collective-permute-start(f32[16,8,128]{2,1,0:T(8,128)S(1)} %get-tuple-element.1179), channel_id=1, source_target_pairs={{1,0},{2,1},{3,2},{4,3},{5,4},{6,5},{7,6},{8,7},{9,8},{10,9},{11,1... | collective-permute-start | bytes 196616 | tf_op jit(solution)/shard_map/ppermute | solution.py:112
  17.9 15.4 %while.133 = (s32[]{:T(128)}, f32[4,8,3,128]{3,1,2,0:T(8,128)S(1)}, f32[4,8,8,128]{3,2,1,0:T(8,128)S(1)}, s32[4,8,3]{1,2,0:T(4,128)S(1)}, f32[64,8,128]{2,1,0:T(8,128)S(1)}, /*index=5*/s32[4,8]{1,0:T(4,128)S(1)}, s32[]{:T(128)}) while((s32[]{:T(128)}, f32[4,8,3,128]{3,1,2,0:T(8,128)S(1)}, f32[4,8,8,128]{3,2,1,0:T(8,128)S(1)}, ...), condition=%wide.region_9.10_spmd, body=%wide.region_5.9_spmd.sunk | while | flops 12980370 | bytes 1156605 | solution.py:81
  19.1 2.6 %multiply_reduce_fusion.17 = (f32[8,128]{1,0:T(8,128)S(1)}, f32[8,128]{1,0:T(8,128)S(1)}, f32[8,128]{1,0:T(8,128)S(1)}) fusion(f32[8,3]{1,0:T(8,128)S(1)} %copy.1148, f32[8,3,128]{2,1,0:T(4,128)S(1)} %copy.1150, f32[8,128]{1,0:T(8,128)S(1)} %get-tuple-element.1844, f32[8,3,128]{2,1,0:T(4,128)S(1)} %copy.1152, f32[8,128]{1,0:T(8,128)S(1)} %get-tuple-element.1848, ...), kind=kLoop, calls=%fused_computation.86.clone.1 | loop fusion | flops 12973056 | bytes 143456 | tf_op jit(solution)/shard_map/while/body/eval_jaxpr/vmap()/reduce_sum | solution.py:62
  23.0 2.6 %multiply_reduce_fusion.17 = (f32[8,128]{1,0:T(8,128)S(1)}, f32[8,128]{1,0:T(8,128)S(1)}, f32[8,128]{1,0:T(8,128)S(1)}) fusion(f32[8,3]{1,0:T(8,128)S(1)} %copy.1148, f32[8,3,128]{2,1,0:T(4,128)S(1)} %copy.1150, f32[8,128]{1,0:T(8,128)S(1)} %get-tuple-element.1844, f32[8,3,128]{2,1,0:T(4,128)S(1)} %copy.1152, f32[8,128]{1,0:T(8,128)S(1)} %get-tuple-element.1848, ...), kind=kLoop, calls=%fused_computation.86.clone.1 | loop fusion | flops 12973056 | bytes 143456 | tf_op jit(solution)/shard_map/while/body/eval_jaxpr/vmap()/reduce_sum | solution.py:62
  26.8 2.6 %multiply_reduce_fusion.17 = (f32[8,128]{1,0:T(8,128)S(1)}, f32[8,128]{1,0:T(8,128)S(1)}, f32[8,128]{1,0:T(8,128)S(1)}) fusion(f32[8,3]{1,0:T(8,128)S(1)} %copy.1148, f32[8,3,128]{2,1,0:T(4,128)S(1)} %copy.1150, f32[8,128]{1,0:T(8,128)S(1)} %get-tuple-element.1844, f32[8,3,128]{2,1,0:T(4,128)S(1)} %copy.1152, f32[8,128]{1,0:T(8,128)S(1)} %get-tuple-element.1848, ...), kind=kLoop, calls=%fused_computation.86.clone.1 | loop fusion | flops 12973056 | bytes 143456 | tf_op jit(solution)/shard_map/while/body/eval_jaxpr/vmap()/reduce_sum | solution.py:62
  30.7 2.6 %multiply_reduce_fusion.17 = (f32[8,128]{1,0:T(8,128)S(1)}, f32[8,128]{1,0:T(8,128)S(1)}, f32[8,128]{1,0:T(8,128)S(1)}) fusion(f32[8,3]{1,0:T(8,128)S(1)} %copy.1148, f32[8,3,128]{2,1,0:T(4,128)S(1)} %copy.1150, f32[8,128]{1,0:T(8,128)S(1)} %get-tuple-element.1844, f32[8,3,128]{2,1,0:T(4,128)S(1)} %copy.1152, f32[8,128]{1,0:T(8,128)S(1)} %get-tuple-element.1848, ...), kind=kLoop, calls=%fused_computation.86.clone.1 | loop fusion | flops 12973056 | bytes 143456 | tf_op jit(solution)/shard_map/while/body/eval_jaxpr/vmap()/reduce_sum | solution.py:62
  34.2 15.4 %while.132 = (s32[]{:T(128)}, f32[4,8,3,128]{3,1,2,0:T(8,128)S(1)}, f32[4,8,8,128]{3,2,1,0:T(8,128)S(1)}, s32[4,8,3]{1,2,0:T(4,128)S(1)}, f32[96,8,128]{2,1,0:T(8,128)S(1)}, /*index=5*/s32[4,8]{1,0:T(4,128)S(1)}, s32[]{:T(128)}) while((s32[]{:T(128)}, f32[4,8,3,128]{3,1,2,0:T(8,128)S(1)}, f32[4,8,8,128]{3,2,1,0:T(8,128)S(1)}, ...), condition=%wide.region_4.5_spmd, body=%wide.region_0.4_spmd.sunk | while | flops 12980370 | bytes 1156605 | solution.py:81
  35.4 2.6 %multiply_reduce_fusion.16 = (f32[8,128]{1,0:T(8,128)S(1)}, f32[8,128]{1,0:T(8,128)S(1)}, f32[8,128]{1,0:T(8,128)S(1)}) fusion(f32[8,3]{1,0:T(8,128)S(1)} %copy.1133, f32[8,3,128]{2,1,0:T(4,128)S(1)} %copy.1135, f32[8,128]{1,0:T(8,128)S(1)} %get-tuple-element.1809, f32[8,3,128]{2,1,0:T(4,128)S(1)} %copy.1137, f32[8,128]{1,0:T(8,128)S(1)} %get-tuple-element.1813, ...), kind=kLoop, calls=%fused_computation.38.clone.1 | loop fusion | flops 12973056 | bytes 143456 | tf_op jit(solution)/shard_map/while/body/eval_jaxpr/vmap()/reduce_sum | solution.py:62
  39.3 2.6 %multiply_reduce_fusion.16 = (f32[8,128]{1,0:T(8,128)S(1)}, f32[8,128]{1,0:T(8,128)S(1)}, f32[8,128]{1,0:T(8,128)S(1)}) fusion(f32[8,3]{1,0:T(8,128)S(1)} %copy.1133, f32[8,3,128]{2,1,0:T(4,128)S(1)} %copy.1135, f32[8,128]{1,0:T(8,128)S(1)} %get-tuple-element.1809, f32[8,3,128]{2,1,0:T(4,128)S(1)} %copy.1137, f32[8,128]{1,0:T(8,128)S(1)} %get-tuple-element.1813, ...), kind=kLoop, calls=%fused_computation.38.clone.1 | loop fusion | flops 12973056 | bytes 143456 | tf_op jit(solution)/shard_map/while/body/eval_jaxpr/vmap()/reduce_sum | solution.py:62
  43.1 2.6 %multiply_reduce_fusion.16 = (f32[8,128]{1,0:T(8,128)S(1)}, f32[8,128]{1,0:T(8,128)S(1)}, f32[8,128]{1,0:T(8,128)S(1)}) fusion(f32[8,3]{1,0:T(8,128)S(1)} %copy.1133, f32[8,3,128]{2,1,0:T(4,128)S(1)} %copy.1135, f32[8,128]{1,0:T(8,128)S(1)} %get-tuple-element.1809, f32[8,3,128]{2,1,0:T(4,128)S(1)} %copy.1137, f32[8,128]{1,0:T(8,128)S(1)} %get-tuple-element.1813, ...), kind=kLoop, calls=%fused_computation.38.clone.1 | loop fusion | flops 12973056 | bytes 143456 | tf_op jit(solution)/shard_map/while/body/eval_jaxpr/vmap()/reduce_sum | solution.py:62
  47.0 2.6 %multiply_reduce_fusion.16 = (f32[8,128]{1,0:T(8,128)S(1)}, f32[8,128]{1,0:T(8,128)S(1)}, f32[8,128]{1,0:T(8,128)S(1)}) fusion(f32[8,3]{1,0:T(8,128)S(1)} %copy.1133, f32[8,3,128]{2,1,0:T(4,128)S(1)} %copy.1135, f32[8,128]{1,0:T(8,128)S(1)} %get-tuple-element.1809, f32[8,3,128]{2,1,0:T(4,128)S(1)} %copy.1137, f32[8,128]{1,0:T(8,128)S(1)} %get-tuple-element.1813, ...), kind=kLoop, calls=%fused_computation.38.clone.1 | loop fusion | flops 12973056 | bytes 143456 | tf_op jit(solution)/shard_map/while/body/eval_jaxpr/vmap()/reduce_sum | solution.py:62
  50.7 1.9 collective-permute-start.2
  52.6 8.1 %collective-permute-start.3 = (f32[16,8,128]{2,1,0:T(8,128)S(1)}, f32[16,8,128]{2,1,0:T(8,128)S(1)}, u32[]{:S(2)}, u32[]{:S(2)}) collective-permute-start(f32[16,8,128]{2,1,0:T(8,128)S(1)} %get-tuple-element.1177), channel_id=1, source_target_pairs={{1,0},{2,1},{3,2},{4,3},{5,4},{6,5},{7,6},{8,7},{9,8},{10,9},{11,1... | collective-permute-start | bytes 196616 | tf_op jit(solution)/shard_map/ppermute | solution.py:112
  60.7 15.4 %while.135 = (s32[]{:T(128)}, f32[4,8,3,128]{3,1,2,0:T(8,128)S(1)}, f32[4,8,8,128]{3,2,1,0:T(8,128)S(1)}, s32[4,8,3]{1,2,0:T(4,128)S(1)}, f32[64,8,128]{2,1,0:T(8,128)S(1)}, /*index=5*/s32[4,8]{1,0:T(4,128)S(1)}, s32[]{:T(128)}) while((s32[]{:T(128)}, f32[4,8,3,128]{3,1,2,0:T(8,128)S(1)}, f32[4,8,8,128]{3,2,1,0:T(8,128)S(1)}, ...), condition=%wide.region_19.20_spmd, body=%wide.region_15.19_spmd.sunk | while | flops 12980370 | bytes 1156605 | solution.py:81
  61.9 2.6 %multiply_reduce_fusion.19 = (f32[8,128]{1,0:T(8,128)S(1)}, f32[8,128]{1,0:T(8,128)S(1)}, f32[8,128]{1,0:T(8,128)S(1)}) fusion(f32[8,3]{1,0:T(8,128)S(1)} %copy.1178, f32[8,3,128]{2,1,0:T(4,128)S(1)} %copy.1180, f32[8,128]{1,0:T(8,128)S(1)} %get-tuple-element.1914, f32[8,3,128]{2,1,0:T(4,128)S(1)} %copy.1182, f32[8,128]{1,0:T(8,128)S(1)} %get-tuple-element.1918, ...), kind=kLoop, calls=%fused_computation.182.clone.1 | loop fusion | flops 12973056 | bytes 143456 | tf_op jit(solution)/shard_map/while/body/eval_jaxpr/vmap()/reduce_sum | solution.py:62
  65.8 2.6 %multiply_reduce_fusion.19 = (f32[8,128]{1,0:T(8,128)S(1)}, f32[8,128]{1,0:T(8,128)S(1)}, f32[8,128]{1,0:T(8,128)S(1)}) fusion(f32[8,3]{1,0:T(8,128)S(1)} %copy.1178, f32[8,3,128]{2,1,0:T(4,128)S(1)} %copy.1180, f32[8,128]{1,0:T(8,128)S(1)} %get-tuple-element.1914, f32[8,3,128]{2,1,0:T(4,128)S(1)} %copy.1182, f32[8,128]{1,0:T(8,128)S(1)} %get-tuple-element.1918, ...), kind=kLoop, calls=%fused_computation.182.clone.1 | loop fusion | flops 12973056 | bytes 143456 | tf_op jit(solution)/shard_map/while/body/eval_jaxpr/vmap()/reduce_sum | solution.py:62
  69.6 2.6 %multiply_reduce_fusion.19 = (f32[8,128]{1,0:T(8,128)S(1)}, f32[8,128]{1,0:T(8,128)S(1)}, f32[8,128]{1,0:T(8,128)S(1)}) fusion(f32[8,3]{1,0:T(8,128)S(1)} %copy.1178, f32[8,3,128]{2,1,0:T(4,128)S(1)} %copy.1180, f32[8,128]{1,0:T(8,128)S(1)} %get-tuple-element.1914, f32[8,3,128]{2,1,0:T(4,128)S(1)} %copy.1182, f32[8,128]{1,0:T(8,128)S(1)} %get-tuple-element.1918, ...), kind=kLoop, calls=%fused_computation.182.clone.1 | loop fusion | flops 12973056 | bytes 143456 | tf_op jit(solution)/shard_map/while/body/eval_jaxpr/vmap()/reduce_sum | solution.py:62
  73.5 2.6 %multiply_reduce_fusion.19 = (f32[8,128]{1,0:T(8,128)S(1)}, f32[8,128]{1,0:T(8,128)S(1)}, f32[8,128]{1,0:T(8,128)S(1)}) fusion(f32[8,3]{1,0:T(8,128)S(1)} %copy.1178, f32[8,3,128]{2,1,0:T(4,128)S(1)} %copy.1180, f32[8,128]{1,0:T(8,128)S(1)} %get-tuple-element.1914, f32[8,3,128]{2,1,0:T(4,128)S(1)} %copy.1182, f32[8,128]{1,0:T(8,128)S(1)} %get-tuple-element.1918, ...), kind=kLoop, calls=%fused_computation.182.clone.1 | loop fusion | flops 12973056 | bytes 143456 | tf_op jit(solution)/shard_map/while/body/eval_jaxpr/vmap()/reduce_sum | solution.py:62
  77.0 15.4 %while.134 = (s32[]{:T(128)}, f32[4,8,3,128]{3,1,2,0:T(8,128)S(1)}, f32[4,8,8,128]{3,2,1,0:T(8,128)S(1)}, s32[4,8,3]{1,2,0:T(4,128)S(1)}, f32[96,8,128]{2,1,0:T(8,128)S(1)}, /*index=5*/s32[4,8]{1,0:T(4,128)S(1)}, s32[]{:T(128)}) while((s32[]{:T(128)}, f32[4,8,3,128]{3,1,2,0:T(8,128)S(1)}, f32[4,8,8,128]{3,2,1,0:T(8,128)S(1)}, ...), condition=%wide.region_14.15_spmd, body=%wide.region_10.14_spmd.sunk | while | flops 12980370 | bytes 1156605 | solution.py:81
  78.1 2.6 %multiply_reduce_fusion.18 = (f32[8,128]{1,0:T(8,128)S(1)}, f32[8,128]{1,0:T(8,128)S(1)}, f32[8,128]{1,0:T(8,128)S(1)}) fusion(f32[8,3]{1,0:T(8,128)S(1)} %copy.1163, f32[8,3,128]{2,1,0:T(4,128)S(1)} %copy.1165, f32[8,128]{1,0:T(8,128)S(1)} %get-tuple-element.1879, f32[8,3,128]{2,1,0:T(4,128)S(1)} %copy.1167, f32[8,128]{1,0:T(8,128)S(1)} %get-tuple-element.1883, ...), kind=kLoop, calls=%fused_computation.134.clone.1 | loop fusion | flops 12973056 | bytes 143456 | tf_op jit(solution)/shard_map/while/body/eval_jaxpr/vmap()/reduce_sum | solution.py:62
  82.0 2.6 %multiply_reduce_fusion.18 = (f32[8,128]{1,0:T(8,128)S(1)}, f32[8,128]{1,0:T(8,128)S(1)}, f32[8,128]{1,0:T(8,128)S(1)}) fusion(f32[8,3]{1,0:T(8,128)S(1)} %copy.1163, f32[8,3,128]{2,1,0:T(4,128)S(1)} %copy.1165, f32[8,128]{1,0:T(8,128)S(1)} %get-tuple-element.1879, f32[8,3,128]{2,1,0:T(4,128)S(1)} %copy.1167, f32[8,128]{1,0:T(8,128)S(1)} %get-tuple-element.1883, ...), kind=kLoop, calls=%fused_computation.134.clone.1 | loop fusion | flops 12973056 | bytes 143456 | tf_op jit(solution)/shard_map/while/body/eval_jaxpr/vmap()/reduce_sum | solution.py:62
  85.8 2.6 %multiply_reduce_fusion.18 = (f32[8,128]{1,0:T(8,128)S(1)}, f32[8,128]{1,0:T(8,128)S(1)}, f32[8,128]{1,0:T(8,128)S(1)}) fusion(f32[8,3]{1,0:T(8,128)S(1)} %copy.1163, f32[8,3,128]{2,1,0:T(4,128)S(1)} %copy.1165, f32[8,128]{1,0:T(8,128)S(1)} %get-tuple-element.1879, f32[8,3,128]{2,1,0:T(4,128)S(1)} %copy.1167, f32[8,128]{1,0:T(8,128)S(1)} %get-tuple-element.1883, ...), kind=kLoop, calls=%fused_computation.134.clone.1 | loop fusion | flops 12973056 | bytes 143456 | tf_op jit(solution)/shard_map/while/body/eval_jaxpr/vmap()/reduce_sum | solution.py:62
  89.7 2.6 %multiply_reduce_fusion.18 = (f32[8,128]{1,0:T(8,128)S(1)}, f32[8,128]{1,0:T(8,128)S(1)}, f32[8,128]{1,0:T(8,128)S(1)}) fusion(f32[8,3]{1,0:T(8,128)S(1)} %copy.1163, f32[8,3,128]{2,1,0:T(4,128)S(1)} %copy.1165, f32[8,128]{1,0:T(8,128)S(1)} %get-tuple-element.1879, f32[8,3,128]{2,1,0:T(4,128)S(1)} %copy.1167, f32[8,128]{1,0:T(8,128)S(1)} %get-tuple-element.1883, ...), kind=kLoop, calls=%fused_computation.134.clone.1 | loop fusion | flops 12973056 | bytes 143456 | tf_op jit(solution)/shard_map/while/body/eval_jaxpr/vmap()/reduce_sum | solution.py:62
  93.3 1.9 collective-permute-start.4
  95.2 8.1 %collective-permute-start.5 = (f32[16,8,128]{2,1,0:T(8,128)S(1)}, f32[16,8,128]{2,1,0:T(8,128)S(1)}, u32[]{:S(2)}, u32[]{:S(2)}) collective-permute-start(f32[16,8,128]{2,1,0:T(8,128)S(1)} %get-tuple-element.1175), channel_id=1, source_target_pairs={{1,0},{2,1},{3,2},{4,3},{5,4},{6,5},{7,6},{8,7},{9,8},{10,9},{11,1... | collective-permute-start | bytes 196616 | tf_op jit(solution)/shard_map/ppermute | solution.py:112
  103.3 15.4 %while.137 = (s32[]{:T(128)}, f32[4,8,3,128]{3,1,2,0:T(8,128)S(1)}, f32[4,8,8,128]{3,2,1,0:T(8,128)S(1)}, s32[4,8,3]{1,2,0:T(4,128)S(1)}, f32[64,8,128]{2,1,0:T(8,128)S(1)}, /*index=5*/s32[4,8]{1,0:T(4,128)S(1)}, s32[]{:T(128)}) while((s32[]{:T(128)}, f32[4,8,3,128]{3,1,2,0:T(8,128)S(1)}, f32[4,8,8,128]{3,2,1,0:T(8,128)S(1)}, ...), condition=%wide.region_29.30_spmd, body=%wide.region_25.29_spmd.sunk | while | flops 12980370 | bytes 1156605 | solution.py:81
  104.5 2.6 %multiply_reduce_fusion.21 = (f32[8,128]{1,0:T(8,128)S(1)}, f32[8,128]{1,0:T(8,128)S(1)}, f32[8,128]{1,0:T(8,128)S(1)}) fusion(f32[8,3]{1,0:T(8,128)S(1)} %copy.1208, f32[8,3,128]{2,1,0:T(4,128)S(1)} %copy.1210, f32[8,128]{1,0:T(8,128)S(1)} %get-tuple-element.1984, f32[8,3,128]{2,1,0:T(4,128)S(1)} %copy.1212, f32[8,128]{1,0:T(8,128)S(1)} %get-tuple-element.1988, ...), kind=kLoop, calls=%fused_computation.278.clone.1 | loop fusion | flops 12973056 | bytes 143456 | tf_op jit(solution)/shard_map/while/body/eval_jaxpr/vmap()/reduce_sum | solution.py:62
  108.4 2.6 %multiply_reduce_fusion.21 = (f32[8,128]{1,0:T(8,128)S(1)}, f32[8,128]{1,0:T(8,128)S(1)}, f32[8,128]{1,0:T(8,128)S(1)}) fusion(f32[8,3]{1,0:T(8,128)S(1)} %copy.1208, f32[8,3,128]{2,1,0:T(4,128)S(1)} %copy.1210, f32[8,128]{1,0:T(8,128)S(1)} %get-tuple-element.1984, f32[8,3,128]{2,1,0:T(4,128)S(1)} %copy.1212, f32[8,128]{1,0:T(8,128)S(1)} %get-tuple-element.1988, ...), kind=kLoop, calls=%fused_computation.278.clone.1 | loop fusion | flops 12973056 | bytes 143456 | tf_op jit(solution)/shard_map/while/body/eval_jaxpr/vmap()/reduce_sum | solution.py:62
  112.2 2.6 %multiply_reduce_fusion.21 = (f32[8,128]{1,0:T(8,128)S(1)}, f32[8,128]{1,0:T(8,128)S(1)}, f32[8,128]{1,0:T(8,128)S(1)}) fusion(f32[8,3]{1,0:T(8,128)S(1)} %copy.1208, f32[8,3,128]{2,1,0:T(4,128)S(1)} %copy.1210, f32[8,128]{1,0:T(8,128)S(1)} %get-tuple-element.1984, f32[8,3,128]{2,1,0:T(4,128)S(1)} %copy.1212, f32[8,128]{1,0:T(8,128)S(1)} %get-tuple-element.1988, ...), kind=kLoop, calls=%fused_computation.278.clone.1 | loop fusion | flops 12973056 | bytes 143456 | tf_op jit(solution)/shard_map/while/body/eval_jaxpr/vmap()/reduce_sum | solution.py:62
  116.1 2.6 %multiply_reduce_fusion.21 = (f32[8,128]{1,0:T(8,128)S(1)}, f32[8,128]{1,0:T(8,128)S(1)}, f32[8,128]{1,0:T(8,128)S(1)}) fusion(f32[8,3]{1,0:T(8,128)S(1)} %copy.1208, f32[8,3,128]{2,1,0:T(4,128)S(1)} %copy.1210, f32[8,128]{1,0:T(8,128)S(1)} %get-tuple-element.1984, f32[8,3,128]{2,1,0:T(4,128)S(1)} %copy.1212, f32[8,128]{1,0:T(8,128)S(1)} %get-tuple-element.1988, ...), kind=kLoop, calls=%fused_computation.278.clone.1 | loop fusion | flops 12973056 | bytes 143456 | tf_op jit(solution)/shard_map/while/body/eval_jaxpr/vmap()/reduce_sum | solution.py:62
  119.6 15.4 %while.136 = (s32[]{:T(128)}, f32[4,8,3,128]{3,1,2,0:T(8,128)S(1)}, f32[4,8,8,128]{3,2,1,0:T(8,128)S(1)}, s32[4,8,3]{1,2,0:T(4,128)S(1)}, f32[96,8,128]{2,1,0:T(8,128)S(1)}, /*index=5*/s32[4,8]{1,0:T(4,128)S(1)}, s32[]{:T(128)}) while((s32[]{:T(128)}, f32[4,8,3,128]{3,1,2,0:T(8,128)S(1)}, f32[4,8,8,128]{3,2,1,0:T(8,128)S(1)}, ...), condition=%wide.region_24.25_spmd, body=%wide.region_20.24_spmd.sunk | while | flops 12980370 | bytes 1156605 | solution.py:81
  120.7 2.6 %multiply_reduce_fusion.20 = (f32[8,128]{1,0:T(8,128)S(1)}, f32[8,128]{1,0:T(8,128)S(1)}, f32[8,128]{1,0:T(8,128)S(1)}) fusion(f32[8,3]{1,0:T(8,128)S(1)} %copy.1193, f32[8,3,128]{2,1,0:T(4,128)S(1)} %copy.1195, f32[8,128]{1,0:T(8,128)S(1)} %get-tuple-element.1949, f32[8,3,128]{2,1,0:T(4,128)S(1)} %copy.1197, f32[8,128]{1,0:T(8,128)S(1)} %get-tuple-element.1953, ...), kind=kLoop, calls=%fused_computation.230.clone.1 | loop fusion | flops 12973056 | bytes 143456 | tf_op jit(solution)/shard_map/while/body/eval_jaxpr/vmap()/reduce_sum | solution.py:62
  124.6 2.6 %multiply_reduce_fusion.20 = (f32[8,128]{1,0:T(8,128)S(1)}, f32[8,128]{1,0:T(8,128)S(1)}, f32[8,128]{1,0:T(8,128)S(1)}) fusion(f32[8,3]{1,0:T(8,128)S(1)} %copy.1193, f32[8,3,128]{2,1,0:T(4,128)S(1)} %copy.1195, f32[8,128]{1,0:T(8,128)S(1)} %get-tuple-element.1949, f32[8,3,128]{2,1,0:T(4,128)S(1)} %copy.1197, f32[8,128]{1,0:T(8,128)S(1)} %get-tuple-element.1953, ...), kind=kLoop, calls=%fused_computation.230.clone.1 | loop fusion | flops 12973056 | bytes 143456 | tf_op jit(solution)/shard_map/while/body/eval_jaxpr/vmap()/reduce_sum | solution.py:62
  128.4 2.6 %multiply_reduce_fusion.20 = (f32[8,128]{1,0:T(8,128)S(1)}, f32[8,128]{1,0:T(8,128)S(1)}, f32[8,128]{1,0:T(8,128)S(1)}) fusion(f32[8,3]{1,0:T(8,128)S(1)} %copy.1193, f32[8,3,128]{2,1,0:T(4,128)S(1)} %copy.1195, f32[8,128]{1,0:T(8,128)S(1)} %get-tuple-element.1949, f32[8,3,128]{2,1,0:T(4,128)S(1)} %copy.1197, f32[8,128]{1,0:T(8,128)S(1)} %get-tuple-element.1953, ...), kind=kLoop, calls=%fused_computation.230.clone.1 | loop fusion | flops 12973056 | bytes 143456 | tf_op jit(solution)/shard_map/while/body/eval_jaxpr/vmap()/reduce_sum | solution.py:62
  132.3 2.6 %multiply_reduce_fusion.20 = (f32[8,128]{1,0:T(8,128)S(1)}, f32[8,128]{1,0:T(8,128)S(1)}, f32[8,128]{1,0:T(8,128)S(1)}) fusion(f32[8,3]{1,0:T(8,128)S(1)} %copy.1193, f32[8,3,128]{2,1,0:T(4,128)S(1)} %copy.1195, f32[8,128]{1,0:T(8,128)S(1)} %get-tuple-element.1949, f32[8,3,128]{2,1,0:T(4,128)S(1)} %copy.1197, f32[8,128]{1,0:T(8,128)S(1)} %get-tuple-element.1953, ...), kind=kLoop, calls=%fused_computation.230.clone.1 | loop fusion | flops 12973056 | bytes 143456 | tf_op jit(solution)/shard_map/while/body/eval_jaxpr/vmap()/reduce_sum | solution.py:62
  135.9 1.9 collective-permute-start.6
  137.8 8.1 %collective-permute-start.7 = (f32[16,8,128]{2,1,0:T(8,128)S(1)}, f32[16,8,128]{2,1,0:T(8,128)S(1)}, u32[]{:S(2)}, u32[]{:S(2)}) collective-permute-start(f32[16,8,128]{2,1,0:T(8,128)S(1)} %get-tuple-element.1173), channel_id=1, source_target_pairs={{1,0},{2,1},{3,2},{4,3},{5,4},{6,5},{7,6},{8,7},{9,8},{10,9},{11,1... | collective-permute-start | bytes 196616 | tf_op jit(solution)/shard_map/ppermute | solution.py:112
  145.9 15.4 %while.139 = (s32[]{:T(128)}, f32[4,8,3,128]{3,1,0,2:T(8,128)S(1)}, f32[4,8,8,128]{3,2,1,0:T(8,128)S(1)}, s32[4,8,3]{1,2,0:T(4,128)S(1)}, f32[64,8,128]{2,1,0:T(8,128)S(1)}, /*index=5*/s32[4,8]{1,0:T(4,128)S(1)}, s32[]{:T(128)}) while((s32[]{:T(128)}, f32[4,8,3,128]{3,1,0,2:T(8,128)S(1)}, f32[4,8,8,128]{3,2,1,0:T(8,128)S(1)}, ...), condition=%wide.region_39.40_spmd, body=%wide.region_35.39_spmd.sunk | while | flops 12980370 | bytes 1156605 | solution.py:81
  147.1 2.6 %multiply_reduce_fusion.23 = (f32[8,128]{1,0:T(8,128)S(1)}, f32[8,128]{1,0:T(8,128)S(1)}, f32[8,128]{1,0:T(8,128)S(1)}) fusion(f32[8,3]{1,0:T(8,128)S(1)} %copy.1238, f32[8,3,128]{2,1,0:T(4,128)S(1)} %copy.1240, f32[8,128]{1,0:T(8,128)S(1)} %get-tuple-element.2054, f32[8,3,128]{2,1,0:T(4,128)S(1)} %copy.1242, f32[8,128]{1,0:T(8,128)S(1)} %get-tuple-element.2058, ...), kind=kLoop, calls=%fused_computation.374.clone.1 | loop fusion | flops 12973056 | bytes 143456 | tf_op jit(solution)/shard_map/while/body/eval_jaxpr/vmap()/reduce_sum | solution.py:62
  151.0 2.6 %multiply_reduce_fusion.23 = (f32[8,128]{1,0:T(8,128)S(1)}, f32[8,128]{1,0:T(8,128)S(1)}, f32[8,128]{1,0:T(8,128)S(1)}) fusion(f32[8,3]{1,0:T(8,128)S(1)} %copy.1238, f32[8,3,128]{2,1,0:T(4,128)S(1)} %copy.1240, f32[8,128]{1,0:T(8,128)S(1)} %get-tuple-element.2054, f32[8,3,128]{2,1,0:T(4,128)S(1)} %copy.1242, f32[8,128]{1,0:T(8,128)S(1)} %get-tuple-element.2058, ...), kind=kLoop, calls=%fused_computation.374.clone.1 | loop fusion | flops 12973056 | bytes 143456 | tf_op jit(solution)/shard_map/while/body/eval_jaxpr/vmap()/reduce_sum | solution.py:62
  154.8 2.6 %multiply_reduce_fusion.23 = (f32[8,128]{1,0:T(8,128)S(1)}, f32[8,128]{1,0:T(8,128)S(1)}, f32[8,128]{1,0:T(8,128)S(1)}) fusion(f32[8,3]{1,0:T(8,128)S(1)} %copy.1238, f32[8,3,128]{2,1,0:T(4,128)S(1)} %copy.1240, f32[8,128]{1,0:T(8,128)S(1)} %get-tuple-element.2054, f32[8,3,128]{2,1,0:T(4,128)S(1)} %copy.1242, f32[8,128]{1,0:T(8,128)S(1)} %get-tuple-element.2058, ...), kind=kLoop, calls=%fused_computation.374.clone.1 | loop fusion | flops 12973056 | bytes 143456 | tf_op jit(solution)/shard_map/while/body/eval_jaxpr/vmap()/reduce_sum | solution.py:62
  158.7 2.6 %multiply_reduce_fusion.23 = (f32[8,128]{1,0:T(8,128)S(1)}, f32[8,128]{1,0:T(8,128)S(1)}, f32[8,128]{1,0:T(8,128)S(1)}) fusion(f32[8,3]{1,0:T(8,128)S(1)} %copy.1238, f32[8,3,128]{2,1,0:T(4,128)S(1)} %copy.1240, f32[8,128]{1,0:T(8,128)S(1)} %get-tuple-element.2054, f32[8,3,128]{2,1,0:T(4,128)S(1)} %copy.1242, f32[8,128]{1,0:T(8,128)S(1)} %get-tuple-element.2058, ...), kind=kLoop, calls=%fused_computation.374.clone.1 | loop fusion | flops 12973056 | bytes 143456 | tf_op jit(solution)/shard_map/while/body/eval_jaxpr/vmap()/reduce_sum | solution.py:62
  162.2 15.4 %while.138 = (s32[]{:T(128)}, f32[4,8,3,128]{3,1,2,0:T(8,128)S(1)}, f32[4,8,8,128]{3,2,1,0:T(8,128)S(1)}, s32[4,8,3]{1,2,0:T(4,128)S(1)}, f32[96,8,128]{2,1,0:T(8,128)S(1)}, /*index=5*/s32[4,8]{1,0:T(4,128)S(1)}, s32[]{:T(128)}) while((s32[]{:T(128)}, f32[4,8,3,128]{3,1,2,0:T(8,128)S(1)}, f32[4,8,8,128]{3,2,1,0:T(8,128)S(1)}, ...), condition=%wide.region_34.35_spmd, body=%wide.region_30.34_spmd.sunk | while | flops 12980370 | bytes 1156605 | solution.py:81
  163.3 2.6 %multiply_reduce_fusion.22 = (f32[8,128]{1,0:T(8,128)S(1)}, f32[8,128]{1,0:T(8,128)S(1)}, f32[8,128]{1,0:T(8,128)S(1)}) fusion(f32[8,3]{1,0:T(8,128)S(1)} %copy.1223, f32[8,3,128]{2,1,0:T(4,128)S(1)} %copy.1225, f32[8,128]{1,0:T(8,128)S(1)} %get-tuple-element.2019, f32[8,3,128]{2,1,0:T(4,128)S(1)} %copy.1227, f32[8,128]{1,0:T(8,128)S(1)} %get-tuple-element.2023, ...), kind=kLoop, calls=%fused_computation.326.clone.1 | loop fusion | flops 12973056 | bytes 143456 | tf_op jit(solution)/shard_map/while/body/eval_jaxpr/vmap()/reduce_sum | solution.py:62
  167.2 2.6 %multiply_reduce_fusion.22 = (f32[8,128]{1,0:T(8,128)S(1)}, f32[8,128]{1,0:T(8,128)S(1)}, f32[8,128]{1,0:T(8,128)S(1)}) fusion(f32[8,3]{1,0:T(8,128)S(1)} %copy.1223, f32[8,3,128]{2,1,0:T(4,128)S(1)} %copy.1225, f32[8,128]{1,0:T(8,128)S(1)} %get-tuple-element.2019, f32[8,3,128]{2,1,0:T(4,128)S(1)} %copy.1227, f32[8,128]{1,0:T(8,128)S(1)} %get-tuple-element.2023, ...), kind=kLoop, calls=%fused_computation.326.clone.1 | loop fusion | flops 12973056 | bytes 143456 | tf_op jit(solution)/shard_map/while/body/eval_jaxpr/vmap()/reduce_sum | solution.py:62
  171.1 2.6 %multiply_reduce_fusion.22 = (f32[8,128]{1,0:T(8,128)S(1)}, f32[8,128]{1,0:T(8,128)S(1)}, f32[8,128]{1,0:T(8,128)S(1)}) fusion(f32[8,3]{1,0:T(8,128)S(1)} %copy.1223, f32[8,3,128]{2,1,0:T(4,128)S(1)} %copy.1225, f32[8,128]{1,0:T(8,128)S(1)} %get-tuple-element.2019, f32[8,3,128]{2,1,0:T(4,128)S(1)} %copy.1227, f32[8,128]{1,0:T(8,128)S(1)} %get-tuple-element.2023, ...), kind=kLoop, calls=%fused_computation.326.clone.1 | loop fusion | flops 12973056 | bytes 143456 | tf_op jit(solution)/shard_map/while/body/eval_jaxpr/vmap()/reduce_sum | solution.py:62
  174.9 2.6 %multiply_reduce_fusion.22 = (f32[8,128]{1,0:T(8,128)S(1)}, f32[8,128]{1,0:T(8,128)S(1)}, f32[8,128]{1,0:T(8,128)S(1)}) fusion(f32[8,3]{1,0:T(8,128)S(1)} %copy.1223, f32[8,3,128]{2,1,0:T(4,128)S(1)} %copy.1225, f32[8,128]{1,0:T(8,128)S(1)} %get-tuple-element.2019, f32[8,3,128]{2,1,0:T(4,128)S(1)} %copy.1227, f32[8,128]{1,0:T(8,128)S(1)} %get-tuple-element.2023, ...), kind=kLoop, calls=%fused_computation.326.clone.1 | loop fusion | flops 12973056 | bytes 143456 | tf_op jit(solution)/shard_map/while/body/eval_jaxpr/vmap()/reduce_sum | solution.py:62
  179.0 2.1 collective-permute-start.8
  181.2 4.0 %while.140 = (s32[]{:T(128)}, f32[3,1024]{1,0:T(4,128)S(1)}, f32[1024]{0:T(1024)S(1)}, f32[2,8,3,128]{3,2,1,0:T(4,128)S(1)}, s32[2,1024]{1,0:T(2,128)S(1)}, /*index=5*/s32[]{:T(128)}, s32[]{:T(128)}) while((s32[]{:T(128)}, f32[3,1024]{1,0:T(4,128)S(1)}, f32[1024]{0:T(1024)S(1)}, f32[2,8,3,128]{3,2,1,0:T(4,128)S(1)}, ...), condition=%wide.region_42.43_spmd.clone, body=%wide.region_40.42_spmd.clone.sunk | while | flops 41950208 | bytes 77920 | solution.py:147
  185.2 4.0 %while.141 = (s32[]{:T(128)}, f32[3,1024]{1,0:T(4,128)S(1)}, f32[1024]{0:T(1024)S(1)}, f32[2,8,3,128]{3,2,1,0:T(4,128)S(1)}, s32[2,1024]{1,0:T(2,128)S(1)}, /*index=5*/s32[]{:T(128)}, s32[]{:T(128)}) while((s32[]{:T(128)}, f32[3,1024]{1,0:T(4,128)S(1)}, f32[1024]{0:T(1024)S(1)}, f32[2,8,3,128]{3,2,1,0:T(4,128)S(1)}, ...), condition=%wide.region_45.46_spmd.clone, body=%wide.region_43.45_spmd.clone.sunk | while | flops 41950208 | bytes 77920 | solution.py:147
  189.9 1.9 collective-permute-start.9
  191.8 4.0 %while.142 = (s32[]{:T(128)}, f32[3,1024]{1,0:T(4,128)S(1)}, f32[1024]{0:T(1024)S(1)}, f32[2,8,3,128]{3,2,1,0:T(4,128)S(1)}, s32[2,1024]{1,0:T(2,128)S(1)}, /*index=5*/s32[]{:T(128)}, s32[]{:T(128)}) while((s32[]{:T(128)}, f32[3,1024]{1,0:T(4,128)S(1)}, f32[1024]{0:T(1024)S(1)}, f32[2,8,3,128]{3,2,1,0:T(4,128)S(1)}, ...), condition=%wide.region_48.49_spmd.clone, body=%wide.region_46.48_spmd.clone.sunk | while | flops 41950208 | bytes 77920 | solution.py:147
  196.9 1.9 collective-permute-start.10
  198.9 4.0 %while.143 = (s32[]{:T(128)}, f32[3,1024]{1,0:T(4,128)S(1)}, f32[1024]{0:T(1024)S(1)}, f32[2,8,3,128]{3,2,1,0:T(4,128)S(1)}, s32[2,1024]{1,0:T(2,128)S(1)}, /*index=5*/s32[]{:T(128)}, s32[]{:T(128)}) while((s32[]{:T(128)}, f32[3,1024]{1,0:T(4,128)S(1)}, f32[1024]{0:T(1024)S(1)}, f32[2,8,3,128]{3,2,1,0:T(4,128)S(1)}, ...), condition=%wide.region_51.52_spmd.clone, body=%wide.region_49.51_spmd.clone.sunk | while | flops 41950208 | bytes 77920 | solution.py:147
  202.9 3.5 %collective-permute-done.10 = f32[8,128]{1,0:T(8,128)S(1)} collective-permute-done((f32[8,128]{1,0:T(8,128)S(1)}, f32[8,128]{1,0:T(8,128)S(1)}, u32[]{:S(2)}, u32[]{:S(2)}) %collective-permute-start.10) | collective-permute-done | bytes 4128 | tf_op jit(solution)/shard_map/ppermute | solution.py:39
  208.3 4.5 %collective-permute-done.11 = f32[8,128]{1,0:T(8,128)S(1)} collective-permute-done((f32[8,128]{1,0:T(8,128)S(1)}, f32[8,128]{1,0:T(8,128)S(1)}, u32[]{:S(2)}, u32[]{:S(2)}) %collective-permute-start.11) | collective-permute-done | bytes 4128 | tf_op jit(solution)/shard_map/ppermute | solution.py:39
  214.7 7.5 %collective-permute-done.12 = f32[8,128]{1,0:T(8,128)S(1)} collective-permute-done((f32[8,128]{1,0:T(8,128)S(1)}, f32[8,128]{1,0:T(8,128)S(1)}, u32[]{:S(2)}, u32[]{:S(2)}) %collective-permute-start.12) | collective-permute-done | bytes 4128 | tf_op jit(solution)/shard_map/ppermute | solution.py:39
  226.6 2.7 %collective-permute-start.14 = (f32[8,1024]{1,0:T(8,128)S(1)}, f32[8,1024]{1,0:T(8,128)S(1)}, u32[]{:S(2)}, u32[]{:S(2)}) collective-permute-start(f32[8,1024]{1,0:T(8,128)S(1)} %fusion.193), channel_id=1, source_target_pairs={{0,64},{32,96},{64,0},{96,32},{128,192},{160,224},{192,128},{224,1... | collective-permute-start | bytes 98312 | tf_op jit(solution)/shard_map/ppermute | solution.py:39
  230.0 2.4 collective-permute-done.14
  232.4 3.3 %collective-permute-start.15 = (f32[8,1024]{1,0:T(8,128)S(1)}, f32[8,1024]{1,0:T(8,128)S(1)}, u32[]{:S(2)}, u32[]{:S(2)}) collective-permute-start(f32[8,1024]{1,0:T(8,128)S(1)} %add.643), channel_id=1, source_target_pairs={{0,128},{32,160},{64,192},{96,224},{128,0},{160,32},{192,64},{224,... | collective-permute-start | bytes 98312 | tf_op jit(solution)/shard_map/ppermute | solution.py:39
  235.9 3.8 %collective-permute-done.15 = f32[8,1024]{1,0:T(8,128)S(1)} collective-permute-done((f32[8,1024]{1,0:T(8,128)S(1)}, f32[8,1024]{1,0:T(8,128)S(1)}, u32[]{:S(2)}, u32[]{:S(2)}) %collective-permute-start.15) | collective-permute-done | bytes 32800 | tf_op jit(solution)/shard_map/ppermute | solution.py:39
  239.7 2.3 collective-permute-start.16
  242.8 2.7 %collective-permute-done.16 = f32[8,1024]{1,0:T(8,128)S(1)} collective-permute-done((f32[8,1024]{1,0:T(8,128)S(1)}, f32[8,1024]{1,0:T(8,128)S(1)}, u32[]{:S(2)}, u32[]{:S(2)}) %collective-permute-start.16) | collective-permute-done | bytes 32800 | tf_op jit(solution)/shard_map/ppermute | solution.py:39
  (977 shorter events, 71.9 us)
Async XLA Ops:
  0.6 1.9 copy-start
  2.6 13.7 %copy-start.4 = (s32[1,64,3]{1,0,2:T(1,128)S(1)}, s32[1,64,3]{1,0,2:T(1,128)}, u32[]{:S(2)}) copy-start(s32[1,64,3]{1,0,2:T(1,128)} %param.36) | copy-start | bytes 2308
  2.7 30.7 %collective-permute-start = (f32[16,8,128]{2,1,0:T(8,128)S(1)}, f32[16,8,128]{2,1,0:T(8,128)S(1)}, u32[]{:S(2)}, u32[]{:S(2)}) collective-permute-start(f32[16,8,128]{2,1,0:T(8,128)S(1)} %get-tuple-element.1178), channel_id=1, source_target_pairs={{0,1},{1,2},{2,3},{3,4},{4,5},{5,6},{6,7},{7,8},{8,9},{9,10},{10,1... | collective-permute-start | bytes 196616 | tf_op jit(solution)/shard_map/ppermute | solution.py:111
  7.0 26.5 %collective-permute-start.1 = (f32[16,8,128]{2,1,0:T(8,128)S(1)}, f32[16,8,128]{2,1,0:T(8,128)S(1)}, u32[]{:S(2)}, u32[]{:S(2)}) collective-permute-start(f32[16,8,128]{2,1,0:T(8,128)S(1)} %get-tuple-element.1179), channel_id=1, source_target_pairs={{1,0},{2,1},{3,2},{4,3},{5,4},{6,5},{7,6},{8,7},{9,8},{10,9},{11,1... | collective-permute-start | bytes 196616 | tf_op jit(solution)/shard_map/ppermute | solution.py:112
  17.9 15.5 %copy-start.3 = (s32[1,64,128]{2,1,0:T(8,128)S(1)}, s32[1,64,128]{2,1,0:T(8,128)}, u32[]{:S(2)}) copy-start(s32[1,64,128]{2,1,0:T(8,128)} %param.37) | copy-start | bytes 98308
  34.2 15.5 %copy-start.1 = (f32[1,64,3,128]{3,1,2,0:T(8,128)S(1)}, f32[1,64,3,128]{3,1,2,0:T(8,128)}, u32[]{:S(2)}) copy-start(f32[1,64,3,128]{3,1,2,0:T(8,128)} %param.32) | copy-start | bytes 294916
  34.2 15.5 %copy-start.2 = (f32[1,64,3,128]{3,1,2,0:T(8,128)S(1)}, f32[1,64,3,128]{3,1,2,0:T(8,128)}, u32[]{:S(2)}) copy-start(f32[1,64,3,128]{3,1,2,0:T(8,128)} %param.33) | copy-start | bytes 294916
  50.7 25.5 %collective-permute-start.2 = (f32[16,8,128]{2,1,0:T(8,128)S(1)}, f32[16,8,128]{2,1,0:T(8,128)S(1)}, u32[]{:S(2)}, u32[]{:S(2)}) collective-permute-start(f32[16,8,128]{2,1,0:T(8,128)S(1)} %get-tuple-element.1176), channel_id=1, source_target_pairs={{0,1},{1,2},{2,3},{3,4},{4,5},{5,6},{6,7},{7,8},{8,9},{9,10},{10,1... | collective-permute-start | bytes 196616 | tf_op jit(solution)/shard_map/ppermute | solution.py:111
  52.6 23.6 %collective-permute-start.3 = (f32[16,8,128]{2,1,0:T(8,128)S(1)}, f32[16,8,128]{2,1,0:T(8,128)S(1)}, u32[]{:S(2)}, u32[]{:S(2)}) collective-permute-start(f32[16,8,128]{2,1,0:T(8,128)S(1)} %get-tuple-element.1177), channel_id=1, source_target_pairs={{1,0},{2,1},{3,2},{4,3},{5,4},{6,5},{7,6},{8,7},{9,8},{10,9},{11,1... | collective-permute-start | bytes 196616 | tf_op jit(solution)/shard_map/ppermute | solution.py:112
  93.3 25.5 %collective-permute-start.4 = (f32[16,8,128]{2,1,0:T(8,128)S(1)}, f32[16,8,128]{2,1,0:T(8,128)S(1)}, u32[]{:S(2)}, u32[]{:S(2)}) collective-permute-start(f32[16,8,128]{2,1,0:T(8,128)S(1)} %get-tuple-element.1174), channel_id=1, source_target_pairs={{0,1},{1,2},{2,3},{3,4},{4,5},{5,6},{6,7},{7,8},{8,9},{9,10},{10,1... | collective-permute-start | bytes 196616 | tf_op jit(solution)/shard_map/ppermute | solution.py:111
  95.2 23.6 %collective-permute-start.5 = (f32[16,8,128]{2,1,0:T(8,128)S(1)}, f32[16,8,128]{2,1,0:T(8,128)S(1)}, u32[]{:S(2)}, u32[]{:S(2)}) collective-permute-start(f32[16,8,128]{2,1,0:T(8,128)S(1)} %get-tuple-element.1175), channel_id=1, source_target_pairs={{1,0},{2,1},{3,2},{4,3},{5,4},{6,5},{7,6},{8,7},{9,8},{10,9},{11,1... | collective-permute-start | bytes 196616 | tf_op jit(solution)/shard_map/ppermute | solution.py:112
  135.9 25.5 %collective-permute-start.6 = (f32[16,8,128]{2,1,0:T(8,128)S(1)}, f32[16,8,128]{2,1,0:T(8,128)S(1)}, u32[]{:S(2)}, u32[]{:S(2)}) collective-permute-start(f32[16,8,128]{2,1,0:T(8,128)S(1)} %get-tuple-element.1172), channel_id=1, source_target_pairs={{0,1},{1,2},{2,3},{3,4},{4,5},{5,6},{6,7},{7,8},{8,9},{9,10},{10,1... | collective-permute-start | bytes 196616 | tf_op jit(solution)/shard_map/ppermute | solution.py:111
  137.8 23.6 %collective-permute-start.7 = (f32[16,8,128]{2,1,0:T(8,128)S(1)}, f32[16,8,128]{2,1,0:T(8,128)S(1)}, u32[]{:S(2)}, u32[]{:S(2)}) collective-permute-start(f32[16,8,128]{2,1,0:T(8,128)S(1)} %get-tuple-element.1173), channel_id=1, source_target_pairs={{1,0},{2,1},{3,2},{4,3},{5,4},{6,5},{7,6},{8,7},{9,8},{10,9},{11,1... | collective-permute-start | bytes 196616 | tf_op jit(solution)/shard_map/ppermute | solution.py:112
  179.0 10.2 %collective-permute-start.8 = (f32[8,128]{1,0:T(8,128)S(1)}, f32[8,128]{1,0:T(8,128)S(1)}, u32[]{:S(2)}, u32[]{:S(2)}) collective-permute-start(f32[8,128]{1,0:T(8,128)S(1)} %broadcast_in_dim.119), channel_id=1, source_target_pairs={{0,1},{1,0},{2,3},{3,2},{4,5},{5,4},{6,7},{7,6},{8,9},{9,8},{10,11... | collective-permute-start | bytes 12296 | tf_op jit(solution)/shard_map/ppermute | solution.py:39
  189.9 6.4 %collective-permute-start.9 = (f32[8,128]{1,0:T(8,128)S(1)}, f32[8,128]{1,0:T(8,128)S(1)}, u32[]{:S(2)}, u32[]{:S(2)}) collective-permute-start(f32[8,128]{1,0:T(8,128)S(1)} %broadcast_add_fusion), channel_id=1, source_target_pairs={{0,2},{1,3},{2,0},{3,1},{4,6},{5,7},{6,4},{7,5},{8,10},{9,11},{10,... | collective-permute-start | bytes 12296 | tf_op jit(solution)/shard_map/ppermute | solution.py:39
  196.9 9.4 %collective-permute-start.10 = (f32[8,128]{1,0:T(8,128)S(1)}, f32[8,128]{1,0:T(8,128)S(1)}, u32[]{:S(2)}, u32[]{:S(2)}) collective-permute-start(f32[8,128]{1,0:T(8,128)S(1)} %fusion.221), channel_id=1, source_target_pairs={{0,4},{1,5},{2,6},{3,7},{4,0},{5,1},{6,2},{7,3},{8,12},{9,13},{10,... | collective-permute-start | bytes 12296 | tf_op jit(solution)/shard_map/ppermute | solution.py:39
  206.3 6.4 %collective-permute-start.11 = (f32[8,128]{1,0:T(8,128)S(1)}, f32[8,128]{1,0:T(8,128)S(1)}, u32[]{:S(2)}, u32[]{:S(2)}) collective-permute-start(f32[8,128]{1,0:T(8,128)S(1)} %add.639), channel_id=1, source_target_pairs={{0,8},{1,9},{2,10},{3,11},{4,12},{5,13},{6,14},{7,15},{8,0},{9,1},... | collective-permute-start | bytes 12296 | tf_op jit(solution)/shard_map/ppermute | solution.py:39
  212.7 9.4 %collective-permute-start.12 = (f32[8,128]{1,0:T(8,128)S(1)}, f32[8,128]{1,0:T(8,128)S(1)}, u32[]{:S(2)}, u32[]{:S(2)}) collective-permute-start(f32[8,128]{1,0:T(8,128)S(1)} %add.640), channel_id=1, source_target_pairs={{0,16},{1,17},{2,18},{3,19},{4,20},{5,21},{6,22},{7,23},{8,24},{9,... | collective-permute-start | bytes 12296 | tf_op jit(solution)/shard_map/ppermute | solution.py:39
  223.5 3.1 %collective-permute-start.13 = (f32[8,1024]{1,0:T(8,128)S(1)}, f32[8,1024]{1,0:T(8,128)S(1)}, u32[]{:S(2)}, u32[]{:S(2)}) collective-permute-start(f32[8,1024]{1,0:T(8,128)S(1)} %maximum_maximum_fusion), channel_id=1, source_target_pairs={{0,32},{32,0},{64,96},{96,64},{128,160},{160,128},{192,224},{224,1... | collective-permute-start | bytes 98312 | tf_op jit(solution)/shard_map/ppermute | solution.py:39
  226.6 5.8 %collective-permute-start.14 = (f32[8,1024]{1,0:T(8,128)S(1)}, f32[8,1024]{1,0:T(8,128)S(1)}, u32[]{:S(2)}, u32[]{:S(2)}) collective-permute-start(f32[8,1024]{1,0:T(8,128)S(1)} %fusion.193), channel_id=1, source_target_pairs={{0,64},{32,96},{64,0},{96,32},{128,192},{160,224},{192,128},{224,1... | collective-permute-start | bytes 98312 | tf_op jit(solution)/shard_map/ppermute | solution.py:39
  232.4 7.3 %collective-permute-start.15 = (f32[8,1024]{1,0:T(8,128)S(1)}, f32[8,1024]{1,0:T(8,128)S(1)}, u32[]{:S(2)}, u32[]{:S(2)}) collective-permute-start(f32[8,1024]{1,0:T(8,128)S(1)} %add.643), channel_id=1, source_target_pairs={{0,128},{32,160},{64,192},{96,224},{128,0},{160,32},{192,64},{224,... | collective-permute-start | bytes 98312 | tf_op jit(solution)/shard_map/ppermute | solution.py:39
  239.7 5.8 %collective-permute-start.16 = (f32[8,1024]{1,0:T(8,128)S(1)}, f32[8,1024]{1,0:T(8,128)S(1)}, u32[]{:S(2)}, u32[]{:S(2)}) collective-permute-start(f32[8,1024]{1,0:T(8,128)S(1)} %add.644), channel_id=1, source_target_pairs={{0,256},{32,288},{64,320},{96,352},{128,384},{160,416},{192,448},{... | collective-permute-start | bytes 98312 | tf_op jit(solution)/shard_map/ppermute | solution.py:39
  242.1 5.3 %copy-start.5 = (f32[1,3,128]{2,0,1:T(1,128)S(1)}, f32[1,3,128]{2,0,1:T(1,128)}, u32[]{:S(2)}) copy-start(f32[1,3,128]{2,0,1:T(1,128)} %param.38) | copy-start | bytes 4612

commit v6 on v5

--- a/solution.py
+++ b/solution.py
@@ -68,7 +68,7 @@
 
 def tile_forces(source, own_index, link_index):
     tiles = own_index.shape[0]
-    group = 8
+    group = 32
     width = source.shape[-1]
     own_tiles = source[own_index]
 

time: 249 us -> 224 us (0.90)
  local copies, waits for them, and re-layouts: 41.8 us -> 21.7 us
  loops' own time: 6.36 us -> 0.29 us
    gather x32 -> x8, local copies, waits for them, and re-layouts: 18.5 us -> 5.53 us  [per_group(): partners = source[link_group]]
    another operation x8 -> x0, loops' own time: 6.02 us -> none  [tile_forces(): lax.map(per_group, (own_tiles.reshape(tiles // group, group, 8, width), l...]
    select_n x64 -> x4, local copies, waits for them, and re-layouts: 5.22 us -> 0.39 us  [per_group(): partners = source[link_group]]
    reduce_sum x32 -> x8, other arithmetic: 84.4 us -> 85.5 us  [bead_forces(): jnp.sum(factor * offset_x, axis=(0, 2))]
  transfers between devices with their start and end apart: 17 -> 17, of which waited for: 8 -> 8; matrix products, arithmetic and copies ran while one was open for 31% -> 27% of each run, Pallas kernels for 0% -> 0%
where the time goes in v6:
time: 224 us; the launch traced here: 223 us
  other arithmetic  95.6 us (43%)
  starting transfers between devices  64.1 us (29%)
  waiting for transfers between devices  25.7 us (11%)
  local copies, waits for them, and re-layouts  21.7 us (10%)
  matrix products  11.7 us (5%)
  between operations  3.83 us (2%)
    reduce_sum x8, other arithmetic, bead_forces(): jnp.sum(factor * offset_x, axis=(0, 2))  85.5 us
    ppermute x4, starting transfers between devices, shards(): after = lax.ppermute(packed[:HALO], 'space', down)  33.9 us
    ppermute x9, waiting for transfers between devices, butterfly_sum(): leaves.append(lax.ppermute(value, axis, pairs))  25.7 us
    ppermute x9, starting transfers between devices, butterfly_sum(): leaves.append(lax.ppermute(value, axis, pairs))  20.2 us
    dot_general x8, matrix products, accumulate(): jnp.dot(rows_now, table, precision=lax.Precision.HIGHEST, preferred_eleme...  11.7 us
    ppermute x4, starting transfers between devices, shards(): before = lax.ppermute(packed[tiles - HALO:], 'space', up)  10 us
    gather x8, local copies, waits for them, and re-layouts, per_group(): partners = source[link_group]  5.53 us
    gather x8, local copies, waits for them, and re-layouts, tile_forces(): own_tiles = source[own_index]  4.68 us
  transfers between devices with their start and end apart: 17, of which 8 were waited for; matrix products, arithmetic and copies ran while one was open for 27% of the time, Pallas kernels for 0%

profile of v6, /device:TPU:46, one launch (start us, length us, event | category | flops | bytes accessed | tf_op | source)
XLA Modules:
  0.0 222.9 jit_solution(16065256522139335105)
XLA Ops:
  0.6 0.8 slice_bitcast_fusion
  1.5 1.0 fusion.136
  2.5 4.3 %collective-permute-start = (f32[16,8,128]{2,0,1:T(8,128)S(1)}, f32[16,8,128]{2,0,1:T(8,128)S(1)}, u32[]{:S(2)}, u32[]{:S(2)}) collective-permute-start(f32[16,8,128]{2,0,1:T(8,128)S(1)} %get-tuple-element.562), channel_id=1, source_target_pairs={{0,1},{1,2},{2,3},{3,4},{4,5},{5,6},{6,7},{7,8},{8,9},{9,10},{10,1... | collective-permute-start | bytes 196616 | tf_op jit(solution)/shard_map/ppermute | solution.py:111
  6.8 9.3 %collective-permute-start.1 = (f32[16,8,128]{2,0,1:T(8,128)S(1)}, f32[16,8,128]{2,0,1:T(8,128)S(1)}, u32[]{:S(2)}, u32[]{:S(2)}) collective-permute-start(f32[16,8,128]{2,0,1:T(8,128)S(1)} %get-tuple-element.563), channel_id=1, source_target_pairs={{1,0},{2,1},{3,2},{4,3},{5,4},{6,5},{7,6},{8,7},{9,8},{10,9},{11,1... | collective-permute-start | bytes 196616 | tf_op jit(solution)/shard_map/ppermute | solution.py:112
  17.6 0.6 gather_fusion.2
  18.3 0.7 gather_fusion.3
  19.7 10.7 %multiply_reduce_fusion.6 = (f32[32,128]{1,0:T(8,128)S(1)}, f32[32,128]{1,0:T(8,128)S(1)}, f32[32,128]{1,0:T(8,128)S(1)}) fusion(f32[32,3]{1,0:T(8,128)S(1)} %copy.333, f32[32,3,128]{2,1,0:T(4,128)S(1)} %copy.332, f32[32,128]{1,0:T(8,128)S(1)} %bitcast.502, f32[32,3,128]{2,1,0:T(4,128)S(1)} %copy.345, f32[32,128]{1,0:T(8,128)S(1)} %bitcast.503, ...), kind=kLoop, calls=%fused_computation.216 | loop fusion | flops 51892224 | bytes 573824 | tf_op jit(solution)/shard_map/while/body/eval_jaxpr/vmap()/reduce_sum | solution.py:62
  30.8 0.6 gather_fusion
  31.4 0.7 gather_fusion.1
  32.9 10.7 %multiply_reduce_fusion.7 = (f32[32,128]{1,0:T(8,128)S(1)}, f32[32,128]{1,0:T(8,128)S(1)}, f32[32,128]{1,0:T(8,128)S(1)}) fusion(f32[32,3]{1,0:T(8,128)S(1)} %copy.313, f32[32,3,128]{2,1,0:T(4,128)S(1)} %copy.312, f32[32,128]{1,0:T(8,128)S(1)} %bitcast.534, f32[32,3,128]{2,1,0:T(4,128)S(1)} %copy.325, f32[32,128]{1,0:T(8,128)S(1)} %bitcast.535, ...), kind=kLoop, calls=%fused_computation.218 | loop fusion | flops 51892224 | bytes 573824 | tf_op jit(solution)/shard_map/while/body/eval_jaxpr/vmap()/reduce_sum | solution.py:62
  44.4 0.7 gather_fusion.7
  45.1 1.9 collective-permute-start.2
  47.1 8.1 %collective-permute-start.3 = (f32[16,8,128]{2,0,1:T(8,128)S(1)}, f32[16,8,128]{2,0,1:T(8,128)S(1)}, u32[]{:S(2)}, u32[]{:S(2)}) collective-permute-start(f32[16,8,128]{2,0,1:T(8,128)S(1)} %get-tuple-element.561), channel_id=1, source_target_pairs={{1,0},{2,1},{3,2},{4,3},{5,4},{6,5},{7,6},{8,7},{9,8},{10,9},{11,1... | collective-permute-start | bytes 196616 | tf_op jit(solution)/shard_map/ppermute | solution.py:112
  56.1 10.7 %multiply_reduce_fusion.4 = (f32[32,128]{1,0:T(8,128)S(1)}, f32[32,128]{1,0:T(8,128)S(1)}, f32[32,128]{1,0:T(8,128)S(1)}) fusion(f32[32,3,128]{2,1,0:T(4,128)S(1)} %copy.369, f32[32,128]{1,0:T(8,128)S(1)} %bitcast.518, f32[32,3]{1,0:T(8,128)S(1)} %copy.333, f32[32,3,128]{2,1,0:T(4,128)S(1)} %copy.381, f32[32,128]{1,0:T(8,128)S(1)} %bitcast.519, ...), kind=kLoop, calls=%fused_computation.212 | loop fusion | flops 51892224 | bytes 573824 | tf_op jit(solution)/shard_map/while/body/eval_jaxpr/vmap()/reduce_sum | solution.py:62
  67.7 0.7 gather_fusion.5
  69.2 10.7 %multiply_reduce_fusion.5 = (f32[32,128]{1,0:T(8,128)S(1)}, f32[32,128]{1,0:T(8,128)S(1)}, f32[32,128]{1,0:T(8,128)S(1)}) fusion(f32[32,3,128]{2,1,0:T(4,128)S(1)} %copy.351, f32[32,128]{1,0:T(8,128)S(1)} %bitcast.550, f32[32,3]{1,0:T(8,128)S(1)} %copy.313, f32[32,3,128]{2,1,0:T(4,128)S(1)} %copy.363, f32[32,128]{1,0:T(8,128)S(1)} %bitcast.551, ...), kind=kLoop, calls=%fused_computation.214 | loop fusion | flops 51892224 | bytes 573824 | tf_op jit(solution)/shard_map/while/body/eval_jaxpr/vmap()/reduce_sum | solution.py:62
  80.8 0.7 gather_fusion.11
  81.5 1.9 collective-permute-start.4
  83.4 8.3 %collective-permute-start.5 = (f32[16,8,128]{2,0,1:T(8,128)S(1)}, f32[16,8,128]{2,0,1:T(8,128)S(1)}, u32[]{:S(2)}, u32[]{:S(2)}) collective-permute-start(f32[16,8,128]{2,0,1:T(8,128)S(1)} %get-tuple-element.559), channel_id=1, source_target_pairs={{1,0},{2,1},{3,2},{4,3},{5,4},{6,5},{7,6},{8,7},{9,8},{10,9},{11,1... | collective-permute-start | bytes 196616 | tf_op jit(solution)/shard_map/ppermute | solution.py:112
  92.5 10.7 %multiply_reduce_fusion.2 = (f32[32,128]{1,0:T(8,128)S(1)}, f32[32,128]{1,0:T(8,128)S(1)}, f32[32,128]{1,0:T(8,128)S(1)}) fusion(f32[32,3,128]{2,1,0:T(4,128)S(1)} %copy.405, f32[32,128]{1,0:T(8,128)S(1)} %bitcast.526, f32[32,3]{1,0:T(8,128)S(1)} %copy.333, f32[32,3,128]{2,1,0:T(4,128)S(1)} %copy.417, f32[32,128]{1,0:T(8,128)S(1)} %bitcast.527, ...), kind=kLoop, calls=%fused_computation.208 | loop fusion | flops 51892224 | bytes 573824 | tf_op jit(solution)/shard_map/while/body/eval_jaxpr/vmap()/reduce_sum | solution.py:62
  104.1 0.7 gather_fusion.9
  105.7 10.7 %multiply_reduce_fusion.3 = (f32[32,128]{1,0:T(8,128)S(1)}, f32[32,128]{1,0:T(8,128)S(1)}, f32[32,128]{1,0:T(8,128)S(1)}) fusion(f32[32,3,128]{2,1,0:T(4,128)S(1)} %copy.387, f32[32,128]{1,0:T(8,128)S(1)} %bitcast.558, f32[32,3]{1,0:T(8,128)S(1)} %copy.313, f32[32,3,128]{2,1,0:T(4,128)S(1)} %copy.399, f32[32,128]{1,0:T(8,128)S(1)} %bitcast.559, ...), kind=kLoop, calls=%fused_computation.210 | loop fusion | flops 51892224 | bytes 573824 | tf_op jit(solution)/shard_map/while/body/eval_jaxpr/vmap()/reduce_sum | solution.py:62
  117.2 0.7 gather_fusion.15
  117.9 1.9 collective-permute-start.6
  119.9 8.1 %collective-permute-start.7 = (f32[16,8,128]{2,0,1:T(8,128)S(1)}, f32[16,8,128]{2,0,1:T(8,128)S(1)}, u32[]{:S(2)}, u32[]{:S(2)}) collective-permute-start(f32[16,8,128]{2,0,1:T(8,128)S(1)} %get-tuple-element.557), channel_id=1, source_target_pairs={{1,0},{2,1},{3,2},{4,3},{5,4},{6,5},{7,6},{8,7},{9,8},{10,9},{11,1... | collective-permute-start | bytes 196616 | tf_op jit(solution)/shard_map/ppermute | solution.py:112
  128.8 10.7 %multiply_reduce_fusion = (f32[32,128]{1,0:T(8,128)S(1)}, f32[32,128]{1,0:T(8,128)S(1)}, f32[32,128]{1,0:T(8,128)S(1)}) fusion(f32[32,3,128]{2,1,0:T(4,128)S(1)} %copy.441, f32[32,128]{1,0:T(8,128)S(1)} %bitcast.510, f32[32,3]{1,0:T(8,128)S(1)} %copy.333, f32[32,3,128]{2,1,0:T(4,128)S(1)} %copy.453, f32[32,128]{1,0:T(8,128)S(1)} %bitcast.511, ...), kind=kLoop, calls=%fused_computation.204 | loop fusion | flops 51892224 | bytes 573824 | tf_op jit(solution)/shard_map/while/body/eval_jaxpr/vmap()/reduce_sum | solution.py:62
  140.5 0.7 gather_fusion.13
  142.0 10.7 %multiply_reduce_fusion.1 = (f32[32,128]{1,0:T(8,128)S(1)}, f32[32,128]{1,0:T(8,128)S(1)}, f32[32,128]{1,0:T(8,128)S(1)}) fusion(f32[32,3,128]{2,1,0:T(4,128)S(1)} %copy.423, f32[32,128]{1,0:T(8,128)S(1)} %bitcast.542, f32[32,3]{1,0:T(8,128)S(1)} %copy.313, f32[32,3,128]{2,1,0:T(4,128)S(1)} %copy.435, f32[32,128]{1,0:T(8,128)S(1)} %bitcast.543, ...), kind=kLoop, calls=%fused_computation.206 | loop fusion | flops 51892224 | bytes 573824 | tf_op jit(solution)/shard_map/while/body/eval_jaxpr/vmap()/reduce_sum | solution.py:62
  152.7 0.7 slice_reduce_fusion
  153.4 4.0 %while.13 = (s32[]{:T(128)}, f32[3,1024]{1,0:T(4,128)S(1)}, f32[1024]{0:T(1024)S(1)}, f32[2,8,3,128]{3,1,0,2:T(8,128)S(1)}, s32[2,1024]{1,0:T(2,128)S(1)}, /*index=5*/s32[]{:T(128)}, s32[]{:T(128)}) while((s32[]{:T(128)}, f32[3,1024]{1,0:T(4,128)S(1)}, f32[1024]{0:T(1024)S(1)}, f32[2,8,3,128]{3,1,0,2:T(8,128)S(1)}, ...), condition=%wide.region_29.30_spmd.clone, body=%wide.region_27.29_spmd.clone.sunk | while | flops 41950208 | bytes 94312 | solution.py:147
  154.0 1.5 fusion.200
  156.0 1.5 fusion.200
  157.4 0.7 broadcast_in_dim.135
  158.1 1.9 collective-permute-start.8
  160.1 4.0 %while.15 = (s32[]{:T(128)}, f32[3,1024]{1,0:T(4,128)S(1)}, f32[1024]{0:T(1024)S(1)}, f32[2,8,3,128]{3,1,0,2:T(8,128)S(1)}, s32[2,1024]{1,0:T(2,128)S(1)}, /*index=5*/s32[]{:T(128)}, s32[]{:T(128)}) while((s32[]{:T(128)}, f32[3,1024]{1,0:T(4,128)S(1)}, f32[1024]{0:T(1024)S(1)}, f32[2,8,3,128]{3,1,0,2:T(8,128)S(1)}, ...), condition=%wide.region_35.36_spmd.clone, body=%wide.region_33.35_spmd.clone.sunk | while | flops 41950208 | bytes 94312 | solution.py:147
  160.6 1.5 fusion.204
  162.6 1.5 fusion.204
  164.1 0.7 broadcast_add_fusion
  164.8 2.1 collective-permute-start.9
  167.0 4.0 %while.14 = (s32[]{:T(128)}, f32[3,1024]{1,0:T(4,128)S(1)}, f32[1024]{0:T(1024)S(1)}, f32[2,8,3,128]{3,1,0,2:T(8,128)S(1)}, s32[2,1024]{1,0:T(2,128)S(1)}, /*index=5*/s32[]{:T(128)}, s32[]{:T(128)}) while((s32[]{:T(128)}, f32[3,1024]{1,0:T(4,128)S(1)}, f32[1024]{0:T(1024)S(1)}, f32[2,8,3,128]{3,1,0,2:T(8,128)S(1)}, ...), condition=%wide.region_32.33_spmd.clone, body=%wide.region_30.32_spmd.clone.sunk | while | flops 41950208 | bytes 94312 | solution.py:147
  167.5 1.5 fusion.202
  169.5 1.5 fusion.202
  171.2 0.7 fusion.189
  171.9 1.9 collective-permute-start.10
  173.8 4.0 %while.12 = (s32[]{:T(128)}, f32[3,1024]{1,0:T(4,128)S(1)}, f32[1024]{0:T(1024)S(1)}, f32[2,8,3,128]{3,1,0,2:T(8,128)S(1)}, s32[2,1024]{1,0:T(2,128)S(1)}, /*index=5*/s32[]{:T(128)}, s32[]{:T(128)}) while((s32[]{:T(128)}, f32[3,1024]{1,0:T(4,128)S(1)}, f32[1024]{0:T(1024)S(1)}, f32[2,8,3,128]{3,1,0,2:T(8,128)S(1)}, ...), condition=%wide.region_26.27_spmd.clone, body=%wide.region_24.26_spmd.clone.sunk | while | flops 41950208 | bytes 94312 | solution.py:147
  174.4 1.5 fusion.198
  176.4 1.5 fusion.198
  177.8 3.5 %collective-permute-done.10 = f32[8,128]{1,0:T(8,128)S(1)} collective-permute-done((f32[8,128]{1,0:T(8,128)S(1)}, f32[8,128]{1,0:T(8,128)S(1)}, u32[]{:S(2)}, u32[]{:S(2)}) %collective-permute-start.10) | collective-permute-done | bytes 4128 | tf_op jit(solution)/shard_map/ppermute | solution.py:39
  181.3 1.9 collective-permute-start.11
  183.2 4.5 %collective-permute-done.11 = f32[8,128]{1,0:T(8,128)S(1)} collective-permute-done((f32[8,128]{1,0:T(8,128)S(1)}, f32[8,128]{1,0:T(8,128)S(1)}, u32[]{:S(2)}, u32[]{:S(2)}) %collective-permute-start.11) | collective-permute-done | bytes 4128 | tf_op jit(solution)/shard_map/ppermute | solution.py:39
  187.7 2.1 collective-permute-start.12
  189.8 7.3 %collective-permute-done.12 = f32[8,128]{1,0:T(8,128)S(1)} collective-permute-done((f32[8,128]{1,0:T(8,128)S(1)}, f32[8,128]{1,0:T(8,128)S(1)}, u32[]{:S(2)}, u32[]{:S(2)}) %collective-permute-start.12) | collective-permute-done | bytes 4128 | tf_op jit(solution)/shard_map/ppermute | solution.py:39
  197.6 0.6 broadcast_in_dim.136
  198.4 1.9 collective-permute-start.13
  200.3 1.2 collective-permute-done.13
  201.6 2.7 %collective-permute-start.14 = (f32[8,1024]{1,0:T(8,128)S(1)}, f32[8,1024]{1,0:T(8,128)S(1)}, u32[]{:S(2)}, u32[]{:S(2)}) collective-permute-start(f32[8,1024]{1,0:T(8,128)S(1)} %fusion.161), channel_id=1, source_target_pairs={{0,64},{32,96},{64,0},{96,32},{128,192},{160,224},{192,128},{224,1... | collective-permute-start | bytes 98312 | tf_op jit(solution)/shard_map/ppermute | solution.py:39
  205.0 2.4 %collective-permute-done.14 = f32[8,1024]{1,0:T(8,128)S(1)} collective-permute-done((f32[8,1024]{1,0:T(8,128)S(1)}, f32[8,1024]{1,0:T(8,128)S(1)}, u32[]{:S(2)}, u32[]{:S(2)}) %collective-permute-start.14) | collective-permute-done | bytes 32800 | tf_op jit(solution)/shard_map/ppermute | solution.py:39
  207.4 3.3 %collective-permute-start.15 = (f32[8,1024]{1,0:T(8,128)S(1)}, f32[8,1024]{1,0:T(8,128)S(1)}, u32[]{:S(2)}, u32[]{:S(2)}) collective-permute-start(f32[8,1024]{1,0:T(8,128)S(1)} %add.816), channel_id=1, source_target_pairs={{0,128},{32,160},{64,192},{96,224},{128,0},{160,32},{192,64},{224,... | collective-permute-start | bytes 98312 | tf_op jit(solution)/shard_map/ppermute | solution.py:39
  210.7 4.0 %collective-permute-done.15 = f32[8,1024]{1,0:T(8,128)S(1)} collective-permute-done((f32[8,1024]{1,0:T(8,128)S(1)}, f32[8,1024]{1,0:T(8,128)S(1)}, u32[]{:S(2)}, u32[]{:S(2)}) %collective-permute-start.15) | collective-permute-done | bytes 32800 | tf_op jit(solution)/shard_map/ppermute | solution.py:39
  214.7 2.3 %collective-permute-start.16 = (f32[8,1024]{1,0:T(8,128)S(1)}, f32[8,1024]{1,0:T(8,128)S(1)}, u32[]{:S(2)}, u32[]{:S(2)}) collective-permute-start(f32[8,1024]{1,0:T(8,128)S(1)} %add.817), channel_id=1, source_target_pairs={{0,256},{32,288},{64,320},{96,352},{128,384},{160,416},{192,448},{... | collective-permute-start | bytes 98312 | tf_op jit(solution)/shard_map/ppermute | solution.py:39
  217.1 0.7 multiply_add_fusion
  217.8 2.7 %collective-permute-done.16 = f32[8,1024]{1,0:T(8,128)S(1)} collective-permute-done((f32[8,1024]{1,0:T(8,128)S(1)}, f32[8,1024]{1,0:T(8,128)S(1)}, u32[]{:S(2)}, u32[]{:S(2)}) %collective-permute-start.16) | collective-permute-done | bytes 32800 | tf_op jit(solution)/shard_map/ppermute | solution.py:39
  221.7 0.6 slice_divide_fusion
  222.3 0.6 broadcast_select_fusion
  (285 shorter events, 18.0 us)
Async XLA Ops:
  1.5 14.6 %copy-start.4 = (s32[1,64,3]{1,0,2:T(1,128)S(1)}, s32[1,64,3]{1,0,2:T(1,128)}, u32[]{:S(2)}) copy-start(s32[1,64,3]{1,0,2:T(1,128)} %param.20) | copy-start | bytes 2308
  2.5 15.1 %copy-start.3 = (s32[1,64,128]{2,1,0:T(8,128)S(1)}, s32[1,64,128]{2,1,0:T(8,128)}, u32[]{:S(2)}) copy-start(s32[1,64,128]{2,1,0:T(8,128)} %param.21) | copy-start | bytes 98308
  2.5 28.0 %collective-permute-start = (f32[16,8,128]{2,0,1:T(8,128)S(1)}, f32[16,8,128]{2,0,1:T(8,128)S(1)}, u32[]{:S(2)}, u32[]{:S(2)}) collective-permute-start(f32[16,8,128]{2,0,1:T(8,128)S(1)} %get-tuple-element.562), channel_id=1, source_target_pairs={{0,1},{1,2},{2,3},{3,4},{4,5},{5,6},{6,7},{7,8},{8,9},{9,10},{10,1... | collective-permute-start | bytes 196616 | tf_op jit(solution)/shard_map/ppermute | solution.py:111
  6.8 23.7 %collective-permute-start.1 = (f32[16,8,128]{2,0,1:T(8,128)S(1)}, f32[16,8,128]{2,0,1:T(8,128)S(1)}, u32[]{:S(2)}, u32[]{:S(2)}) collective-permute-start(f32[16,8,128]{2,0,1:T(8,128)S(1)} %get-tuple-element.563), channel_id=1, source_target_pairs={{1,0},{2,1},{3,2},{4,3},{5,4},{6,5},{7,6},{8,7},{9,8},{10,9},{11,1... | collective-permute-start | bytes 196616 | tf_op jit(solution)/shard_map/ppermute | solution.py:112
  19.7 10.8 %copy-start = (f32[1,64,128]{2,1,0:T(8,128)S(1)}, f32[1,64,128]{2,1,0:T(8,128)}, u32[]{:S(2)}) copy-start(f32[1,64,128]{2,1,0:T(8,128)} %param.18) | copy-start | bytes 98308
  19.7 10.8 %copy-start.1 = (f32[1,64,3,128]{3,1,2,0:T(8,128)S(1)}, f32[1,64,3,128]{3,1,2,0:T(8,128)}, u32[]{:S(2)}) copy-start(f32[1,64,3,128]{3,1,2,0:T(8,128)} %param.16) | copy-start | bytes 294916
  19.7 10.8 %copy-start.2 = (f32[1,64,3,128]{3,1,2,0:T(8,128)S(1)}, f32[1,64,3,128]{3,1,2,0:T(8,128)}, u32[]{:S(2)}) copy-start(f32[1,64,3,128]{3,1,2,0:T(8,128)} %param.17) | copy-start | bytes 294916
  45.1 21.6 %collective-permute-start.2 = (f32[16,8,128]{2,0,1:T(8,128)S(1)}, f32[16,8,128]{2,0,1:T(8,128)S(1)}, u32[]{:S(2)}, u32[]{:S(2)}) collective-permute-start(f32[16,8,128]{2,0,1:T(8,128)S(1)} %get-tuple-element.560), channel_id=1, source_target_pairs={{0,1},{1,2},{2,3},{3,4},{4,5},{5,6},{6,7},{7,8},{8,9},{9,10},{10,1... | collective-permute-start | bytes 196616 | tf_op jit(solution)/shard_map/ppermute | solution.py:111
  47.1 19.7 %collective-permute-start.3 = (f32[16,8,128]{2,0,1:T(8,128)S(1)}, f32[16,8,128]{2,0,1:T(8,128)S(1)}, u32[]{:S(2)}, u32[]{:S(2)}) collective-permute-start(f32[16,8,128]{2,0,1:T(8,128)S(1)} %get-tuple-element.561), channel_id=1, source_target_pairs={{1,0},{2,1},{3,2},{4,3},{5,4},{6,5},{7,6},{8,7},{9,8},{10,9},{11,1... | collective-permute-start | bytes 196616 | tf_op jit(solution)/shard_map/ppermute | solution.py:112
  81.5 21.8 %collective-permute-start.4 = (f32[16,8,128]{2,0,1:T(8,128)S(1)}, f32[16,8,128]{2,0,1:T(8,128)S(1)}, u32[]{:S(2)}, u32[]{:S(2)}) collective-permute-start(f32[16,8,128]{2,0,1:T(8,128)S(1)} %get-tuple-element.558), channel_id=1, source_target_pairs={{0,1},{1,2},{2,3},{3,4},{4,5},{5,6},{6,7},{7,8},{8,9},{9,10},{10,1... | collective-permute-start | bytes 196616 | tf_op jit(solution)/shard_map/ppermute | solution.py:111
  83.4 19.9 %collective-permute-start.5 = (f32[16,8,128]{2,0,1:T(8,128)S(1)}, f32[16,8,128]{2,0,1:T(8,128)S(1)}, u32[]{:S(2)}, u32[]{:S(2)}) collective-permute-start(f32[16,8,128]{2,0,1:T(8,128)S(1)} %get-tuple-element.559), channel_id=1, source_target_pairs={{1,0},{2,1},{3,2},{4,3},{5,4},{6,5},{7,6},{8,7},{9,8},{10,9},{11,1... | collective-permute-start | bytes 196616 | tf_op jit(solution)/shard_map/ppermute | solution.py:112
  117.9 21.6 %collective-permute-start.6 = (f32[16,8,128]{2,0,1:T(8,128)S(1)}, f32[16,8,128]{2,0,1:T(8,128)S(1)}, u32[]{:S(2)}, u32[]{:S(2)}) collective-permute-start(f32[16,8,128]{2,0,1:T(8,128)S(1)} %get-tuple-element.556), channel_id=1, source_target_pairs={{0,1},{1,2},{2,3},{3,4},{4,5},{5,6},{6,7},{7,8},{8,9},{9,10},{10,1... | collective-permute-start | bytes 196616 | tf_op jit(solution)/shard_map/ppermute | solution.py:111
  119.9 19.7 %collective-permute-start.7 = (f32[16,8,128]{2,0,1:T(8,128)S(1)}, f32[16,8,128]{2,0,1:T(8,128)S(1)}, u32[]{:S(2)}, u32[]{:S(2)}) collective-permute-start(f32[16,8,128]{2,0,1:T(8,128)S(1)} %get-tuple-element.557), channel_id=1, source_target_pairs={{1,0},{2,1},{3,2},{4,3},{5,4},{6,5},{7,6},{8,7},{9,8},{10,9},{11,1... | collective-permute-start | bytes 196616 | tf_op jit(solution)/shard_map/ppermute | solution.py:112
  158.1 5.9 %collective-permute-start.8 = (f32[8,128]{1,0:T(8,128)S(1)}, f32[8,128]{1,0:T(8,128)S(1)}, u32[]{:S(2)}, u32[]{:S(2)}) collective-permute-start(f32[8,128]{1,0:T(8,128)S(1)} %broadcast_in_dim.135), channel_id=1, source_target_pairs={{0,1},{1,0},{2,3},{3,2},{4,5},{5,4},{6,7},{7,6},{8,9},{9,8},{10,11... | collective-permute-start | bytes 12296 | tf_op jit(solution)/shard_map/ppermute | solution.py:39
  164.8 6.4 %collective-permute-start.9 = (f32[8,128]{1,0:T(8,128)S(1)}, f32[8,128]{1,0:T(8,128)S(1)}, u32[]{:S(2)}, u32[]{:S(2)}) collective-permute-start(f32[8,128]{1,0:T(8,128)S(1)} %broadcast_add_fusion), channel_id=1, source_target_pairs={{0,2},{1,3},{2,0},{3,1},{4,6},{5,7},{6,4},{7,5},{8,10},{9,11},{10,... | collective-permute-start | bytes 12296 | tf_op jit(solution)/shard_map/ppermute | solution.py:39
  171.9 9.4 %collective-permute-start.10 = (f32[8,128]{1,0:T(8,128)S(1)}, f32[8,128]{1,0:T(8,128)S(1)}, u32[]{:S(2)}, u32[]{:S(2)}) collective-permute-start(f32[8,128]{1,0:T(8,128)S(1)} %fusion.189), channel_id=1, source_target_pairs={{0,4},{1,5},{2,6},{3,7},{4,0},{5,1},{6,2},{7,3},{8,12},{9,13},{10,... | collective-permute-start | bytes 12296 | tf_op jit(solution)/shard_map/ppermute | solution.py:39
  181.3 6.4 %collective-permute-start.11 = (f32[8,128]{1,0:T(8,128)S(1)}, f32[8,128]{1,0:T(8,128)S(1)}, u32[]{:S(2)}, u32[]{:S(2)}) collective-permute-start(f32[8,128]{1,0:T(8,128)S(1)} %add.812), channel_id=1, source_target_pairs={{0,8},{1,9},{2,10},{3,11},{4,12},{5,13},{6,14},{7,15},{8,0},{9,1},... | collective-permute-start | bytes 12296 | tf_op jit(solution)/shard_map/ppermute | solution.py:39
  187.7 9.4 %collective-permute-start.12 = (f32[8,128]{1,0:T(8,128)S(1)}, f32[8,128]{1,0:T(8,128)S(1)}, u32[]{:S(2)}, u32[]{:S(2)}) collective-permute-start(f32[8,128]{1,0:T(8,128)S(1)} %add.813), channel_id=1, source_target_pairs={{0,16},{1,17},{2,18},{3,19},{4,20},{5,21},{6,22},{7,23},{8,24},{9,... | collective-permute-start | bytes 12296 | tf_op jit(solution)/shard_map/ppermute | solution.py:39
  198.4 3.1 %collective-permute-start.13 = (f32[8,1024]{1,0:T(8,128)S(1)}, f32[8,1024]{1,0:T(8,128)S(1)}, u32[]{:S(2)}, u32[]{:S(2)}) collective-permute-start(f32[8,1024]{1,0:T(8,128)S(1)} %maximum_maximum_fusion), channel_id=1, source_target_pairs={{0,32},{32,0},{64,96},{96,64},{128,160},{160,128},{192,224},{224,1... | collective-permute-start | bytes 98312 | tf_op jit(solution)/shard_map/ppermute | solution.py:39
  201.6 5.8 %collective-permute-start.14 = (f32[8,1024]{1,0:T(8,128)S(1)}, f32[8,1024]{1,0:T(8,128)S(1)}, u32[]{:S(2)}, u32[]{:S(2)}) collective-permute-start(f32[8,1024]{1,0:T(8,128)S(1)} %fusion.161), channel_id=1, source_target_pairs={{0,64},{32,96},{64,0},{96,32},{128,192},{160,224},{192,128},{224,1... | collective-permute-start | bytes 98312 | tf_op jit(solution)/shard_map/ppermute | solution.py:39
  207.4 7.3 %collective-permute-start.15 = (f32[8,1024]{1,0:T(8,128)S(1)}, f32[8,1024]{1,0:T(8,128)S(1)}, u32[]{:S(2)}, u32[]{:S(2)}) collective-permute-start(f32[8,1024]{1,0:T(8,128)S(1)} %add.816), channel_id=1, source_target_pairs={{0,128},{32,160},{64,192},{96,224},{128,0},{160,32},{192,64},{224,... | collective-permute-start | bytes 98312 | tf_op jit(solution)/shard_map/ppermute | solution.py:39
  214.7 5.8 %collective-permute-start.16 = (f32[8,1024]{1,0:T(8,128)S(1)}, f32[8,1024]{1,0:T(8,128)S(1)}, u32[]{:S(2)}, u32[]{:S(2)}) collective-permute-start(f32[8,1024]{1,0:T(8,128)S(1)} %add.817), channel_id=1, source_target_pairs={{0,256},{32,288},{64,320},{96,352},{128,384},{160,416},{192,448},{... | collective-permute-start | bytes 98312 | tf_op jit(solution)/shard_map/ppermute | solution.py:39
  217.1 5.3 %copy-start.5 = (f32[1,3,128]{2,0,1:T(1,128)S(1)}, f32[1,3,128]{2,0,1:T(1,128)}, u32[]{:S(2)}) copy-start(f32[1,3,128]{2,0,1:T(1,128)} %param.22) | copy-start | bytes 4612

commit v7 on v6

--- a/solution.py
+++ b/solution.py
@@ -66,11 +66,10 @@
     )
 
 
-def tile_forces(source, own_index, link_index):
+def tile_forces(source, own_tiles, own_index, link_index):
     tiles = own_index.shape[0]
     group = 32
     width = source.shape[-1]
-    own_tiles = source[own_index]
 
     def per_group(item):
         own_group, link_group, index_group = item
@@ -110,9 +109,10 @@
         )
         before = lax.ppermute(packed[tiles - HALO :], "space", up)
         after = lax.ppermute(packed[:HALO], "space", down)
-        inner_force = tile_forces(packed, inner, inner_links)
+        inner_force = tile_forces(packed, packed[HALO : tiles - HALO], inner, inner_links)
         extended = jnp.concatenate([before, packed, after], axis=0)
-        outer_force = tile_forces(extended, outer + HALO, outer_links)
+        outer_tiles = jnp.concatenate([packed[:HALO], packed[tiles - HALO :]], axis=0)
+        outer_force = tile_forces(extended, outer_tiles, outer + HALO, outer_links)
         force = jnp.concatenate(
             [outer_force[:HALO], inner_force, outer_force[HALO:]], axis=0
         )

time: 224 us -> 219 us (0.978)
  local copies, waits for them, and re-layouts: 21.7 us -> 16.4 us
    gather x8 -> x0, local copies, waits for them, and re-layouts: 4.68 us -> none  [tile_forces(): own_tiles = source[own_index]]
  transfers between devices with their start and end apart: 17 -> 17, of which waited for: 8 -> 8; matrix products, arithmetic and copies ran while one was open for 27% -> 30% of each run, Pallas kernels for 0% -> 0%
where the time goes in v7:
time: 219 us; the launch traced here: 218 us
  other arithmetic  95.5 us (44%)
  starting transfers between devices  64.4 us (29%)
  waiting for transfers between devices  25.6 us (12%)
  local copies, waits for them, and re-layouts  16.4 us (7%)
  matrix products  11.7 us (5%)
  between operations  3.91 us (2%)
    reduce_sum x8, other arithmetic, bead_forces(): jnp.sum(factor * offset_x, axis=(0, 2))  85.5 us
    ppermute x4, starting transfers between devices, shards(): after = lax.ppermute(packed[:HALO], 'space', down)  33.9 us
    ppermute x9, waiting for transfers between devices, butterfly_sum(): leaves.append(lax.ppermute(value, axis, pairs))  25.5 us
    ppermute x9, starting transfers between devices, butterfly_sum(): leaves.append(lax.ppermute(value, axis, pairs))  20.3 us
    dot_general x8, matrix products, accumulate(): jnp.dot(rows_now, table, precision=lax.Precision.HIGHEST, preferred_eleme...  11.7 us
    ppermute x4, starting transfers between devices, shards(): before = lax.ppermute(packed[tiles - HALO:], 'space', up)  10.2 us
    gather x8, local copies, waits for them, and re-layouts, per_group(): partners = source[link_group]  5.53 us
  transfers between devices with their start and end apart: 17, of which 8 were waited for; matrix products, arithmetic and copies ran while one was open for 30% of the time, Pallas kernels for 0%

profile of v7, /device:TPU:46, one launch (start us, length us, event | category | flops | bytes accessed | tf_op | source)
XLA Modules:
  0.0 217.8 jit_solution(10257695215388874415)
XLA Ops:
  0.6 0.8 slice_bitcast_fusion
  1.5 1.0 fusion.136
  2.5 4.4 %collective-permute-start = (f32[16,8,128]{2,0,1:T(8,128)S(1)}, f32[16,8,128]{2,0,1:T(8,128)S(1)}, u32[]{:S(2)}, u32[]{:S(2)}) collective-permute-start(f32[16,8,128]{2,0,1:T(8,128)S(1)} %get-tuple-element.562), channel_id=1, source_target_pairs={{0,1},{1,2},{2,3},{3,4},{4,5},{5,6},{6,7},{7,8},{8,9},{9,10},{10,1... | collective-permute-start | bytes 196616 | tf_op jit(solution)/shard_map/ppermute | solution.py:110
  6.9 9.3 %collective-permute-start.1 = (f32[16,8,128]{2,0,1:T(8,128)S(1)}, f32[16,8,128]{2,0,1:T(8,128)S(1)}, u32[]{:S(2)}, u32[]{:S(2)}) collective-permute-start(f32[16,8,128]{2,0,1:T(8,128)S(1)} %get-tuple-element.563), channel_id=1, source_target_pairs={{1,0},{2,1},{3,2},{4,3},{5,4},{6,5},{7,6},{8,7},{9,8},{10,9},{11,1... | collective-permute-start | bytes 196616 | tf_op jit(solution)/shard_map/ppermute | solution.py:111
  17.0 0.7 gather_fusion.1
  19.2 10.7 %multiply_reduce_fusion.6 = (f32[32,128]{1,0:T(8,128)S(1)}, f32[32,128]{1,0:T(8,128)S(1)}, f32[32,128]{1,0:T(8,128)S(1)}) fusion(f32[32,3]{1,0:T(8,128)S(1)} %copy.331, f32[32,3,128]{2,1,0:T(4,128)S(1)} %copy.330, f32[32,128]{1,0:T(8,128)S(1)} %get-tuple-element.682, f32[32,3,128]{2,1,0:T(4,128)S(1)} %copy.343, f32[32,128]{1,0:T(8,128)S(1)} %get-tuple-element.567, ...), kind=kLoop, calls=%fused_computation.208 | loop fusion | flops 51892224 | bytes 573824 | tf_op jit(solution)/shard_map/while/body/eval_jaxpr/vmap()/reduce_sum | solution.py:62
  30.3 0.7 gather_fusion
  31.7 10.7 %multiply_reduce_fusion.7 = (f32[32,128]{1,0:T(8,128)S(1)}, f32[32,128]{1,0:T(8,128)S(1)}, f32[32,128]{1,0:T(8,128)S(1)}) fusion(f32[32,3]{1,0:T(8,128)S(1)} %copy.312, f32[32,3,128]{2,1,0:T(4,128)S(1)} %copy.311, f32[32,128]{1,0:T(8,128)S(1)} %get-tuple-element.597, f32[32,3,128]{2,1,0:T(4,128)S(1)} %copy.324, f32[32,128]{1,0:T(8,128)S(1)} %get-tuple-element.602, ...), kind=kLoop, calls=%fused_computation.210 | loop fusion | flops 51892224 | bytes 573824 | tf_op jit(solution)/shard_map/while/body/eval_jaxpr/vmap()/reduce_sum | solution.py:62
  42.6 1.9 collective-permute-start.2
  44.6 8.1 %collective-permute-start.3 = (f32[16,8,128]{2,0,1:T(8,128)S(1)}, f32[16,8,128]{2,0,1:T(8,128)S(1)}, u32[]{:S(2)}, u32[]{:S(2)}) collective-permute-start(f32[16,8,128]{2,0,1:T(8,128)S(1)} %get-tuple-element.561), channel_id=1, source_target_pairs={{1,0},{2,1},{3,2},{4,3},{5,4},{6,5},{7,6},{8,7},{9,8},{10,9},{11,1... | collective-permute-start | bytes 196616 | tf_op jit(solution)/shard_map/ppermute | solution.py:111
  52.7 0.7 gather_fusion.3
  54.2 10.7 %multiply_reduce_fusion.4 = (f32[32,128]{1,0:T(8,128)S(1)}, f32[32,128]{1,0:T(8,128)S(1)}, f32[32,128]{1,0:T(8,128)S(1)}) fusion(f32[32,3,128]{2,1,0:T(4,128)S(1)} %copy.365, f32[32,128]{1,0:T(8,128)S(1)} %get-tuple-element.622, f32[32,3]{1,0:T(8,128)S(1)} %copy.331, f32[32,3,128]{2,1,0:T(4,128)S(1)} %copy.377, f32[32,128]{1,0:T(8,128)S(1)} %get-tuple-element.566, ...), kind=kLoop, calls=%fused_computation.204 | loop fusion | flops 51892224 | bytes 573824 | tf_op jit(solution)/shard_map/while/body/eval_jaxpr/vmap()/reduce_sum | solution.py:62
  65.2 0.7 gather_fusion.2
  66.6 10.7 %multiply_reduce_fusion.5 = (f32[32,128]{1,0:T(8,128)S(1)}, f32[32,128]{1,0:T(8,128)S(1)}, f32[32,128]{1,0:T(8,128)S(1)}) fusion(f32[32,3,128]{2,1,0:T(4,128)S(1)} %copy.348, f32[32,128]{1,0:T(8,128)S(1)} %get-tuple-element.589, f32[32,3]{1,0:T(8,128)S(1)} %copy.312, f32[32,3,128]{2,1,0:T(4,128)S(1)} %copy.360, f32[32,128]{1,0:T(8,128)S(1)} %get-tuple-element.594, ...), kind=kLoop, calls=%fused_computation.206 | loop fusion | flops 51892224 | bytes 573824 | tf_op jit(solution)/shard_map/while/body/eval_jaxpr/vmap()/reduce_sum | solution.py:62
  77.6 1.9 collective-permute-start.4
  79.6 8.3 %collective-permute-start.5 = (f32[16,8,128]{2,0,1:T(8,128)S(1)}, f32[16,8,128]{2,0,1:T(8,128)S(1)}, u32[]{:S(2)}, u32[]{:S(2)}) collective-permute-start(f32[16,8,128]{2,0,1:T(8,128)S(1)} %get-tuple-element.559), channel_id=1, source_target_pairs={{1,0},{2,1},{3,2},{4,3},{5,4},{6,5},{7,6},{8,7},{9,8},{10,9},{11,1... | collective-permute-start | bytes 196616 | tf_op jit(solution)/shard_map/ppermute | solution.py:111
  87.9 0.7 gather_fusion.5
  89.3 10.7 %multiply_reduce_fusion.2 = (f32[32,128]{1,0:T(8,128)S(1)}, f32[32,128]{1,0:T(8,128)S(1)}, f32[32,128]{1,0:T(8,128)S(1)}) fusion(f32[32,3,128]{2,1,0:T(4,128)S(1)} %copy.399, f32[32,128]{1,0:T(8,128)S(1)} %get-tuple-element.616, f32[32,3]{1,0:T(8,128)S(1)} %copy.331, f32[32,3,128]{2,1,0:T(4,128)S(1)} %copy.411, f32[32,128]{1,0:T(8,128)S(1)} %get-tuple-element.565, ...), kind=kLoop, calls=%fused_computation.200 | loop fusion | flops 51892224 | bytes 573824 | tf_op jit(solution)/shard_map/while/body/eval_jaxpr/vmap()/reduce_sum | solution.py:62
  100.3 0.7 gather_fusion.4
  101.8 10.7 %multiply_reduce_fusion.3 = (f32[32,128]{1,0:T(8,128)S(1)}, f32[32,128]{1,0:T(8,128)S(1)}, f32[32,128]{1,0:T(8,128)S(1)}) fusion(f32[32,3,128]{2,1,0:T(4,128)S(1)} %copy.382, f32[32,128]{1,0:T(8,128)S(1)} %get-tuple-element.581, f32[32,3]{1,0:T(8,128)S(1)} %copy.312, f32[32,3,128]{2,1,0:T(4,128)S(1)} %copy.394, f32[32,128]{1,0:T(8,128)S(1)} %get-tuple-element.586, ...), kind=kLoop, calls=%fused_computation.202 | loop fusion | flops 51892224 | bytes 573824 | tf_op jit(solution)/shard_map/while/body/eval_jaxpr/vmap()/reduce_sum | solution.py:62
  112.8 1.9 collective-permute-start.6
  114.7 8.1 %collective-permute-start.7 = (f32[16,8,128]{2,0,1:T(8,128)S(1)}, f32[16,8,128]{2,0,1:T(8,128)S(1)}, u32[]{:S(2)}, u32[]{:S(2)}) collective-permute-start(f32[16,8,128]{2,0,1:T(8,128)S(1)} %get-tuple-element.557), channel_id=1, source_target_pairs={{1,0},{2,1},{3,2},{4,3},{5,4},{6,5},{7,6},{8,7},{9,8},{10,9},{11,1... | collective-permute-start | bytes 196616 | tf_op jit(solution)/shard_map/ppermute | solution.py:111
  122.9 0.7 gather_fusion.7
  124.3 10.7 %multiply_reduce_fusion = (f32[32,128]{1,0:T(8,128)S(1)}, f32[32,128]{1,0:T(8,128)S(1)}, f32[32,128]{1,0:T(8,128)S(1)}) fusion(f32[32,3,128]{2,1,0:T(4,128)S(1)} %copy.433, f32[32,128]{1,0:T(8,128)S(1)} %get-tuple-element.610, f32[32,3]{1,0:T(8,128)S(1)} %copy.331, f32[32,3,128]{2,1,0:T(4,128)S(1)} %copy.445, f32[32,128]{1,0:T(8,128)S(1)} %get-tuple-element.564, ...), kind=kLoop, calls=%fused_computation.196 | loop fusion | flops 51892224 | bytes 573824 | tf_op jit(solution)/shard_map/while/body/eval_jaxpr/vmap()/reduce_sum | solution.py:62
  135.3 0.7 gather_fusion.6
  136.7 10.7 %multiply_reduce_fusion.1 = (f32[32,128]{1,0:T(8,128)S(1)}, f32[32,128]{1,0:T(8,128)S(1)}, f32[32,128]{1,0:T(8,128)S(1)}) fusion(f32[32,3,128]{2,1,0:T(4,128)S(1)} %copy.416, f32[32,128]{1,0:T(8,128)S(1)} %get-tuple-element.569, f32[32,3]{1,0:T(8,128)S(1)} %copy.312, f32[32,3,128]{2,1,0:T(4,128)S(1)} %copy.428, f32[32,128]{1,0:T(8,128)S(1)} %get-tuple-element.574, ...), kind=kLoop, calls=%fused_computation.198 | loop fusion | flops 51892224 | bytes 573824 | tf_op jit(solution)/shard_map/while/body/eval_jaxpr/vmap()/reduce_sum | solution.py:62
  147.5 0.7 slice_reduce_fusion
  148.2 0.7 broadcast_in_dim.118
  148.9 1.9 collective-permute-start.8
  150.8 4.1 %while.12 = (s32[]{:T(128)}, f32[3,1024]{1,0:T(4,128)S(1)}, f32[1024]{0:T(1024)S(1)}, f32[2,8,3,128]{3,1,0,2:T(8,128)S(1)}, s32[2,1024]{1,0:T(2,128)S(1)}, /*index=5*/s32[]{:T(128)}, s32[]{:T(128)}) while((s32[]{:T(128)}, f32[3,1024]{1,0:T(4,128)S(1)}, f32[1024]{0:T(1024)S(1)}, f32[2,8,3,128]{3,1,0,2:T(8,128)S(1)}, ...), condition=%wide.region_26.27_spmd.clone, body=%wide.region_24.26_spmd.clone.sunk | while | flops 41950208 | bytes 94304 | solution.py:147
  150.8 1.5 fusion.249
  152.9 1.5 fusion.249
  154.9 4.1 %while.13 = (s32[]{:T(128)}, f32[3,1024]{1,0:T(4,128)S(1)}, f32[1024]{0:T(1024)S(1)}, f32[2,8,3,128]{3,1,0,2:T(8,128)S(1)}, s32[2,1024]{1,0:T(2,128)S(1)}, /*index=5*/s32[]{:T(128)}, s32[]{:T(128)}) while((s32[]{:T(128)}, f32[3,1024]{1,0:T(4,128)S(1)}, f32[1024]{0:T(1024)S(1)}, f32[2,8,3,128]{3,1,0,2:T(8,128)S(1)}, ...), condition=%wide.region_29.30_spmd.clone, body=%wide.region_27.29_spmd.clone.sunk | while | flops 41950208 | bytes 94304 | solution.py:147
  154.9 1.5 fusion.251
  156.9 1.5 fusion.251
  158.9 0.7 broadcast_add_fusion
  159.6 2.1 collective-permute-start.9
  161.8 4.1 %while.14 = (s32[]{:T(128)}, f32[3,1024]{1,0:T(4,128)S(1)}, f32[1024]{0:T(1024)S(1)}, f32[2,8,3,128]{3,1,0,2:T(8,128)S(1)}, s32[2,1024]{1,0:T(2,128)S(1)}, /*index=5*/s32[]{:T(128)}, s32[]{:T(128)}) while((s32[]{:T(128)}, f32[3,1024]{1,0:T(4,128)S(1)}, f32[1024]{0:T(1024)S(1)}, f32[2,8,3,128]{3,1,0,2:T(8,128)S(1)}, ...), condition=%wide.region_32.33_spmd.clone, body=%wide.region_30.32_spmd.clone.sunk | while | flops 41950208 | bytes 94304 | solution.py:147
  161.8 1.5 fusion.253
  163.9 1.5 fusion.253
  166.0 0.7 fusion.240
  166.7 1.9 collective-permute-start.10
  168.7 4.1 %while.15 = (s32[]{:T(128)}, f32[3,1024]{1,0:T(4,128)S(1)}, f32[1024]{0:T(1024)S(1)}, f32[2,8,3,128]{3,1,0,2:T(8,128)S(1)}, s32[2,1024]{1,0:T(2,128)S(1)}, /*index=5*/s32[]{:T(128)}, s32[]{:T(128)}) while((s32[]{:T(128)}, f32[3,1024]{1,0:T(4,128)S(1)}, f32[1024]{0:T(1024)S(1)}, f32[2,8,3,128]{3,1,0,2:T(8,128)S(1)}, ...), condition=%wide.region_35.36_spmd.clone, body=%wide.region_33.35_spmd.clone.sunk | while | flops 41950208 | bytes 94304 | solution.py:147
  168.7 1.5 fusion.255
  170.7 1.5 fusion.255
  172.7 3.4 %collective-permute-done.10 = f32[8,128]{1,0:T(8,128)S(1)} collective-permute-done((f32[8,128]{1,0:T(8,128)S(1)}, f32[8,128]{1,0:T(8,128)S(1)}, u32[]{:S(2)}, u32[]{:S(2)}) %collective-permute-start.10) | collective-permute-done | bytes 4128 | tf_op jit(solution)/shard_map/ppermute | solution.py:39
  176.1 1.9 collective-permute-start.11
  178.1 4.5 %collective-permute-done.11 = f32[8,128]{1,0:T(8,128)S(1)} collective-permute-done((f32[8,128]{1,0:T(8,128)S(1)}, f32[8,128]{1,0:T(8,128)S(1)}, u32[]{:S(2)}, u32[]{:S(2)}) %collective-permute-start.11) | collective-permute-done | bytes 4128 | tf_op jit(solution)/shard_map/ppermute | solution.py:39
  182.5 2.1 collective-permute-start.12
  184.7 7.2 %collective-permute-done.12 = f32[8,128]{1,0:T(8,128)S(1)} collective-permute-done((f32[8,128]{1,0:T(8,128)S(1)}, f32[8,128]{1,0:T(8,128)S(1)}, u32[]{:S(2)}, u32[]{:S(2)}) %collective-permute-start.12) | collective-permute-done | bytes 4128 | tf_op jit(solution)/shard_map/ppermute | solution.py:39
  191.9 0.5 slice.910
  192.5 0.6 broadcast_in_dim.119
  193.3 1.9 collective-permute-start.13
  195.2 1.2 collective-permute-done.13
  196.4 2.7 %collective-permute-start.14 = (f32[8,1024]{1,0:T(8,128)S(1)}, f32[8,1024]{1,0:T(8,128)S(1)}, u32[]{:S(2)}, u32[]{:S(2)}) collective-permute-start(f32[8,1024]{1,0:T(8,128)S(1)} %fusion.220), channel_id=1, source_target_pairs={{0,64},{32,96},{64,0},{96,32},{128,192},{160,224},{192,128},{224,1... | collective-permute-start | bytes 98312 | tf_op jit(solution)/shard_map/ppermute | solution.py:39
  199.8 2.4 %collective-permute-done.14 = f32[8,1024]{1,0:T(8,128)S(1)} collective-permute-done((f32[8,1024]{1,0:T(8,128)S(1)}, f32[8,1024]{1,0:T(8,128)S(1)}, u32[]{:S(2)}, u32[]{:S(2)}) %collective-permute-start.14) | collective-permute-done | bytes 32800 | tf_op jit(solution)/shard_map/ppermute | solution.py:39
  202.2 3.3 %collective-permute-start.15 = (f32[8,1024]{1,0:T(8,128)S(1)}, f32[8,1024]{1,0:T(8,128)S(1)}, u32[]{:S(2)}, u32[]{:S(2)}) collective-permute-start(f32[8,1024]{1,0:T(8,128)S(1)} %add.774), channel_id=1, source_target_pairs={{0,128},{32,160},{64,192},{96,224},{128,0},{160,32},{192,64},{224,... | collective-permute-start | bytes 98312 | tf_op jit(solution)/shard_map/ppermute | solution.py:39
  205.5 4.0 %collective-permute-done.15 = f32[8,1024]{1,0:T(8,128)S(1)} collective-permute-done((f32[8,1024]{1,0:T(8,128)S(1)}, f32[8,1024]{1,0:T(8,128)S(1)}, u32[]{:S(2)}, u32[]{:S(2)}) %collective-permute-start.15) | collective-permute-done | bytes 32800 | tf_op jit(solution)/shard_map/ppermute | solution.py:39
  209.5 2.3 %collective-permute-start.16 = (f32[8,1024]{1,0:T(8,128)S(1)}, f32[8,1024]{1,0:T(8,128)S(1)}, u32[]{:S(2)}, u32[]{:S(2)}) collective-permute-start(f32[8,1024]{1,0:T(8,128)S(1)} %add.775), channel_id=1, source_target_pairs={{0,256},{32,288},{64,320},{96,352},{128,384},{160,416},{192,448},{... | collective-permute-start | bytes 98312 | tf_op jit(solution)/shard_map/ppermute | solution.py:39
  211.9 0.7 multiply_add_fusion
  212.6 2.7 %collective-permute-done.16 = f32[8,1024]{1,0:T(8,128)S(1)} collective-permute-done((f32[8,1024]{1,0:T(8,128)S(1)}, f32[8,1024]{1,0:T(8,128)S(1)}, u32[]{:S(2)}, u32[]{:S(2)}) %collective-permute-start.16) | collective-permute-done | bytes 32800 | tf_op jit(solution)/shard_map/ppermute | solution.py:39
  215.3 0.5 slice.1097
  215.9 0.6 slice_divide_fusion
  217.1 0.6 broadcast_select_fusion
  (281 shorter events, 12.8 us)
Async XLA Ops:
  2.4 13.9 %copy-start.1 = (f32[1,64,3,128]{3,1,2,0:T(8,128)S(1)}, f32[1,64,3,128]{3,1,2,0:T(8,128)}, u32[]{:S(2)}) copy-start(f32[1,64,3,128]{3,1,2,0:T(8,128)} %param.16) | copy-start | bytes 294916
  2.5 13.9 %copy-start.2 = (f32[1,64,3,128]{3,1,2,0:T(8,128)S(1)}, f32[1,64,3,128]{3,1,2,0:T(8,128)}, u32[]{:S(2)}) copy-start(f32[1,64,3,128]{3,1,2,0:T(8,128)} %param.17) | copy-start | bytes 294916
  2.5 13.9 %copy-start.3 = (f32[4,1,64,128]{3,2,1,0:T(8,128)S(1)}, f32[4,1,64,128]{3,2,1,0:T(8,128)}, u32[]{:S(2)}) copy-start(f32[4,1,64,128]{3,2,1,0:T(8,128)} %param.19) | copy-start | bytes 393220
  2.5 27.5 %collective-permute-start = (f32[16,8,128]{2,0,1:T(8,128)S(1)}, f32[16,8,128]{2,0,1:T(8,128)S(1)}, u32[]{:S(2)}, u32[]{:S(2)}) collective-permute-start(f32[16,8,128]{2,0,1:T(8,128)S(1)} %get-tuple-element.562), channel_id=1, source_target_pairs={{0,1},{1,2},{2,3},{3,4},{4,5},{5,6},{6,7},{7,8},{8,9},{9,10},{10,1... | collective-permute-start | bytes 196616 | tf_op jit(solution)/shard_map/ppermute | solution.py:110
  6.9 9.5 %copy-start.5 = (s32[1,64,3]{1,0,2:T(1,128)S(1)}, s32[1,64,3]{1,0,2:T(1,128)}, u32[]{:S(2)}) copy-start(s32[1,64,3]{1,0,2:T(1,128)} %param.20) | copy-start | bytes 2308
  6.9 9.7 %copy-start = (f32[1,64,128]{2,1,0:T(8,128)S(1)}, f32[1,64,128]{2,1,0:T(8,128)}, u32[]{:S(2)}) copy-start(f32[1,64,128]{2,1,0:T(8,128)} %param.18) | copy-start | bytes 98308
  6.9 23.0 %collective-permute-start.1 = (f32[16,8,128]{2,0,1:T(8,128)S(1)}, f32[16,8,128]{2,0,1:T(8,128)S(1)}, u32[]{:S(2)}, u32[]{:S(2)}) collective-permute-start(f32[16,8,128]{2,0,1:T(8,128)S(1)} %get-tuple-element.563), channel_id=1, source_target_pairs={{1,0},{2,1},{3,2},{4,3},{5,4},{6,5},{7,6},{8,7},{9,8},{10,9},{11,1... | collective-permute-start | bytes 196616 | tf_op jit(solution)/shard_map/ppermute | solution.py:111
  18.2 1.0 copy-start.4
  42.6 22.2 %collective-permute-start.2 = (f32[16,8,128]{2,0,1:T(8,128)S(1)}, f32[16,8,128]{2,0,1:T(8,128)S(1)}, u32[]{:S(2)}, u32[]{:S(2)}) collective-permute-start(f32[16,8,128]{2,0,1:T(8,128)S(1)} %get-tuple-element.560), channel_id=1, source_target_pairs={{0,1},{1,2},{2,3},{3,4},{4,5},{5,6},{6,7},{7,8},{8,9},{9,10},{10,1... | collective-permute-start | bytes 196616 | tf_op jit(solution)/shard_map/ppermute | solution.py:110
  44.6 20.3 %collective-permute-start.3 = (f32[16,8,128]{2,0,1:T(8,128)S(1)}, f32[16,8,128]{2,0,1:T(8,128)S(1)}, u32[]{:S(2)}, u32[]{:S(2)}) collective-permute-start(f32[16,8,128]{2,0,1:T(8,128)S(1)} %get-tuple-element.561), channel_id=1, source_target_pairs={{1,0},{2,1},{3,2},{4,3},{5,4},{6,5},{7,6},{8,7},{9,8},{10,9},{11,1... | collective-permute-start | bytes 196616 | tf_op jit(solution)/shard_map/ppermute | solution.py:111
  77.6 22.4 %collective-permute-start.4 = (f32[16,8,128]{2,0,1:T(8,128)S(1)}, f32[16,8,128]{2,0,1:T(8,128)S(1)}, u32[]{:S(2)}, u32[]{:S(2)}) collective-permute-start(f32[16,8,128]{2,0,1:T(8,128)S(1)} %get-tuple-element.558), channel_id=1, source_target_pairs={{0,1},{1,2},{2,3},{3,4},{4,5},{5,6},{6,7},{7,8},{8,9},{9,10},{10,1... | collective-permute-start | bytes 196616 | tf_op jit(solution)/shard_map/ppermute | solution.py:110
  79.6 20.5 %collective-permute-start.5 = (f32[16,8,128]{2,0,1:T(8,128)S(1)}, f32[16,8,128]{2,0,1:T(8,128)S(1)}, u32[]{:S(2)}, u32[]{:S(2)}) collective-permute-start(f32[16,8,128]{2,0,1:T(8,128)S(1)} %get-tuple-element.559), channel_id=1, source_target_pairs={{1,0},{2,1},{3,2},{4,3},{5,4},{6,5},{7,6},{8,7},{9,8},{10,9},{11,1... | collective-permute-start | bytes 196616 | tf_op jit(solution)/shard_map/ppermute | solution.py:111
  112.8 22.2 %collective-permute-start.6 = (f32[16,8,128]{2,0,1:T(8,128)S(1)}, f32[16,8,128]{2,0,1:T(8,128)S(1)}, u32[]{:S(2)}, u32[]{:S(2)}) collective-permute-start(f32[16,8,128]{2,0,1:T(8,128)S(1)} %get-tuple-element.556), channel_id=1, source_target_pairs={{0,1},{1,2},{2,3},{3,4},{4,5},{5,6},{6,7},{7,8},{8,9},{9,10},{10,1... | collective-permute-start | bytes 196616 | tf_op jit(solution)/shard_map/ppermute | solution.py:110
  114.7 20.3 %collective-permute-start.7 = (f32[16,8,128]{2,0,1:T(8,128)S(1)}, f32[16,8,128]{2,0,1:T(8,128)S(1)}, u32[]{:S(2)}, u32[]{:S(2)}) collective-permute-start(f32[16,8,128]{2,0,1:T(8,128)S(1)} %get-tuple-element.557), channel_id=1, source_target_pairs={{1,0},{2,1},{3,2},{4,3},{5,4},{6,5},{7,6},{8,7},{9,8},{10,9},{11,1... | collective-permute-start | bytes 196616 | tf_op jit(solution)/shard_map/ppermute | solution.py:111
  148.9 10.1 %collective-permute-start.8 = (f32[8,128]{1,0:T(8,128)S(1)}, f32[8,128]{1,0:T(8,128)S(1)}, u32[]{:S(2)}, u32[]{:S(2)}) collective-permute-start(f32[8,128]{1,0:T(8,128)S(1)} %broadcast_in_dim.118), channel_id=1, source_target_pairs={{0,1},{1,0},{2,3},{3,2},{4,5},{5,4},{6,7},{7,6},{8,9},{9,8},{10,11... | collective-permute-start | bytes 12296 | tf_op jit(solution)/shard_map/ppermute | solution.py:39
  159.6 6.4 %collective-permute-start.9 = (f32[8,128]{1,0:T(8,128)S(1)}, f32[8,128]{1,0:T(8,128)S(1)}, u32[]{:S(2)}, u32[]{:S(2)}) collective-permute-start(f32[8,128]{1,0:T(8,128)S(1)} %broadcast_add_fusion), channel_id=1, source_target_pairs={{0,2},{1,3},{2,0},{3,1},{4,6},{5,7},{6,4},{7,5},{8,10},{9,11},{10,... | collective-permute-start | bytes 12296 | tf_op jit(solution)/shard_map/ppermute | solution.py:39
  166.7 9.4 %collective-permute-start.10 = (f32[8,128]{1,0:T(8,128)S(1)}, f32[8,128]{1,0:T(8,128)S(1)}, u32[]{:S(2)}, u32[]{:S(2)}) collective-permute-start(f32[8,128]{1,0:T(8,128)S(1)} %fusion.240), channel_id=1, source_target_pairs={{0,4},{1,5},{2,6},{3,7},{4,0},{5,1},{6,2},{7,3},{8,12},{9,13},{10,... | collective-permute-start | bytes 12296 | tf_op jit(solution)/shard_map/ppermute | solution.py:39
  176.1 6.4 %collective-permute-start.11 = (f32[8,128]{1,0:T(8,128)S(1)}, f32[8,128]{1,0:T(8,128)S(1)}, u32[]{:S(2)}, u32[]{:S(2)}) collective-permute-start(f32[8,128]{1,0:T(8,128)S(1)} %add.770), channel_id=1, source_target_pairs={{0,8},{1,9},{2,10},{3,11},{4,12},{5,13},{6,14},{7,15},{8,0},{9,1},... | collective-permute-start | bytes 12296 | tf_op jit(solution)/shard_map/ppermute | solution.py:39
  182.5 9.4 %collective-permute-start.12 = (f32[8,128]{1,0:T(8,128)S(1)}, f32[8,128]{1,0:T(8,128)S(1)}, u32[]{:S(2)}, u32[]{:S(2)}) collective-permute-start(f32[8,128]{1,0:T(8,128)S(1)} %add.771), channel_id=1, source_target_pairs={{0,16},{1,17},{2,18},{3,19},{4,20},{5,21},{6,22},{7,23},{8,24},{9,... | collective-permute-start | bytes 12296 | tf_op jit(solution)/shard_map/ppermute | solution.py:39
  193.3 3.1 %collective-permute-start.13 = (f32[8,1024]{1,0:T(8,128)S(1)}, f32[8,1024]{1,0:T(8,128)S(1)}, u32[]{:S(2)}, u32[]{:S(2)}) collective-permute-start(f32[8,1024]{1,0:T(8,128)S(1)} %maximum_maximum_fusion), channel_id=1, source_target_pairs={{0,32},{32,0},{64,96},{96,64},{128,160},{160,128},{192,224},{224,1... | collective-permute-start | bytes 98312 | tf_op jit(solution)/shard_map/ppermute | solution.py:39
  196.4 5.8 %collective-permute-start.14 = (f32[8,1024]{1,0:T(8,128)S(1)}, f32[8,1024]{1,0:T(8,128)S(1)}, u32[]{:S(2)}, u32[]{:S(2)}) collective-permute-start(f32[8,1024]{1,0:T(8,128)S(1)} %fusion.220), channel_id=1, source_target_pairs={{0,64},{32,96},{64,0},{96,32},{128,192},{160,224},{192,128},{224,1... | collective-permute-start | bytes 98312 | tf_op jit(solution)/shard_map/ppermute | solution.py:39
  202.2 7.3 %collective-permute-start.15 = (f32[8,1024]{1,0:T(8,128)S(1)}, f32[8,1024]{1,0:T(8,128)S(1)}, u32[]{:S(2)}, u32[]{:S(2)}) collective-permute-start(f32[8,1024]{1,0:T(8,128)S(1)} %add.774), channel_id=1, source_target_pairs={{0,128},{32,160},{64,192},{96,224},{128,0},{160,32},{192,64},{224,... | collective-permute-start | bytes 98312 | tf_op jit(solution)/shard_map/ppermute | solution.py:39
  209.5 5.8 %collective-permute-start.16 = (f32[8,1024]{1,0:T(8,128)S(1)}, f32[8,1024]{1,0:T(8,128)S(1)}, u32[]{:S(2)}, u32[]{:S(2)}) collective-permute-start(f32[8,1024]{1,0:T(8,128)S(1)} %add.775), channel_id=1, source_target_pairs={{0,256},{32,288},{64,320},{96,352},{128,384},{160,416},{192,448},{... | collective-permute-start | bytes 98312 | tf_op jit(solution)/shard_map/ppermute | solution.py:39
  211.9 5.3 %copy-start.6 = (f32[1,3,128]{2,0,1:T(1,128)S(1)}, f32[1,3,128]{2,0,1:T(1,128)}, u32[]{:S(2)}) copy-start(f32[1,3,128]{2,0,1:T(1,128)} %param.22) | copy-start | bytes 4612
